TPU v7x, 512 devices: a whole 4x4x16 slice. The times are simulated.
512 devices in a mesh: gy: 4 (over x_lo, core), gz: 128 (over y, x_hi, z).
Axes of the slice: x: 4 (x_hi: 2, x_lo: 2; x = x_hi * 2 + x_lo), y: 4, z: 16, core: 2. Of those that a mesh axis runs over, the one named last changes fastest.
Arguments:
- fields: float32 [2, 3, 2, 1024, 2048], P(None, None, None, 'gz', 'gy'), may hold values from -6 to 6
- eigenstrain: float32 [3, 6], replicated, may hold values from -3 to 3
- moduli: float32 [3], replicated, may hold values from 0.6 to 2.6, as said below
Outputs:
- driving: float32 [2, 3, 2, 1024, 2048], P(None, None, None, 'gz', 'gy')
Inputs may be any that keep to these rules, and one draw needn't show every extreme that they name: moduli = (C11, C12, C44) with C11 in 2.0 to 2.6, C12 in 0.9 to 1.3, C44 in 0.6 to 1.0.
All inputs are finite; a program needn't handle non-finite values.
Results may differ from a plain program's by a relative error of at most 0.0003.
Values sent between devices are 32-bit elements; how exact they have to be, the bound alone decides.
No kernel may reach another device: no remote copies, remote signals or barrier semaphores. Data moves between devices by JAX's collectives and lax.ppermute only.
A program may use at most 64 MiB of HBM per device.

v0:
```python
import math

import jax
import jax.numpy as jnp
from jax import lax
from jax.sharding import PartitionSpec as P

NX = 2048
NY = 2048
NZ = 1024


highest = lax.Precision.HIGHEST


def partner_2(value, axis, stride):
    mask = 2**stride
    pairs = [(source, source ^ mask) for source in range(lax.axis_size(axis))]
    return lax.ppermute(value, axis, pairs)


def signed_wave(index, length):
    return jnp.where(index < length // 2, index, index - length).astype(jnp.float32) / length


def voigt_tensor(entries):
    return [
        [entries[0], entries[5], entries[4]],
        [entries[5], entries[1], entries[3]],
        [entries[4], entries[3], entries[2]],
    ]


def kernel_rows(kx_wave, ky_wave, kz_wave, eigenstrain, moduli):
    stiff_a = moduli[0]
    stiff_b = moduli[1]
    shear = moduli[2]
    square = kx_wave * kx_wave + ky_wave * ky_wave + kz_wave * kz_wave
    inside = square > 0.0
    inverse = lax.rsqrt(jnp.where(inside, square, 1.0))
    normal = [kx_wave * inverse, ky_wave * inverse, kz_wave * inverse]
    g_diag = [shear + (stiff_a - shear) * normal[axis_id] * normal[axis_id] for axis_id in range(3)]
    cross_coef = stiff_b + shear
    g_zero_one = cross_coef * normal[0] * normal[1]
    g_zero_two = cross_coef * normal[0] * normal[2]
    g_one_two = cross_coef * normal[1] * normal[2]
    cof_zz = g_diag[1] * g_diag[2] - g_one_two * g_one_two
    cof_zo = g_zero_two * g_one_two - g_zero_one * g_diag[2]
    cof_zt = g_zero_one * g_one_two - g_zero_two * g_diag[1]
    cof_oo = g_diag[0] * g_diag[2] - g_zero_two * g_zero_two
    cof_ot = g_zero_one * g_zero_two - g_diag[0] * g_one_two
    cof_tt = g_diag[0] * g_diag[1] - g_zero_one * g_zero_one
    determinant = g_diag[0] * cof_zz + g_zero_one * cof_zo + g_zero_two * cof_zt
    recip = 1.0 / determinant
    omega = [
        [cof_zz * recip, cof_zo * recip, cof_zt * recip],
        [cof_zo * recip, cof_oo * recip, cof_ot * recip],
        [cof_zt * recip, cof_ot * recip, cof_tt * recip],
    ]
    strains = []
    stresses = []
    for variant in range(3):
        entries = [eigenstrain[variant, column] for column in range(6)]
        trace = entries[0] + entries[1] + entries[2]
        stress = [stiff_b * trace + (stiff_a - stiff_b) * entries[column] for column in range(3)]
        stress = stress + [2.0 * shear * entries[column] for column in range(3, 6)]
        strains.append(voigt_tensor(entries))
        stresses.append(voigt_tensor(stress))
    traction = []
    for variant in range(3):
        traction.append(
            [
                sum((stresses[variant][first][second] * normal[second] for second in range(3)))
                for first in range(3)
            ]
        )
    response = []
    for variant in range(3):
        response.append(
            [
                sum((omega[first][second] * traction[variant][second] for second in range(3)))
                for first in range(3)
            ]
        )
    kernel = []
    for source in range(3):
        kernel_row = []
        for target in range(3):
            energy = sum(
                (
                    stresses[source][first][second] * strains[target][first][second]
                    for first in range(3)
                    for second in range(3)
                )
            )
            coupling = sum(
                (traction[source][first] * response[target][first] for first in range(3))
            )
            kernel_row.append(jnp.where(inside, energy - coupling, 0.0))
        kernel.append(kernel_row)
    return kernel


def cos_sin(numer, length):
    angle = (2.0 * math.pi / length) * (numer % length).astype(jnp.float32)
    return (jnp.cos(angle), jnp.sin(angle))


def stacked_table(length, axis):
    rows_idx = lax.broadcasted_iota(jnp.int32, (length, length), 0)
    cols_idx = lax.broadcasted_iota(jnp.int32, (length, length), 1)
    cosine, sine = cos_sin(rows_idx * cols_idx, length)
    return jnp.concatenate([cosine, sine], axis=axis)


def block_dft8(inverse):
    size = 192
    rows_idx = lax.broadcasted_iota(jnp.int32, (size, size), 0)
    cols_idx = lax.broadcasted_iota(jnp.int32, (size, size), 1)
    same = (rows_idx // 32 == cols_idx // 32) & (rows_idx % 4 == cols_idx % 4)
    cosine, sine = cos_sin(((rows_idx // 4) % 8) * ((cols_idx // 4) % 8), 8)
    cosine = jnp.where(same, cosine, 0.0)
    sine = jnp.where(same, sine, 0.0)
    if inverse:
        top = jnp.concatenate([cosine, sine], axis=1)
        bottom = jnp.concatenate([-sine, cosine], axis=1)
    else:
        top = jnp.concatenate([cosine, -sine], axis=1)
        bottom = jnp.concatenate([sine, cosine], axis=1)
    return jnp.concatenate([top, bottom], axis=0)


def matmul(spec, left, right):
    return jnp.einsum(spec, left, right, precision=highest)


def combine_rows(product, sign):
    c_re = product[:128, :192]
    c_im = product[:128, 192:]
    s_re = product[128:, :192]
    s_im = product[128:, 192:]
    if sign < 0:
        return (c_re + s_im, c_im - s_re)
    return (c_re - s_im, c_im + s_re)


def twiddle(values, factor_cos, factor_sin):
    real_part = values[0] * factor_cos - values[1] * factor_sin
    imag_part = values[1] * factor_cos + values[0] * factor_sin
    return jnp.stack([real_part, imag_part])


def rotate_neg(values):
    return jnp.stack([values[1], -values[0]])


def rotate_pos(values):
    return jnp.stack([-values[1], values[0]])


def times_i(re, im, sign):
    return (-sign * im, sign * re)


def dft4(parts, sign):
    (r0, i0), (r1, i1), (r2, i2), (r3, i3) = parts
    ar, ai = r0 + r2, i0 + i2
    br, bi = r0 - r2, i0 - i2
    cr, ci = r1 + r3, i1 + i3
    dr, di = times_i(r1 - r3, i1 - i3, sign)
    return [(ar + cr, ai + ci), (br + dr, bi + di), (ar - cr, ai - ci), (br - dr, bi - di)]


def y_forward(spectral):
    parts = [(spectral[0, ..., 128 * a:128 * a + 128], spectral[1, ..., 128 * a:128 * a + 128]) for a in range(4)]
    mixed = dft4(parts, -1)
    lanes = lax.broadcasted_iota(jnp.int32, (128,), 0)
    out = []
    for k1 in range(4):
        tw_cos, tw_sin = cos_sin(lanes * k1, 512)
        re, im = mixed[k1]
        out.append(jnp.stack([re * tw_cos + im * tw_sin, im * tw_cos - re * tw_sin]))
    stacked = jnp.stack(out, axis=-2).reshape(384, 128)
    product = matmul("kb,rb->kr", stacked_table(128, 0), stacked)
    re, im = combine_rows(product, -1)
    return jnp.concatenate([re, im], axis=1)


def y_inverse(returned):
    product = matmul("kr,kb->rb", returned, stacked_table(128, 1))
    c_re = product[:192, :128]
    s_re = product[:192, 128:]
    c_im = product[192:, :128]
    s_im = product[192:, 128:]
    re = (c_re - s_im).reshape(3, 2, 8, 4, 128)
    im = (c_im + s_re).reshape(3, 2, 8, 4, 128)
    lanes = lax.broadcasted_iota(jnp.int32, (128,), 0)
    parts = []
    for k1 in range(4):
        tw_cos, tw_sin = cos_sin(lanes * k1, 512)
        r = re[..., k1, :]
        i = im[..., k1, :]
        parts.append((r * tw_cos - i * tw_sin, i * tw_cos + r * tw_sin))
    mixed = dft4(parts, 1)
    real_part = jnp.concatenate([m[0] for m in mixed], axis=-1)
    imag_part = jnp.concatenate([m[1] for m in mixed], axis=-1)
    return jnp.stack([real_part, imag_part])


def z_twiddle(re, im, sign):
    rows_idx = lax.broadcasted_iota(jnp.int32, (128, 192), 0)
    cols_idx = lax.broadcasted_iota(jnp.int32, (128, 192), 1)
    tw_cos, tw_sin = cos_sin(rows_idx * ((cols_idx // 4) % 8), 1024)
    tw_sin = sign * tw_sin
    return jnp.concatenate([re * tw_cos - im * tw_sin, im * tw_cos + re * tw_sin], axis=1)


def shards(fields, eigenstrain, moduli):
    gy_count = lax.axis_size("gy")
    gy_index = lax.axis_index("gy")
    gz_index = lax.axis_index("gz")
    low_bit = gy_index % 2
    high_bit = gy_index // 2
    y_local = fields.shape[4]
    positions = lax.broadcasted_iota(jnp.int32, (y_local,), 0)
    partner = partner_2(fields, "gy", 1)
    halves = jnp.where(high_bit == 1, partner - fields, fields + partner)
    halves = jnp.where(high_bit * low_bit == 1, rotate_neg(halves), halves)
    partner = partner_2(halves, "gy", 0)
    spectral = jnp.where(low_bit == 1, partner - halves, halves + partner)
    residue = 2 * low_bit + high_bit
    angle = 2.0 * math.pi / NY * (positions * residue % NY).astype(jnp.float32)
    phase_cos = jnp.cos(angle)
    phase_sin = jnp.sin(angle)
    spectral = twiddle(spectral, phase_cos, -phase_sin)
    slabs = y_forward(spectral)
    pencils = lax.all_to_all(slabs, "gz", split_axis=0, concat_axis=0, tiled=True)
    table = stacked_table(128, 0)
    re, im = combine_rows(matmul("kg,gc->kc", table, pencils), -1)
    spectrum = jnp.dot(z_twiddle(re, im, -1), block_dft8(False), precision=highest)
    rows_idx = lax.broadcasted_iota(jnp.int32, (128, 64), 0)
    cols_idx = lax.broadcasted_iota(jnp.int32, (128, 64), 1)
    plane = cols_idx // 32
    kz_index = rows_idx + 128 * ((cols_idx // 4) % 8)
    ky_index = residue + gy_count * (cols_idx % 4 + 4 * gz_index)
    kx_wave = plane.astype(jnp.float32) / NX
    ky_wave = signed_wave(ky_index, NY)
    kz_wave = signed_wave(kz_index, NZ)
    kernel = kernel_rows(kx_wave, ky_wave, kz_wave, eigenstrain, moduli)
    scale = 1.0 / (NY * NZ)
    spec = spectrum.reshape(128, 2, 3, 64)
    forced = jnp.stack(
        [
            jnp.stack(
                [
                    sum((kernel[source][target] * spec[:, part, target] for target in range(3))) * scale
                    for source in range(3)
                ],
                axis=1,
            )
            for part in range(2)
        ],
        axis=1,
    ).reshape(128, 384)
    back = jnp.dot(forced, block_dft8(True), precision=highest)
    back = z_twiddle(back[:, :192], back[:, 192:], 1)
    re, im = combine_rows(matmul("kg,gc->kc", table, back), 1)
    back = jnp.concatenate([re, im], axis=1)
    returned = lax.all_to_all(back, "gz", split_axis=0, concat_axis=0, tiled=True)
    spatial = y_inverse(returned)
    spatial = twiddle(spatial, phase_cos, phase_sin)
    partner = partner_2(spatial, "gy", 0)
    halves = jnp.where(low_bit == 1, partner - spatial, spatial + partner)
    halves = jnp.where(high_bit * low_bit == 1, rotate_pos(halves), halves)
    partner = partner_2(halves, "gy", 1)
    result = jnp.where(high_bit == 1, partner - halves, halves + partner)
    return result


def solution(mesh):
    in_specs = (P(None, None, None, "gz", "gy"), P(), P())
    out_specs = P(None, None, None, "gz", "gy")
    return jax.shard_map(shards, mesh=mesh, in_specs=in_specs, out_specs=out_specs, check_vma=False)
```

profile of v0, /device:TPU:1, one launch (start us, length us, event | category | flops | bytes accessed | tf_op | source)
XLA Modules:
  0.0 164.0 jit_solution(5526428606163635631)
XLA Ops:
  0.0 3.9 %collective-permute-start = (f32[2,3,2,8,512]{4,3,2,1,0:T(8,128)}, f32[2,3,2,8,512]{4,3,2,1,0:T(8,128)S(1)}, u32[]{:S(2)}, u32[]{:S(2)}) collective-permute-start(f32[2,3,2,8,512]{4,3,2,1,0:T(8,128)} %param.3), channel_id=1, source_target_pairs={{0,256},{128,384},{256,0},{384,128},{1,257},{129,385},{257,1},{385... | collective-permute-start | bytes 589832 | tf_op jit(solution)/shard_map/ppermute | solution.py:19
  4.0 0.1 fusion.83
  4.1 0.0 copy-start.1
  4.1 0.1 fusion.81
  4.1 0.6 copy-done.1
  4.8 0.7 fusion.98
  5.5 0.0 copy-done.2
  5.5 0.6 fusion.99
  11.7 0.0 copy-start
  62.5 0.1 fusion.72
  62.8 0.1 fusion.68
  62.8 0.0 collective-permute-done
  62.8 0.0 copy-done
  62.9 6.8 %collective-permute-start.1 = (f32[2,3,2,8,512]{4,3,2,1,0:T(8,128)S(1)}, f32[2,3,2,8,512]{4,3,2,1,0:T(8,128)S(1)}, u32[]{:S(2)}, u32[]{:S(2)}) collective-permute-start(f32[2,3,2,8,512]{4,3,2,1,0:T(8,128)S(1)} %maximum_select_fusion), channel_id=1, source_target_pairs={{0,128},{128,0},{256,384},{384,256},{1,129},{129,1},{257,385},{385... | collective-permute-start | bytes 589832 | tf_op jit(solution)/shard_map/ppermute | solution.py:19
  69.7 0.3 fusion.59
  70.0 0.8 collective-permute-done.1
  71.0 0.1 copy.27
  71.1 0.5 fusion.38
  71.6 0.1 slice_add_fusion.2
  71.8 0.1 maximum_bitcast_fusion
  71.9 0.9 copy.28
  72.7 18.1 %all-to-all-start = ((f32[128,1,384]{2,1,0:T(1,128)}), f32[128,1,384]{2,1,0:T(1,128)S(1)}, u32[]{:S(2)}, u32[]{:S(2)}) async-start(f32[128,1,384]{2,1,0:T(1,128)} %copy.28), calls=%async_computation | async-start | bytes 393216 | tf_op jit(solution)/shard_map/all_to_all | solution.py:237
  90.9 1.6 fusion.62
  92.5 18.8 %all-to-all-done = f32[128,1,384]{2,1,0:T(1,128)S(1)} async-done(((f32[128,1,384]{2,1,0:T(1,128)}), f32[128,1,384]{2,1,0:T(1,128)S(1)}, u32[]{:S(2)}, u32[]{:S(2)}) %all-to-all-start) | async-done | bytes 196640 | tf_op jit(solution)/shard_map/all_to_all | solution.py:237
  111.3 0.5 fusion.26
  111.8 0.6 multiply_subtract_fusion.1
  112.4 1.3 fusion.1
  113.7 0.9 add_multiply_fusion.5
  114.6 0.9 add_multiply_fusion.2
  115.5 0.9 add_multiply_fusion.4
  116.4 0.9 add_multiply_fusion.1
  117.2 0.9 add_multiply_fusion.3
  118.1 0.9 add_multiply_fusion
  119.1 0.8 fusion.4
  119.8 0.6 multiply_subtract_fusion
  120.4 0.5 fusion.19
  121.0 0.1 slice_subtract_fusion
  121.1 0.1 maximum_bitcast_fusion.1
  121.2 0.2 copy.30
  121.4 25.8 %all_to_all.24 = f32[128,1,384]{2,1,0:T(1,128)S(1)} all-to-all(f32[128,1,384]{2,1,0:T(1,128)S(1)} %copy.30), channel_id=1, replica_groups=mesh['gy'=4,'gz'=128] {'gz'}, dimensions={0} | all-to-all | bytes 393216 | tf_op jit(solution)/shard_map/all_to_all | solution.py:269
  147.2 0.5 fusion.23
  147.7 0.1 fusion.96
  147.8 0.1 fusion.97
  148.1 6.0 %collective-permute-start.2 = (f32[2,3,2,8,512]{4,3,2,1,0:T(8,128)S(1)}, f32[2,3,2,8,512]{4,3,2,1,0:T(8,128)S(1)}, u32[]{:S(2)}, u32[]{:S(2)}) collective-permute-start(f32[2,3,2,8,512]{4,3,2,1,0:T(8,128)S(1)} %pad_maximum_fusion.8), channel_id=1, source_target_pairs={{0,128},{128,0},{256,384},{384,256},{1,129},{129,1},{257,385},{385... | collective-permute-start | bytes 589832 | tf_op jit(solution)/shard_map/ppermute | solution.py:19
  154.1 1.0 collective-permute-done.2
  155.3 1.9 %collective-permute-start.3 = (f32[2,3,2,8,512]{4,3,2,1,0:T(8,128)S(1)}, f32[2,3,2,8,512]{4,3,2,1,0:T(8,128)S(1)}, u32[]{:S(2)}, u32[]{:S(2)}) collective-permute-start(f32[2,3,2,8,512]{4,3,2,1,0:T(8,128)S(1)} %maximum_select_fusion.1), channel_id=1, source_target_pairs={{0,256},{128,384},{256,0},{384,128},{1,257},{129,385},{257,1},{385... | collective-permute-start | bytes 589832 | tf_op jit(solution)/shard_map/ppermute | solution.py:19
  157.2 6.1 %collective-permute-done.3 = f32[2,3,2,8,512]{4,3,2,1,0:T(8,128)S(1)} collective-permute-done((f32[2,3,2,8,512]{4,3,2,1,0:T(8,128)S(1)}, f32[2,3,2,8,512]{4,3,2,1,0:T(8,128)S(1)}, u32[]{:S(2)}, u32[]{:S(2)}) %collective-permute-start.3) | collective-permute-done | bytes 196640 | tf_op jit(solution)/shard_map/ppermute | solution.py:19
  163.3 0.7 add_select_fusion.3
  (38 shorter events, 0.6 us)
Async XLA Ops:
  0.0 62.8 %collective-permute-start = (f32[2,3,2,8,512]{4,3,2,1,0:T(8,128)}, f32[2,3,2,8,512]{4,3,2,1,0:T(8,128)S(1)}, u32[]{:S(2)}, u32[]{:S(2)}) collective-permute-start(f32[2,3,2,8,512]{4,3,2,1,0:T(8,128)} %param.3), channel_id=1, source_target_pairs={{0,256},{128,384},{256,0},{384,128},{1,257},{129,385},{257,1},{385... | collective-permute-start | bytes 589832 | tf_op jit(solution)/shard_map/ppermute | solution.py:19
  4.1 0.7 copy-start.1
  4.8 0.7 copy-start.2
  11.7 51.1 %copy-start = (f32[2,3,2,8,512]{4,3,2,1,0:T(8,128)S(1)}, f32[2,3,2,8,512]{4,3,2,1,0:T(8,128)}, u32[]{:S(2)}) copy-start(f32[2,3,2,8,512]{4,3,2,1,0:T(8,128)} %param.3) | copy-start | bytes 589828
  62.9 7.8 %collective-permute-start.1 = (f32[2,3,2,8,512]{4,3,2,1,0:T(8,128)S(1)}, f32[2,3,2,8,512]{4,3,2,1,0:T(8,128)S(1)}, u32[]{:S(2)}, u32[]{:S(2)}) collective-permute-start(f32[2,3,2,8,512]{4,3,2,1,0:T(8,128)S(1)} %maximum_select_fusion), channel_id=1, source_target_pairs={{0,128},{128,0},{256,384},{384,256},{1,129},{129,1},{257,385},{385... | collective-permute-start | bytes 589832 | tf_op jit(solution)/shard_map/ppermute | solution.py:19
  72.7 38.6 %all-to-all-start = ((f32[128,1,384]{2,1,0:T(1,128)}), f32[128,1,384]{2,1,0:T(1,128)S(1)}, u32[]{:S(2)}, u32[]{:S(2)}) async-start(f32[128,1,384]{2,1,0:T(1,128)} %copy.28), calls=%async_computation | async-start | bytes 393216 | tf_op jit(solution)/shard_map/all_to_all | solution.py:237
  148.1 7.1 %collective-permute-start.2 = (f32[2,3,2,8,512]{4,3,2,1,0:T(8,128)S(1)}, f32[2,3,2,8,512]{4,3,2,1,0:T(8,128)S(1)}, u32[]{:S(2)}, u32[]{:S(2)}) collective-permute-start(f32[2,3,2,8,512]{4,3,2,1,0:T(8,128)S(1)} %pad_maximum_fusion.8), channel_id=1, source_target_pairs={{0,128},{128,0},{256,384},{384,256},{1,129},{129,1},{257,385},{385... | collective-permute-start | bytes 589832 | tf_op jit(solution)/shard_map/ppermute | solution.py:19
  155.3 8.0 %collective-permute-start.3 = (f32[2,3,2,8,512]{4,3,2,1,0:T(8,128)S(1)}, f32[2,3,2,8,512]{4,3,2,1,0:T(8,128)S(1)}, u32[]{:S(2)}, u32[]{:S(2)}) collective-permute-start(f32[2,3,2,8,512]{4,3,2,1,0:T(8,128)S(1)} %maximum_select_fusion.1), channel_id=1, source_target_pairs={{0,256},{128,384},{256,0},{384,128},{1,257},{129,385},{257,1},{385... | collective-permute-start | bytes 589832 | tf_op jit(solution)/shard_map/ppermute | solution.py:19
where the time goes:
time: 165 us; the launch traced here: 164 us
  between operations  57.1 us (35%)
  starting transfers between devices  36.8 us (22%)
  waiting for transfers between devices  26.7 us (16%)
  blocking collectives  25.8 us (16%)
  other arithmetic  10.4 us (6%)
  matrix products  4.05 us (2%)
  local copies, waits for them, and re-layouts  3.28 us (2%)
    all_to_all x1, blocking collectives, shards(): lax.all_to_all(back, 'gz', split_axis=0, concat_axis=0, tiled=True)  25.8 us
    all_to_all x1, waiting for transfers between devices, shards(): lax.all_to_all(slabs, 'gz', split_axis=0, concat_axis=0, tiled=True)  18.8 us
    ppermute x4, starting transfers between devices, partner_2(): return lax.ppermute(value, axis, pairs)  18.7 us
    all_to_all x1, starting transfers between devices, shards(): lax.all_to_all(slabs, 'gz', split_axis=0, concat_axis=0, tiled=True)  18.1 us
    ppermute x4, waiting for transfers between devices, partner_2(): return lax.ppermute(value, axis, pairs)  7.89 us
    mul x6, other arithmetic, shards(): sum((kernel[source][target] * spec[:, part, target] for target in range(3)))  5.28 us
  transfers between devices with their start and end apart: 5, of which 4 were waited for; matrix products, arithmetic and copies ran while one was open for 2% of the time, Pallas kernels for 0%

commit v1 on v0

--- a/solution.py
+++ b/solution.py
@@ -23,18 +23,29 @@
     return jnp.where(index < length // 2, index, index - length).astype(jnp.float32) / length
 
 
-def voigt_tensor(entries):
-    return [
-        [entries[0], entries[5], entries[4]],
-        [entries[5], entries[1], entries[3]],
-        [entries[4], entries[3], entries[2]],
-    ]
-
-
 def kernel_rows(kx_wave, ky_wave, kz_wave, eigenstrain, moduli):
-    stiff_a = moduli[0]
-    stiff_b = moduli[1]
-    shear = moduli[2]
+    constants = moduli.reshape(3, 1, 1)
+    stiff_a = constants[0]
+    stiff_b = constants[1]
+    shear = constants[2]
+    strain = eigenstrain
+    trace = strain[:, 0:1] + strain[:, 1:2] + strain[:, 2:3]
+    stress = jnp.concatenate(
+        [
+            moduli[1:2] * trace + (moduli[0:1] - moduli[1:2]) * strain[:, 0:3],
+            2.0 * moduli[2:3] * strain[:, 3:6],
+        ],
+        axis=1,
+    )
+    voigt = [[0, 5, 4], [5, 1, 3], [4, 3, 2]]
+    energy = sum(
+        (
+            stress[:, None, voigt[first][second]] * strain[None, :, voigt[first][second]]
+            for first in range(3)
+            for second in range(3)
+        )
+    ).reshape(3, 3, 1, 1)
+    stress_b = stress.reshape(3, 6, 1, 1)
     square = kx_wave * kx_wave + ky_wave * ky_wave + kz_wave * kz_wave
     inside = square > 0.0
     inverse = lax.rsqrt(jnp.where(inside, square, 1.0))
@@ -57,20 +68,11 @@
         [cof_zo * recip, cof_oo * recip, cof_ot * recip],
         [cof_zt * recip, cof_ot * recip, cof_tt * recip],
     ]
-    strains = []
-    stresses = []
-    for variant in range(3):
-        entries = [eigenstrain[variant, column] for column in range(6)]
-        trace = entries[0] + entries[1] + entries[2]
-        stress = [stiff_b * trace + (stiff_a - stiff_b) * entries[column] for column in range(3)]
-        stress = stress + [2.0 * shear * entries[column] for column in range(3, 6)]
-        strains.append(voigt_tensor(entries))
-        stresses.append(voigt_tensor(stress))
     traction = []
     for variant in range(3):
         traction.append(
             [
-                sum((stresses[variant][first][second] * normal[second] for second in range(3)))
+                sum((stress_b[variant, voigt[first][second]] * normal[second] for second in range(3)))
                 for first in range(3)
             ]
         )
@@ -86,17 +88,10 @@
     for source in range(3):
         kernel_row = []
         for target in range(3):
-            energy = sum(
-                (
-                    stresses[source][first][second] * strains[target][first][second]
-                    for first in range(3)
-                    for second in range(3)
-                )
-            )
             coupling = sum(
                 (traction[source][first] * response[target][first] for first in range(3))
             )
-            kernel_row.append(jnp.where(inside, energy - coupling, 0.0))
+            kernel_row.append(jnp.where(inside, energy[source, target] - coupling, 0.0))
         kernel.append(kernel_row)
     return kernel
 
@@ -219,8 +214,8 @@
     gy_count = lax.axis_size("gy")
     gy_index = lax.axis_index("gy")
     gz_index = lax.axis_index("gz")
-    low_bit = gy_index % 2
-    high_bit = gy_index // 2
+    low_bit = lax.rem(gy_index, 2)
+    high_bit = lax.div(gy_index, 2)
     y_local = fields.shape[4]
     positions = lax.broadcasted_iota(jnp.int32, (y_local,), 0)
     partner = partner_2(fields, "gy", 1)

time: 165 us -> 194 us (1.18)
  other arithmetic: 10.4 us -> 91.2 us
  between operations: 57.1 us -> 4.74 us
    mul x6, other arithmetic: 5.28 us -> 84 us  [shards(): sum((kernel[source][target] * spec[:, part, target] for target in range(3)))]
  transfers between devices with their start and end apart: 5 -> 5, of which waited for: 4 -> 4; matrix products, arithmetic and copies ran while one was open for 2% -> 3% of each run, Pallas kernels for 0% -> 0%
where the time goes in v1:
time: 194 us; the launch traced here: 193 us
  other arithmetic  91.2 us (47%)
  starting transfers between devices  36.8 us (19%)
  blocking collectives  25.8 us (13%)
  waiting for transfers between devices  25.3 us (13%)
  local copies, waits for them, and re-layouts  4.87 us (3%)
  between operations  4.74 us (2%)
  matrix products  4.06 us (2%)
    mul x6, other arithmetic, shards(): sum((kernel[source][target] * spec[:, part, target] for target in range(3)))  84 us
    all_to_all x1, blocking collectives, shards(): lax.all_to_all(back, 'gz', split_axis=0, concat_axis=0, tiled=True)  25.8 us
    ppermute x4, starting transfers between devices, partner_2(): return lax.ppermute(value, axis, pairs)  18.7 us
    all_to_all x1, starting transfers between devices, shards(): lax.all_to_all(slabs, 'gz', split_axis=0, concat_axis=0, tiled=True)  18.1 us
    all_to_all x1, waiting for transfers between devices, shards(): lax.all_to_all(slabs, 'gz', split_axis=0, concat_axis=0, tiled=True)  17.4 us
    ppermute x4, waiting for transfers between devices, partner_2(): return lax.ppermute(value, axis, pairs)  7.89 us
  transfers between devices with their start and end apart: 5, of which 4 were waited for; matrix products, arithmetic and copies ran while one was open for 3% of the time, Pallas kernels for 0%

profile of v1, /device:TPU:1, one launch (start us, length us, event | category | flops | bytes accessed | tf_op | source)
XLA Modules:
  0.0 192.7 jit_solution(12898305845136739792)
XLA Ops:
  0.0 3.9 %collective-permute-start = (f32[2,3,2,8,512]{4,3,2,1,0:T(8,128)}, f32[2,3,2,8,512]{4,3,2,1,0:T(8,128)S(1)}, u32[]{:S(2)}, u32[]{:S(2)}) collective-permute-start(f32[2,3,2,8,512]{4,3,2,1,0:T(8,128)} %param.3), channel_id=1, source_target_pairs={{0,256},{128,384},{256,0},{384,128},{1,257},{129,385},{257,1},{385... | collective-permute-start | bytes 589832 | tf_op jit(solution)/shard_map/ppermute | solution.py:19
  4.0 0.1 fusion.74
  4.3 0.6 copy-done.1
  4.9 0.6 fusion.102
  9.8 0.7 copy-done
  10.5 0.9 slice_reduce_fusion.11
  11.4 0.1 multiply_add_fusion.37
  11.5 0.1 maximum_bitcast_fusion.8
  11.6 0.3 slice_reduce_fusion.7
  11.8 1.0 add_select_fusion.8
  12.9 6.8 %collective-permute-start.1 = (f32[2,3,2,8,512]{4,3,2,1,0:T(8,128)S(1)}, f32[2,3,2,8,512]{4,3,2,1,0:T(8,128)S(1)}, u32[]{:S(2)}, u32[]{:S(2)}) collective-permute-start(f32[2,3,2,8,512]{4,3,2,1,0:T(8,128)S(1)} %maximum_select_fusion), channel_id=1, source_target_pairs={{0,128},{128,0},{256,384},{384,256},{1,129},{129,1},{257,385},{385... | collective-permute-start | bytes 589832 | tf_op jit(solution)/shard_map/ppermute | solution.py:19
  19.7 0.3 fusion.59
  19.9 0.8 collective-permute-done.1
  20.9 0.1 copy.27
  21.1 0.5 fusion.38
  21.6 0.1 slice_add_fusion.2
  21.7 0.1 maximum_bitcast_fusion
  21.8 0.9 copy.28
  22.7 18.1 %all-to-all-start = ((f32[128,1,384]{2,1,0:T(1,128)}), f32[128,1,384]{2,1,0:T(1,128)S(1)}, u32[]{:S(2)}, u32[]{:S(2)}) async-start(f32[128,1,384]{2,1,0:T(1,128)} %copy.28), calls=%async_computation | async-start | bytes 393216 | tf_op jit(solution)/shard_map/all_to_all | solution.py:232
  40.8 0.1 fusion.63
  41.0 0.6 fusion.100
  41.6 0.7 fusion.101
  42.3 1.6 fusion.64
  43.9 17.4 %all-to-all-done = f32[128,1,384]{2,1,0:T(1,128)S(1)} async-done(((f32[128,1,384]{2,1,0:T(1,128)}), f32[128,1,384]{2,1,0:T(1,128)S(1)}, u32[]{:S(2)}, u32[]{:S(2)}) %all-to-all-start) | async-done | bytes 196640 | tf_op jit(solution)/shard_map/all_to_all | solution.py:232
  61.3 0.5 fusion.26
  61.7 0.6 multiply_subtract_fusion.1
  62.3 1.3 fusion.1
  63.6 14.0 %add_multiply_fusion.5 = f32[128,1,64]{0,2,1:T(8,128)S(1)} fusion(f32[128,2,3,64]{0,3,2,1:T(8,128)S(1)} %bitcast.152, f32[]{:T(128)} %bitcast.13, f32[]{:T(128)} %bitcast.12, f32[]{:T(128)} %bitcast.11, f32[]{:T(128)} %bitcast.10, f32[]{:T(128)} %bitcast.9, f32[]{:T(128)} %bitcast.8, f32[]{:T(128)} %bitcast.7, f32[]{:T(128)} %bitcast.6, f32[]{:T(128)} %bitcast.5, ...), kind=kLoop, calls=%fused_computation.152 | loop fusion | flops 1654784 | bytes 132904 | tf_op jit(solution)/shard_map/mul | solution.py:251
  77.7 14.0 %add_multiply_fusion.2 = f32[128,1,64]{0,2,1:T(8,128)S(1)} fusion(f32[128,2,3,64]{0,3,2,1:T(8,128)S(1)} %bitcast.153, f32[]{:T(128)} %bitcast.13, f32[]{:T(128)} %bitcast.12, f32[]{:T(128)} %bitcast.11, f32[]{:T(128)} %bitcast.10, f32[]{:T(128)} %bitcast.9, f32[]{:T(128)} %bitcast.8, f32[]{:T(128)} %bitcast.7, f32[]{:T(128)} %bitcast.6, f32[]{:T(128)} %bitcast.5, ...), kind=kLoop, calls=%fused_computation.143 | loop fusion | flops 1654784 | bytes 132904 | tf_op jit(solution)/shard_map/mul | solution.py:251
  91.7 13.9 %add_multiply_fusion.4 = f32[128,1,64]{0,2,1:T(8,128)S(1)} fusion(f32[128,2,3,64]{0,3,2,1:T(8,128)S(1)} %bitcast.154, f32[]{:T(128)} %bitcast.28, f32[]{:T(128)} %bitcast.27, f32[]{:T(128)} %bitcast.26, f32[]{:T(128)} %bitcast.10, f32[]{:T(128)} %bitcast.9, f32[]{:T(128)} %bitcast.8, f32[]{:T(128)} %bitcast.25, f32[]{:T(128)} %bitcast.24, f32[]{:T(128)} %bitcast.23, ...), kind=kLoop, calls=%fused_computation.148 | loop fusion | flops 1654784 | bytes 132904 | tf_op jit(solution)/shard_map/mul | solution.py:251
  105.7 13.9 %add_multiply_fusion.1 = f32[128,1,64]{0,2,1:T(8,128)S(1)} fusion(f32[128,2,3,64]{0,3,2,1:T(8,128)S(1)} %bitcast.155, f32[]{:T(128)} %bitcast.28, f32[]{:T(128)} %bitcast.27, f32[]{:T(128)} %bitcast.26, f32[]{:T(128)} %bitcast.10, f32[]{:T(128)} %bitcast.9, f32[]{:T(128)} %bitcast.8, f32[]{:T(128)} %bitcast.25, f32[]{:T(128)} %bitcast.24, f32[]{:T(128)} %bitcast.23, ...), kind=kLoop, calls=%fused_computation.142 | loop fusion | flops 1654784 | bytes 132904 | tf_op jit(solution)/shard_map/mul | solution.py:251
  119.6 14.0 %add_multiply_fusion.3 = f32[128,1,64]{0,2,1:T(8,128)S(1)} fusion(f32[128,2,3,64]{0,3,2,1:T(8,128)S(1)} %bitcast.156, f32[]{:T(128)} %bitcast.36, f32[]{:T(128)} %bitcast.35, f32[]{:T(128)} %bitcast.34, f32[]{:T(128)} %bitcast.10, f32[]{:T(128)} %bitcast.9, f32[]{:T(128)} %bitcast.8, f32[]{:T(128)} %bitcast.33, f32[]{:T(128)} %bitcast.32, f32[]{:T(128)} %bitcast.31, ...), kind=kLoop, calls=%fused_computation.144 | loop fusion | flops 1654784 | bytes 132904 | tf_op jit(solution)/shard_map/mul | solution.py:251
  133.6 14.0 %add_multiply_fusion = f32[128,1,64]{0,2,1:T(8,128)S(1)} fusion(f32[128,2,3,64]{0,3,2,1:T(8,128)S(1)} %bitcast.157, f32[]{:T(128)} %bitcast.36, f32[]{:T(128)} %bitcast.35, f32[]{:T(128)} %bitcast.34, f32[]{:T(128)} %bitcast.10, f32[]{:T(128)} %bitcast.9, f32[]{:T(128)} %bitcast.8, f32[]{:T(128)} %bitcast.33, f32[]{:T(128)} %bitcast.32, f32[]{:T(128)} %bitcast.31, ...), kind=kLoop, calls=%fused_computation.141 | loop fusion | flops 1654784 | bytes 132904 | tf_op jit(solution)/shard_map/mul | solution.py:251
  147.7 0.8 fusion.4
  148.5 0.6 multiply_subtract_fusion
  149.1 0.5 fusion.19
  149.6 0.1 slice_subtract_fusion
  149.8 0.1 maximum_bitcast_fusion.1
  149.9 0.2 copy.30
  150.1 25.8 %all_to_all.24 = f32[128,1,384]{2,1,0:T(1,128)S(1)} all-to-all(f32[128,1,384]{2,1,0:T(1,128)S(1)} %copy.30), channel_id=1, replica_groups=mesh['gy'=4,'gz'=128] {'gz'}, dimensions={0} | all-to-all | bytes 393216 | tf_op jit(solution)/shard_map/all_to_all | solution.py:264
  175.9 0.5 fusion.23
  176.4 0.1 fusion.98
  176.5 0.1 fusion.99
  176.8 6.0 %collective-permute-start.2 = (f32[2,3,2,8,512]{4,3,2,1,0:T(8,128)S(1)}, f32[2,3,2,8,512]{4,3,2,1,0:T(8,128)S(1)}, u32[]{:S(2)}, u32[]{:S(2)}) collective-permute-start(f32[2,3,2,8,512]{4,3,2,1,0:T(8,128)S(1)} %pad_maximum_fusion.8), channel_id=1, source_target_pairs={{0,128},{128,0},{256,384},{384,256},{1,129},{129,1},{257,385},{385... | collective-permute-start | bytes 589832 | tf_op jit(solution)/shard_map/ppermute | solution.py:19
  182.8 1.0 collective-permute-done.2
  184.0 1.9 collective-permute-start.3
  185.9 6.1 %collective-permute-done.3 = f32[2,3,2,8,512]{4,3,2,1,0:T(8,128)S(1)} collective-permute-done((f32[2,3,2,8,512]{4,3,2,1,0:T(8,128)S(1)}, f32[2,3,2,8,512]{4,3,2,1,0:T(8,128)S(1)}, u32[]{:S(2)}, u32[]{:S(2)}) %collective-permute-start.3) | collective-permute-done | bytes 196640 | tf_op jit(solution)/shard_map/ppermute | solution.py:19
  192.0 0.7 add_select_fusion.3
  (42 shorter events, 0.8 us)
Async XLA Ops:
  0.0 11.8 %collective-permute-start = (f32[2,3,2,8,512]{4,3,2,1,0:T(8,128)}, f32[2,3,2,8,512]{4,3,2,1,0:T(8,128)S(1)}, u32[]{:S(2)}, u32[]{:S(2)}) collective-permute-start(f32[2,3,2,8,512]{4,3,2,1,0:T(8,128)} %param.3), channel_id=1, source_target_pairs={{0,256},{128,384},{256,0},{384,128},{1,257},{129,385},{257,1},{385... | collective-permute-start | bytes 589832 | tf_op jit(solution)/shard_map/ppermute | solution.py:19
  4.3 0.7 copy-start.1
  9.8 0.7 copy-start
  12.9 7.8 %collective-permute-start.1 = (f32[2,3,2,8,512]{4,3,2,1,0:T(8,128)S(1)}, f32[2,3,2,8,512]{4,3,2,1,0:T(8,128)S(1)}, u32[]{:S(2)}, u32[]{:S(2)}) collective-permute-start(f32[2,3,2,8,512]{4,3,2,1,0:T(8,128)S(1)} %maximum_select_fusion), channel_id=1, source_target_pairs={{0,128},{128,0},{256,384},{384,256},{1,129},{129,1},{257,385},{385... | collective-permute-start | bytes 589832 | tf_op jit(solution)/shard_map/ppermute | solution.py:19
  22.7 38.6 %all-to-all-start = ((f32[128,1,384]{2,1,0:T(1,128)}), f32[128,1,384]{2,1,0:T(1,128)S(1)}, u32[]{:S(2)}, u32[]{:S(2)}) async-start(f32[128,1,384]{2,1,0:T(1,128)} %copy.28), calls=%async_computation | async-start | bytes 393216 | tf_op jit(solution)/shard_map/all_to_all | solution.py:232
  176.8 7.1 %collective-permute-start.2 = (f32[2,3,2,8,512]{4,3,2,1,0:T(8,128)S(1)}, f32[2,3,2,8,512]{4,3,2,1,0:T(8,128)S(1)}, u32[]{:S(2)}, u32[]{:S(2)}) collective-permute-start(f32[2,3,2,8,512]{4,3,2,1,0:T(8,128)S(1)} %pad_maximum_fusion.8), channel_id=1, source_target_pairs={{0,128},{128,0},{256,384},{384,256},{1,129},{129,1},{257,385},{385... | collective-permute-start | bytes 589832 | tf_op jit(solution)/shard_map/ppermute | solution.py:19
  184.0 8.0 %collective-permute-start.3 = (f32[2,3,2,8,512]{4,3,2,1,0:T(8,128)S(1)}, f32[2,3,2,8,512]{4,3,2,1,0:T(8,128)S(1)}, u32[]{:S(2)}, u32[]{:S(2)}) collective-permute-start(f32[2,3,2,8,512]{4,3,2,1,0:T(8,128)S(1)} %maximum_select_fusion.1), channel_id=1, source_target_pairs={{0,256},{128,384},{256,0},{384,128},{1,257},{129,385},{257,1},{385... | collective-permute-start | bytes 589832 | tf_op jit(solution)/shard_map/ppermute | solution.py:19

commit v2 on v1

--- a/solution.py
+++ b/solution.py
@@ -46,6 +46,10 @@
         )
     ).reshape(3, 3, 1, 1)
     stress_b = stress.reshape(3, 6, 1, 1)
+    constants, stress_b, energy = lax.optimization_barrier((constants, stress_b, energy))
+    stiff_a = constants[0]
+    stiff_b = constants[1]
+    shear = constants[2]
     square = kx_wave * kx_wave + ky_wave * ky_wave + kz_wave * kz_wave
     inside = square > 0.0
     inverse = lax.rsqrt(jnp.where(inside, square, 1.0))
@@ -242,6 +246,7 @@
     ky_wave = signed_wave(ky_index, NY)
     kz_wave = signed_wave(kz_index, NZ)
     kernel = kernel_rows(kx_wave, ky_wave, kz_wave, eigenstrain, moduli)
+    kernel = lax.optimization_barrier(jnp.stack([jnp.stack(row) for row in kernel]))
     scale = 1.0 / (NY * NZ)
     spec = spectrum.reshape(128, 2, 3, 64)
     forced = jnp.stack(

time: 194 us -> 182 us (0.938)
  other arithmetic: 91.2 us -> 76.5 us
    mul x6 -> x2, other arithmetic: 84 us -> 0.07 us  [shards(): sum((kernel[source][target] * spec[:, part, target] for target in range(3)))]
    select_n x0 -> x9, other arithmetic: none -> 70.1 us  [kernel_rows(): kernel_row.append(jnp.where(inside, energy[source, target] - coupling, 0.0))]
  transfers between devices with their start and end apart: 5 -> 5, of which waited for: 4 -> 4; matrix products, arithmetic and copies ran while one was open for 3% -> 42% of each run, Pallas kernels for 0% -> 0%
where the time goes in v2:
time: 182 us; the launch traced here: 180 us
  other arithmetic  76.5 us (42%)
  starting transfers between devices  36.8 us (20%)
  waiting for transfers between devices  26.6 us (15%)
  blocking collectives  25.8 us (14%)
  local copies, waits for them, and re-layouts  5.74 us (3%)
  between operations  4.87 us (3%)
  matrix products  4.05 us (2%)
    select_n x9, other arithmetic, kernel_rows(): kernel_row.append(jnp.where(inside, energy[source, target] - coupling, 0.0))  70.1 us
    all_to_all x1, blocking collectives, shards(): lax.all_to_all(back, 'gz', split_axis=0, concat_axis=0, tiled=True)  25.8 us
    all_to_all x1, waiting for transfers between devices, shards(): lax.all_to_all(slabs, 'gz', split_axis=0, concat_axis=0, tiled=True)  18.8 us
    ppermute x4, starting transfers between devices, partner_2(): return lax.ppermute(value, axis, pairs)  18.7 us
    all_to_all x1, starting transfers between devices, shards(): lax.all_to_all(slabs, 'gz', split_axis=0, concat_axis=0, tiled=True)  18.1 us
    ppermute x4, waiting for transfers between devices, partner_2(): return lax.ppermute(value, axis, pairs)  7.85 us
  transfers between devices with their start and end apart: 5, of which 4 were waited for; matrix products, arithmetic and copies ran while one was open for 42% of the time, Pallas kernels for 0%

profile of v2, /device:TPU:1, one launch (start us, length us, event | category | flops | bytes accessed | tf_op | source)
XLA Modules:
  0.0 180.3 jit_solution(7696091987685473880)
XLA Ops:
  0.0 3.9 %collective-permute-start = (f32[2,3,2,8,512]{4,3,2,1,0:T(8,128)}, f32[2,3,2,8,512]{4,3,2,1,0:T(8,128)S(1)}, u32[]{:S(2)}, u32[]{:S(2)}) collective-permute-start(f32[2,3,2,8,512]{4,3,2,1,0:T(8,128)} %param.3), channel_id=1, source_target_pairs={{0,256},{128,384},{256,0},{384,128},{1,257},{129,385},{257,1},{385... | collective-permute-start | bytes 589832 | tf_op jit(solution)/shard_map/ppermute | solution.py:19
  4.1 0.6 copy-done.2
  4.7 0.6 fusion.103
  7.2 0.9 slice_reduce_fusion.11
  8.2 0.1 multiply_add_fusion.31
  8.2 0.1 maximum_bitcast_fusion.11
  8.3 0.3 slice_reduce_fusion.7
  8.6 0.1 fusion.67
  8.7 0.7 fusion.102
  11.8 0.7 fusion.101
  12.5 0.7 fusion.100
  13.2 5.2 %subtract_select_fusion.8 = f32[1,128,64]{1,2,0:T(8,128)S(1)} fusion(f32[]{:T(128)} %bitcast.5, f32[]{:T(128)} %bitcast.8, f32[]{:T(128)} %bitcast.7, s32[64]{0:T(128)S(1)} %get-tuple-element.141, s32[64]{0:T(128)S(1)} %get-tuple-element.144, pred[64]{0:T(512)(128)(4,1)S(1)} %compare_and_fusion.4, s32[]{:T(128)S(6)} %mul.4929, ...), kind=kLoop, calls=%fused_computation.180 | loop fusion | flops 999424 | bytes 34544 | tf_op jit(solution)/shard_map/jit(_where)/select_n | solution.py:98
  18.5 9.0 %subtract_select_fusion.2 = f32[1,128,64]{1,2,0:T(8,128)S(1)} fusion(f32[]{:T(128)} %bitcast.34, f32[]{:T(128)} %bitcast.25, f32[]{:T(128)} %bitcast.24, s32[64]{0:T(128)S(1)} %get-tuple-element.141, s32[64]{0:T(128)S(1)} %get-tuple-element.144, pred[64]{0:T(512)(128)(4,1)S(1)} %compare_and_fusion.4, s32[]{:T(128)S(6)} %mul.4929, ...), kind=kLoop, calls=%fused_computation.162 | loop fusion | flops 1122304 | bytes 34568 | tf_op jit(solution)/shard_map/jit(_where)/select_n | solution.py:98
  27.5 8.9 %subtract_select_fusion.6 = f32[1,128,64]{1,2,0:T(8,128)S(1)} fusion(f32[]{:T(128)} %bitcast.22, f32[]{:T(128)} %bitcast.8, f32[]{:T(128)} %bitcast.7, s32[64]{0:T(128)S(1)} %get-tuple-element.141, s32[64]{0:T(128)S(1)} %get-tuple-element.144, pred[64]{0:T(512)(128)(4,1)S(1)} %compare_and_fusion.4, s32[]{:T(128)S(6)} %mul.4929, ...), kind=kLoop, calls=%fused_computation.166 | loop fusion | flops 1122304 | bytes 34568 | tf_op jit(solution)/shard_map/jit(_where)/select_n | solution.py:98
  36.4 9.1 %subtract_select_fusion.7 = f32[1,128,64]{1,2,0:T(8,128)S(1)} fusion(f32[]{:T(128)} %bitcast.15, f32[]{:T(128)} %bitcast.8, f32[]{:T(128)} %bitcast.7, s32[64]{0:T(128)S(1)} %get-tuple-element.141, s32[64]{0:T(128)S(1)} %get-tuple-element.144, pred[64]{0:T(512)(128)(4,1)S(1)} %compare_and_fusion.4, s32[]{:T(128)S(6)} %mul.4929, ...), kind=kLoop, calls=%fused_computation.173 | loop fusion | flops 1122304 | bytes 34568 | tf_op jit(solution)/shard_map/jit(_where)/select_n | solution.py:98
  45.5 9.1 %subtract_select_fusion.5 = f32[1,128,64]{1,2,0:T(8,128)S(1)} fusion(f32[]{:T(128)} %bitcast.30, f32[]{:T(128)} %bitcast.18, f32[]{:T(128)} %bitcast.17, s32[64]{0:T(128)S(1)} %get-tuple-element.141, s32[64]{0:T(128)S(1)} %get-tuple-element.144, pred[64]{0:T(512)(128)(4,1)S(1)} %compare_and_fusion.4, s32[]{:T(128)S(6)} %mul.4929, ...), kind=kLoop, calls=%fused_computation.165 | loop fusion | flops 1122304 | bytes 34568 | tf_op jit(solution)/shard_map/jit(_where)/select_n | solution.py:98
  54.6 9.1 %subtract_select_fusion.3 = f32[1,128,64]{1,2,0:T(8,128)S(1)} fusion(f32[]{:T(128)} %bitcast.32, f32[]{:T(128)} %bitcast.18, f32[]{:T(128)} %bitcast.17, s32[64]{0:T(128)S(1)} %get-tuple-element.141, s32[64]{0:T(128)S(1)} %get-tuple-element.144, pred[64]{0:T(512)(128)(4,1)S(1)} %compare_and_fusion.4, s32[]{:T(128)S(6)} %mul.4929, ...), kind=kLoop, calls=%fused_computation.163 | loop fusion | flops 1122304 | bytes 34568 | tf_op jit(solution)/shard_map/jit(_where)/select_n | solution.py:98
  63.7 9.1 %subtract_select_fusion.1 = f32[1,128,64]{1,2,0:T(8,128)S(1)} fusion(f32[]{:T(128)} %bitcast.35, f32[]{:T(128)} %bitcast.25, f32[]{:T(128)} %bitcast.24, s32[64]{0:T(128)S(1)} %get-tuple-element.141, s32[64]{0:T(128)S(1)} %get-tuple-element.144, pred[64]{0:T(512)(128)(4,1)S(1)} %compare_and_fusion.4, s32[]{:T(128)S(6)} %mul.4929, ...), kind=kLoop, calls=%fused_computation.161 | loop fusion | flops 1122304 | bytes 34568 | tf_op jit(solution)/shard_map/jit(_where)/select_n | solution.py:98
  72.8 5.2 %subtract_select_fusion.4 = f32[1,128,64]{1,2,0:T(8,128)S(1)} fusion(f32[]{:T(128)} %bitcast.31, f32[]{:T(128)} %bitcast.18, f32[]{:T(128)} %bitcast.17, s32[64]{0:T(128)S(1)} %get-tuple-element.141, s32[64]{0:T(128)S(1)} %get-tuple-element.144, pred[64]{0:T(512)(128)(4,1)S(1)} %compare_and_fusion.4, s32[]{:T(128)S(6)} %mul.4929, ...), kind=kLoop, calls=%fused_computation.164 | loop fusion | flops 999424 | bytes 34544 | tf_op jit(solution)/shard_map/jit(_where)/select_n | solution.py:98
  78.1 5.3 %subtract_select_fusion = f32[1,128,64]{1,2,0:T(8,128)S(1)} fusion(f32[]{:T(128)} %bitcast.36, f32[]{:T(128)} %bitcast.25, f32[]{:T(128)} %bitcast.24, s32[64]{0:T(128)S(1)} %get-tuple-element.141, s32[64]{0:T(128)S(1)} %get-tuple-element.144, pred[64]{0:T(512)(128)(4,1)S(1)} %compare_and_fusion.4, s32[]{:T(128)S(6)} %mul.4929, ...), kind=kLoop, calls=%fused_computation.160 | loop fusion | flops 999424 | bytes 34544 | tf_op jit(solution)/shard_map/jit(_where)/select_n | solution.py:98
  83.6 0.8 copy-done
  84.4 6.8 %collective-permute-start.1 = (f32[2,3,2,8,512]{4,3,2,1,0:T(8,128)S(1)}, f32[2,3,2,8,512]{4,3,2,1,0:T(8,128)S(1)}, u32[]{:S(2)}, u32[]{:S(2)}) collective-permute-start(f32[2,3,2,8,512]{4,3,2,1,0:T(8,128)S(1)} %maximum_select_fusion), channel_id=1, source_target_pairs={{0,128},{128,0},{256,384},{384,256},{1,129},{129,1},{257,385},{385... | collective-permute-start | bytes 589832 | tf_op jit(solution)/shard_map/ppermute | solution.py:19
  91.3 0.3 fusion.59
  91.5 0.7 collective-permute-done.1
  92.5 0.1 copy.39
  92.6 0.5 fusion.38
  93.1 0.1 slice_add_fusion.2
  93.3 0.1 maximum_bitcast_fusion
  93.4 0.9 copy.40
  94.3 18.1 %all-to-all-start = ((f32[128,1,384]{2,1,0:T(1,128)}), f32[128,1,384]{2,1,0:T(1,128)S(1)}, u32[]{:S(2)}, u32[]{:S(2)}) async-start(f32[128,1,384]{2,1,0:T(1,128)} %copy.40), calls=%async_computation | async-start | bytes 393216 | tf_op jit(solution)/shard_map/all_to_all | solution.py:236
  112.5 1.6 fusion.62
  114.1 18.8 %all-to-all-done = f32[128,1,384]{2,1,0:T(1,128)S(1)} async-done(((f32[128,1,384]{2,1,0:T(1,128)}), f32[128,1,384]{2,1,0:T(1,128)S(1)}, u32[]{:S(2)}, u32[]{:S(2)}) %all-to-all-start) | async-done | bytes 196640 | tf_op jit(solution)/shard_map/all_to_all | solution.py:236
  132.8 0.5 fusion.26
  133.3 0.6 multiply_subtract_fusion.1
  133.9 1.3 fusion.1
  135.3 0.8 fusion.4
  136.1 0.6 multiply_subtract_fusion
  136.7 0.5 fusion.19
  137.2 0.1 slice_subtract_fusion
  137.4 0.1 maximum_bitcast_fusion.1
  137.5 0.2 copy.42
  137.7 25.8 %all_to_all.24 = f32[128,1,384]{2,1,0:T(1,128)S(1)} all-to-all(f32[128,1,384]{2,1,0:T(1,128)S(1)} %copy.42), channel_id=1, replica_groups=mesh['gy'=4,'gz'=128] {'gz'}, dimensions={0} | all-to-all | bytes 393216 | tf_op jit(solution)/shard_map/all_to_all | solution.py:269
  163.5 0.5 fusion.23
  164.4 6.1 %collective-permute-start.2 = (f32[2,3,2,8,512]{4,3,2,1,0:T(8,128)S(1)}, f32[2,3,2,8,512]{4,3,2,1,0:T(8,128)S(1)}, u32[]{:S(2)}, u32[]{:S(2)}) collective-permute-start(f32[2,3,2,8,512]{4,3,2,1,0:T(8,128)S(1)} %pad_maximum_fusion.9), channel_id=1, source_target_pairs={{0,128},{128,0},{256,384},{384,256},{1,129},{129,1},{257,385},{385... | collective-permute-start | bytes 589832 | tf_op jit(solution)/shard_map/ppermute | solution.py:19
  170.4 1.0 collective-permute-done.2
  171.6 1.9 %collective-permute-start.3 = (f32[2,3,2,8,512]{4,3,2,1,0:T(8,128)S(1)}, f32[2,3,2,8,512]{4,3,2,1,0:T(8,128)S(1)}, u32[]{:S(2)}, u32[]{:S(2)}) collective-permute-start(f32[2,3,2,8,512]{4,3,2,1,0:T(8,128)S(1)} %maximum_select_fusion.1), channel_id=1, source_target_pairs={{0,256},{128,384},{256,0},{384,128},{1,257},{129,385},{257,1},{385... | collective-permute-start | bytes 589832 | tf_op jit(solution)/shard_map/ppermute | solution.py:19
  173.5 6.1 %collective-permute-done.3 = f32[2,3,2,8,512]{4,3,2,1,0:T(8,128)S(1)} collective-permute-done((f32[2,3,2,8,512]{4,3,2,1,0:T(8,128)S(1)}, f32[2,3,2,8,512]{4,3,2,1,0:T(8,128)S(1)}, u32[]{:S(2)}, u32[]{:S(2)}) %collective-permute-start.3) | collective-permute-done | bytes 196640 | tf_op jit(solution)/shard_map/ppermute | solution.py:19
  179.6 0.7 add_select_fusion.3
  (54 shorter events, 1.1 us)
Async XLA Ops:
  0.0 83.6 %collective-permute-start = (f32[2,3,2,8,512]{4,3,2,1,0:T(8,128)}, f32[2,3,2,8,512]{4,3,2,1,0:T(8,128)S(1)}, u32[]{:S(2)}, u32[]{:S(2)}) collective-permute-start(f32[2,3,2,8,512]{4,3,2,1,0:T(8,128)} %param.3), channel_id=1, source_target_pairs={{0,256},{128,384},{256,0},{384,128},{1,257},{129,385},{257,1},{385... | collective-permute-start | bytes 589832 | tf_op jit(solution)/shard_map/ppermute | solution.py:19
  4.0 0.7 copy-start.2
  5.9 1.3 copy-start.1
  83.4 0.9 copy-start
  84.4 7.8 %collective-permute-start.1 = (f32[2,3,2,8,512]{4,3,2,1,0:T(8,128)S(1)}, f32[2,3,2,8,512]{4,3,2,1,0:T(8,128)S(1)}, u32[]{:S(2)}, u32[]{:S(2)}) collective-permute-start(f32[2,3,2,8,512]{4,3,2,1,0:T(8,128)S(1)} %maximum_select_fusion), channel_id=1, source_target_pairs={{0,128},{128,0},{256,384},{384,256},{1,129},{129,1},{257,385},{385... | collective-permute-start | bytes 589832 | tf_op jit(solution)/shard_map/ppermute | solution.py:19
  94.3 38.6 %all-to-all-start = ((f32[128,1,384]{2,1,0:T(1,128)}), f32[128,1,384]{2,1,0:T(1,128)S(1)}, u32[]{:S(2)}, u32[]{:S(2)}) async-start(f32[128,1,384]{2,1,0:T(1,128)} %copy.40), calls=%async_computation | async-start | bytes 393216 | tf_op jit(solution)/shard_map/all_to_all | solution.py:236
  164.4 7.1 %collective-permute-start.2 = (f32[2,3,2,8,512]{4,3,2,1,0:T(8,128)S(1)}, f32[2,3,2,8,512]{4,3,2,1,0:T(8,128)S(1)}, u32[]{:S(2)}, u32[]{:S(2)}) collective-permute-start(f32[2,3,2,8,512]{4,3,2,1,0:T(8,128)S(1)} %pad_maximum_fusion.9), channel_id=1, source_target_pairs={{0,128},{128,0},{256,384},{384,256},{1,129},{129,1},{257,385},{385... | collective-permute-start | bytes 589832 | tf_op jit(solution)/shard_map/ppermute | solution.py:19
  171.6 8.0 %collective-permute-start.3 = (f32[2,3,2,8,512]{4,3,2,1,0:T(8,128)S(1)}, f32[2,3,2,8,512]{4,3,2,1,0:T(8,128)S(1)}, u32[]{:S(2)}, u32[]{:S(2)}) collective-permute-start(f32[2,3,2,8,512]{4,3,2,1,0:T(8,128)S(1)} %maximum_select_fusion.1), channel_id=1, source_target_pairs={{0,256},{128,384},{256,0},{384,128},{1,257},{129,385},{257,1},{385... | collective-permute-start | bytes 589832 | tf_op jit(solution)/shard_map/ppermute | solution.py:19

commit v3 on v2

--- a/solution.py
+++ b/solution.py
@@ -44,8 +44,11 @@
             for first in range(3)
             for second in range(3)
         )
-    ).reshape(3, 3, 1, 1)
-    stress_b = stress.reshape(3, 6, 1, 1)
+    )
+    width = kx_wave.shape[-1]
+    constants = jnp.broadcast_to(moduli[:, None], (3, width))
+    stress_b = jnp.broadcast_to(stress[:, :, None], (3, 6, width))
+    energy = jnp.broadcast_to(energy[:, :, None], (3, 3, width))
     constants, stress_b, energy = lax.optimization_barrier((constants, stress_b, energy))
     stiff_a = constants[0]
     stiff_b = constants[1]
@@ -246,7 +249,6 @@
     ky_wave = signed_wave(ky_index, NY)
     kz_wave = signed_wave(kz_index, NZ)
     kernel = kernel_rows(kx_wave, ky_wave, kz_wave, eigenstrain, moduli)
-    kernel = lax.optimization_barrier(jnp.stack([jnp.stack(row) for row in kernel]))
     scale = 1.0 / (NY * NZ)
     spec = spectrum.reshape(128, 2, 3, 64)
     forced = jnp.stack(

time: 182 us -> 111 us (0.61)
  other arithmetic: 76.5 us -> 10.3 us
  between operations: 4.87 us -> 2.41 us
    select_n x9 -> x0, other arithmetic: 70.1 us -> none  [kernel_rows(): kernel_row.append(jnp.where(inside, energy[source, target] - coupling, 0.0))]
    mul x2 -> x6, other arithmetic: 0.07 us -> 2.34 us  [shards(): sum((kernel[source][target] * spec[:, part, target] for target in range(3)))]
    slice x3 -> x0, local copies, waits for them, and re-layouts: 2.06 us -> none  [the longest x1 0.72 us: kernel_rows(): stress_b[variant, voigt[first][second]] * normal[second]]
  transfers between devices with their start and end apart: 5 -> 5, of which waited for: 4 -> 4; matrix products, arithmetic and copies ran while one was open for 42% -> 7% of each run, Pallas kernels for 0% -> 0%
where the time goes in v3:
time: 111 us; the launch traced here: 110 us
  starting transfers between devices  36.9 us (33%)
  waiting for transfers between devices  27 us (24%)
  blocking collectives  25.8 us (23%)
  other arithmetic  10.3 us (9%)
  matrix products  4.05 us (4%)
  local copies, waits for them, and re-layouts  3.93 us (4%)
  between operations  2.41 us (2%)
    all_to_all x1, blocking collectives, shards(): lax.all_to_all(back, 'gz', split_axis=0, concat_axis=0, tiled=True)  25.8 us
    all_to_all x1, waiting for transfers between devices, shards(): lax.all_to_all(slabs, 'gz', split_axis=0, concat_axis=0, tiled=True)  18.8 us
    ppermute x4, starting transfers between devices, partner_2(): return lax.ppermute(value, axis, pairs)  18.8 us
    all_to_all x1, starting transfers between devices, shards(): lax.all_to_all(slabs, 'gz', split_axis=0, concat_axis=0, tiled=True)  18.1 us
    ppermute x4, waiting for transfers between devices, partner_2(): return lax.ppermute(value, axis, pairs)  8.17 us
    mul x6, other arithmetic, shards(): sum((kernel[source][target] * spec[:, part, target] for target in range(3)))  2.34 us
  transfers between devices with their start and end apart: 5, of which 4 were waited for; matrix products, arithmetic and copies ran while one was open for 7% of the time, Pallas kernels for 0%

profile of v3, /device:TPU:1, one launch (start us, length us, event | category | flops | bytes accessed | tf_op | source)
XLA Modules:
  0.0 110.3 jit_solution(11749929373239891918)
XLA Ops:
  0.0 4.1 %collective-permute-start = (f32[2,3,2,8,512]{4,3,2,1,0:T(8,128)}, f32[2,3,2,8,512]{4,3,2,1,0:T(8,128)S(1)}, u32[]{:S(2)}, u32[]{:S(2)}) collective-permute-start(f32[2,3,2,8,512]{4,3,2,1,0:T(8,128)} %param.3), channel_id=1, source_target_pairs={{0,256},{128,384},{256,0},{384,128},{1,257},{129,385},{257,1},{385... | collective-permute-start | bytes 589832 | tf_op jit(solution)/shard_map/ppermute | solution.py:19
  4.1 0.1 fusion.70
  4.1 0.1 fusion.74
  4.2 0.1 fusion.85
  4.4 1.4 %fusion.100 = (f32[1]{0:T(128)}, f32[1]{0:T(128)}, f32[1]{0:T(128)}) fusion(f32[3]{0:T(128)} %param.5), kind=kLoop, calls=%fused_computation.346 | loop fusion | bytes 24 | tf_op jit(solution)/shard_map/slice | solution.py:35
  7.2 1.8 %slice_reduce_fusion.11 = (f32[3]{0:T(128)S(1)}, f32[3]{0:T(128)S(1)}, f32[3]{0:T(128)S(1)}, f32[3]{0:T(128)S(1)}, f32[3]{0:T(128)S(1)}, /*index=5*/f32[3]{0:T(128)S(1)}, f32[3]{0:T(128)S(1)}) fusion(f32[3,6]{1,0:T(4,128)} %param.4, f32[]{:T(128)} %bitcast), kind=kLoop, calls=%fused_computation.270 | loop fusion | flops 9 | bytes 160 | tf_op jit(solution)/shard_map/slice | solution.py:32
  9.6 0.8 multiply_add_fusion.37
  10.4 0.3 slice_reduce_fusion.7
  10.7 0.1 pad_maximum_fusion.15
  10.8 0.1 fusion.64
  10.9 0.1 broadcast_in_dim.27
  10.9 0.1 broadcast_in_dim.26
  11.0 0.7 broadcast_in_dim.25
  11.7 0.3 fusion.59
  12.1 6.8 %collective-permute-start.1 = (f32[2,3,2,8,512]{4,3,2,1,0:T(8,128)S(1)}, f32[2,3,2,8,512]{4,3,2,1,0:T(8,128)S(1)}, u32[]{:S(2)}, u32[]{:S(2)}) collective-permute-start(f32[2,3,2,8,512]{4,3,2,1,0:T(8,128)S(1)} %maximum_select_fusion), channel_id=1, source_target_pairs={{0,128},{128,0},{256,384},{384,256},{1,129},{129,1},{257,385},{385... | collective-permute-start | bytes 589832 | tf_op jit(solution)/shard_map/ppermute | solution.py:19
  18.9 1.0 collective-permute-done.1
  20.2 0.1 copy.27
  20.3 0.5 fusion.38
  20.8 0.1 slice_add_fusion.2
  21.0 0.1 maximum_bitcast_fusion
  21.1 0.9 copy.28
  21.9 18.1 %all-to-all-start = ((f32[128,1,384]{2,1,0:T(1,128)}), f32[128,1,384]{2,1,0:T(1,128)S(1)}, u32[]{:S(2)}, u32[]{:S(2)}) async-start(f32[128,1,384]{2,1,0:T(1,128)} %copy.28), calls=%async_computation | async-start | bytes 393216 | tf_op jit(solution)/shard_map/all_to_all | solution.py:239
  40.1 1.6 %fusion.62 = (f32[192,192]{1,0:T(8,128)S(1)}, f32[192,192]{1,0:T(8,128)S(1)}, f32[192,192]{1,0:T(8,128)S(1)}) fusion(s32[192]{0:T(256)S(1)} %get-tuple-element.127, s32[192]{0:T(256)S(1)} %get-tuple-element.128, pred[192]{0:T(512)(128)(4,1)S(1)} %fusion.69, s32[192]{0:T(256)S(1)} %get-tuple-element.129, s32[192]{0:T(256)S(1)} %get-tuple-element.133, ...), kind=kLoop, calls=%fused_computation.235 | loop fusion | flops 1769472 | bytes 447552 | tf_op jit(solution)/shard_map/neg | solution.py:130
  41.7 18.8 %all-to-all-done = f32[128,1,384]{2,1,0:T(1,128)S(1)} async-done(((f32[128,1,384]{2,1,0:T(1,128)}), f32[128,1,384]{2,1,0:T(1,128)S(1)}, u32[]{:S(2)}, u32[]{:S(2)}) %all-to-all-start) | async-done | bytes 196640 | tf_op jit(solution)/shard_map/all_to_all | solution.py:239
  60.5 0.5 fusion.26
  61.0 0.6 multiply_subtract_fusion.1
  61.6 1.3 %fusion.1 = f32[128,384]{0,1:T(8,128)S(1)} fusion(f32[192,192]{1,0:T(8,128)S(1)} %get-tuple-element.109, f32[192,192]{1,0:T(8,128)S(1)} %get-tuple-element.108, f32[192,192]{1,0:T(8,128)S(1)} %get-tuple-element.107, f32[128,192]{1,0:T(8,128)S(1)} %get-tuple-element.46, f32[128,192]{1,0:T(8,128)S(1)} %get-tuple-element.45), kind=kOutput, calls=%fused_computation.5 | convolution fusion | flops 226983936 | bytes 835584 | tf_op jit(solution)/shard_map/dot_general | solution.py:242
  62.9 0.4 add_multiply_fusion.5
  63.3 0.4 add_multiply_fusion.2
  63.7 0.4 add_multiply_fusion.4
  64.1 0.4 add_multiply_fusion.1
  64.5 0.4 add_multiply_fusion.3
  64.9 0.4 add_multiply_fusion
  65.3 0.8 fusion.4
  66.1 0.6 multiply_subtract_fusion
  66.7 0.5 fusion.19
  67.2 0.1 slice_subtract_fusion
  67.4 0.1 maximum_bitcast_fusion.1
  67.5 0.2 copy.30
  67.7 25.8 %all_to_all.24 = f32[128,1,384]{2,1,0:T(1,128)S(1)} all-to-all(f32[128,1,384]{2,1,0:T(1,128)S(1)} %copy.30), channel_id=1, replica_groups=mesh['gy'=4,'gz'=128] {'gz'}, dimensions={0} | all-to-all | bytes 393216 | tf_op jit(solution)/shard_map/all_to_all | solution.py:271
  93.5 0.5 fusion.23
  94.0 0.1 fusion.98
  94.1 0.1 fusion.99
  94.4 6.0 %collective-permute-start.2 = (f32[2,3,2,8,512]{4,3,2,1,0:T(8,128)S(1)}, f32[2,3,2,8,512]{4,3,2,1,0:T(8,128)S(1)}, u32[]{:S(2)}, u32[]{:S(2)}) collective-permute-start(f32[2,3,2,8,512]{4,3,2,1,0:T(8,128)S(1)} %pad_maximum_fusion.8), channel_id=1, source_target_pairs={{0,128},{128,0},{256,384},{384,256},{1,129},{129,1},{257,385},{385... | collective-permute-start | bytes 589832 | tf_op jit(solution)/shard_map/ppermute | solution.py:19
  100.4 1.0 collective-permute-done.2
  101.6 1.9 %collective-permute-start.3 = (f32[2,3,2,8,512]{4,3,2,1,0:T(8,128)S(1)}, f32[2,3,2,8,512]{4,3,2,1,0:T(8,128)S(1)}, u32[]{:S(2)}, u32[]{:S(2)}) collective-permute-start(f32[2,3,2,8,512]{4,3,2,1,0:T(8,128)S(1)} %maximum_select_fusion.1), channel_id=1, source_target_pairs={{0,256},{128,384},{256,0},{384,128},{1,257},{129,385},{257,1},{385... | collective-permute-start | bytes 589832 | tf_op jit(solution)/shard_map/ppermute | solution.py:19
  103.5 6.1 %collective-permute-done.3 = f32[2,3,2,8,512]{4,3,2,1,0:T(8,128)S(1)} collective-permute-done((f32[2,3,2,8,512]{4,3,2,1,0:T(8,128)S(1)}, f32[2,3,2,8,512]{4,3,2,1,0:T(8,128)S(1)}, u32[]{:S(2)}, u32[]{:S(2)}) %collective-permute-start.3) | collective-permute-done | bytes 196640 | tf_op jit(solution)/shard_map/ppermute | solution.py:19
  109.6 0.7 add_select_fusion.3
  (44 shorter events, 0.7 us)
Async XLA Ops:
  0.0 12.0 %copy-start = (f32[2,3,2,8,512]{4,3,2,1,0:T(8,128)S(1)}, f32[2,3,2,8,512]{4,3,2,1,0:T(8,128)}, u32[]{:S(2)}) copy-start(f32[2,3,2,8,512]{4,3,2,1,0:T(8,128)} %param.3) | copy-start | bytes 589828
  0.0 12.0 %collective-permute-start = (f32[2,3,2,8,512]{4,3,2,1,0:T(8,128)}, f32[2,3,2,8,512]{4,3,2,1,0:T(8,128)S(1)}, u32[]{:S(2)}, u32[]{:S(2)}) collective-permute-start(f32[2,3,2,8,512]{4,3,2,1,0:T(8,128)} %param.3), channel_id=1, source_target_pairs={{0,256},{128,384},{256,0},{384,128},{1,257},{129,385},{257,1},{385... | collective-permute-start | bytes 589832 | tf_op jit(solution)/shard_map/ppermute | solution.py:19
  12.1 7.8 %collective-permute-start.1 = (f32[2,3,2,8,512]{4,3,2,1,0:T(8,128)S(1)}, f32[2,3,2,8,512]{4,3,2,1,0:T(8,128)S(1)}, u32[]{:S(2)}, u32[]{:S(2)}) collective-permute-start(f32[2,3,2,8,512]{4,3,2,1,0:T(8,128)S(1)} %maximum_select_fusion), channel_id=1, source_target_pairs={{0,128},{128,0},{256,384},{384,256},{1,129},{129,1},{257,385},{385... | collective-permute-start | bytes 589832 | tf_op jit(solution)/shard_map/ppermute | solution.py:19
  21.9 38.6 %all-to-all-start = ((f32[128,1,384]{2,1,0:T(1,128)}), f32[128,1,384]{2,1,0:T(1,128)S(1)}, u32[]{:S(2)}, u32[]{:S(2)}) async-start(f32[128,1,384]{2,1,0:T(1,128)} %copy.28), calls=%async_computation | async-start | bytes 393216 | tf_op jit(solution)/shard_map/all_to_all | solution.py:239
  94.4 7.1 %collective-permute-start.2 = (f32[2,3,2,8,512]{4,3,2,1,0:T(8,128)S(1)}, f32[2,3,2,8,512]{4,3,2,1,0:T(8,128)S(1)}, u32[]{:S(2)}, u32[]{:S(2)}) collective-permute-start(f32[2,3,2,8,512]{4,3,2,1,0:T(8,128)S(1)} %pad_maximum_fusion.8), channel_id=1, source_target_pairs={{0,128},{128,0},{256,384},{384,256},{1,129},{129,1},{257,385},{385... | collective-permute-start | bytes 589832 | tf_op jit(solution)/shard_map/ppermute | solution.py:19
  101.6 8.0 %collective-permute-start.3 = (f32[2,3,2,8,512]{4,3,2,1,0:T(8,128)S(1)}, f32[2,3,2,8,512]{4,3,2,1,0:T(8,128)S(1)}, u32[]{:S(2)}, u32[]{:S(2)}) collective-permute-start(f32[2,3,2,8,512]{4,3,2,1,0:T(8,128)S(1)} %maximum_select_fusion.1), channel_id=1, source_target_pairs={{0,256},{128,384},{256,0},{384,128},{1,257},{129,385},{257,1},{385... | collective-permute-start | bytes 589832 | tf_op jit(solution)/shard_map/ppermute | solution.py:19

commit v4 on v3

--- a/solution.py
+++ b/solution.py
@@ -1,4 +1,6 @@
 import math
+
+import numpy as np
 
 import jax
 import jax.numpy as jnp
@@ -108,28 +110,38 @@
     return (jnp.cos(angle), jnp.sin(angle))
 
 
-def stacked_table(length, axis):
-    rows_idx = lax.broadcasted_iota(jnp.int32, (length, length), 0)
-    cols_idx = lax.broadcasted_iota(jnp.int32, (length, length), 1)
-    cosine, sine = cos_sin(rows_idx * cols_idx, length)
-    return jnp.concatenate([cosine, sine], axis=axis)
-
-
-def block_dft8(inverse):
+def np_cos_sin(numer, length):
+    angle = (2.0 * np.pi / length) * (numer % length).astype(np.float64)
+    return (np.cos(angle).astype(np.float32), np.sin(angle).astype(np.float32))
+
+
+def stacked_table(length):
+    index = np.arange(length)
+    cosine, sine = np_cos_sin(np.outer(index, index), length)
+    return np.concatenate([cosine, sine], axis=0)
+
+
+def block_dft8():
     size = 192
-    rows_idx = lax.broadcasted_iota(jnp.int32, (size, size), 0)
-    cols_idx = lax.broadcasted_iota(jnp.int32, (size, size), 1)
+    rows_idx = np.arange(size)[:, None]
+    cols_idx = np.arange(size)[None, :]
     same = (rows_idx // 32 == cols_idx // 32) & (rows_idx % 4 == cols_idx % 4)
-    cosine, sine = cos_sin(((rows_idx // 4) % 8) * ((cols_idx // 4) % 8), 8)
-    cosine = jnp.where(same, cosine, 0.0)
-    sine = jnp.where(same, sine, 0.0)
-    if inverse:
-        top = jnp.concatenate([cosine, sine], axis=1)
-        bottom = jnp.concatenate([-sine, cosine], axis=1)
-    else:
-        top = jnp.concatenate([cosine, -sine], axis=1)
-        bottom = jnp.concatenate([sine, cosine], axis=1)
-    return jnp.concatenate([top, bottom], axis=0)
+    cosine, sine = np_cos_sin(((rows_idx // 4) % 8) * ((cols_idx // 4) % 8), 8)
+    cosine = np.where(same, cosine, 0.0).astype(np.float32)
+    sine = np.where(same, sine, 0.0).astype(np.float32)
+    top = np.concatenate([cosine, -sine], axis=1)
+    bottom = np.concatenate([sine, cosine], axis=1)
+    return np.concatenate([top, bottom], axis=0)
+
+
+def z_twiddle_table():
+    rows_idx = np.arange(128)[:, None]
+    cols_idx = np.arange(192)[None, :]
+    return np.stack(np_cos_sin(rows_idx * ((cols_idx // 4) % 8), 1024))
+
+
+def y_twiddle_table():
+    return np.stack(np_cos_sin(np.arange(4)[:, None] * np.arange(128)[None, :], 512))
 
 
 def matmul(spec, left, right):
@@ -176,30 +188,30 @@
 def y_forward(spectral):
     parts = [(spectral[0, ..., 128 * a:128 * a + 128], spectral[1, ..., 128 * a:128 * a + 128]) for a in range(4)]
     mixed = dft4(parts, -1)
-    lanes = lax.broadcasted_iota(jnp.int32, (128,), 0)
+    table = y_twiddle_table()
     out = []
     for k1 in range(4):
-        tw_cos, tw_sin = cos_sin(lanes * k1, 512)
+        tw_cos, tw_sin = table[0, k1], table[1, k1]
         re, im = mixed[k1]
         out.append(jnp.stack([re * tw_cos + im * tw_sin, im * tw_cos - re * tw_sin]))
     stacked = jnp.stack(out, axis=-2).reshape(384, 128)
-    product = matmul("kb,rb->kr", stacked_table(128, 0), stacked)
+    product = matmul("kb,rb->kr", stacked_table(128), stacked)
     re, im = combine_rows(product, -1)
     return jnp.concatenate([re, im], axis=1)
 
 
 def y_inverse(returned):
-    product = matmul("kr,kb->rb", returned, stacked_table(128, 1))
+    product = matmul("kr,bk->rb", returned, stacked_table(128))
     c_re = product[:192, :128]
     s_re = product[:192, 128:]
     c_im = product[192:, :128]
     s_im = product[192:, 128:]
     re = (c_re - s_im).reshape(3, 2, 8, 4, 128)
     im = (c_im + s_re).reshape(3, 2, 8, 4, 128)
-    lanes = lax.broadcasted_iota(jnp.int32, (128,), 0)
+    table = y_twiddle_table()
     parts = []
     for k1 in range(4):
-        tw_cos, tw_sin = cos_sin(lanes * k1, 512)
+        tw_cos, tw_sin = table[0, k1], table[1, k1]
         r = re[..., k1, :]
         i = im[..., k1, :]
         parts.append((r * tw_cos - i * tw_sin, i * tw_cos + r * tw_sin))
@@ -210,10 +222,9 @@
 
 
 def z_twiddle(re, im, sign):
-    rows_idx = lax.broadcasted_iota(jnp.int32, (128, 192), 0)
-    cols_idx = lax.broadcasted_iota(jnp.int32, (128, 192), 1)
-    tw_cos, tw_sin = cos_sin(rows_idx * ((cols_idx // 4) % 8), 1024)
-    tw_sin = sign * tw_sin
+    table = z_twiddle_table()
+    tw_cos = table[0]
+    tw_sin = sign * table[1]
     return jnp.concatenate([re * tw_cos - im * tw_sin, im * tw_cos + re * tw_sin], axis=1)
 
 
@@ -237,9 +248,9 @@
     spectral = twiddle(spectral, phase_cos, -phase_sin)
     slabs = y_forward(spectral)
     pencils = lax.all_to_all(slabs, "gz", split_axis=0, concat_axis=0, tiled=True)
-    table = stacked_table(128, 0)
+    table = stacked_table(128)
     re, im = combine_rows(matmul("kg,gc->kc", table, pencils), -1)
-    spectrum = jnp.dot(z_twiddle(re, im, -1), block_dft8(False), precision=highest)
+    spectrum = jnp.dot(z_twiddle(re, im, -1), block_dft8(), precision=highest)
     rows_idx = lax.broadcasted_iota(jnp.int32, (128, 64), 0)
     cols_idx = lax.broadcasted_iota(jnp.int32, (128, 64), 1)
     plane = cols_idx // 32
@@ -264,7 +275,7 @@
         ],
         axis=1,
     ).reshape(128, 384)
-    back = jnp.dot(forced, block_dft8(True), precision=highest)
+    back = matmul("kr,sr->ks", forced, block_dft8())
     back = z_twiddle(back[:, :192], back[:, 192:], 1)
     re, im = combine_rows(matmul("kg,gc->kc", table, back), 1)
     back = jnp.concatenate([re, im], axis=1)

time: 111 us -> 111 us (level)
  other arithmetic: 10.3 us -> 6.4 us
  local copies, waits for them, and re-layouts: 3.93 us -> 6.6 us
  waiting for transfers between devices: 27 us -> 28.4 us
    unnamed x2 -> x30, local copies, waits for them, and re-layouts: 0.01 us -> 3.99 us
    all_to_all x1, waiting for transfers between devices: 18.8 us -> 20.5 us  [shards(): lax.all_to_all(slabs, 'gz', split_axis=0, concat_axis=0, tiled=True)]
    neg x1 -> x0, other arithmetic: 1.6 us -> none  [block_dft8(): top = jnp.concatenate([cosine, -sine], axis=1)]
    dot_general x2, matrix products: 2.06 us -> 0.88 us  [shards(): spectrum = jnp.dot(z_twiddle(re, im, -1), block_dft8(), precision=highest)]
    ppermute x4, starting transfers between devices: 18.8 us -> 19.9 us  [partner_2(): return lax.ppermute(value, axis, pairs)]
    dot_general x4 -> x5, matrix products: 1.99 us -> 2.82 us  [matmul(): return jnp.einsum(spec, left, right, precision=highest)]
  transfers between devices with their start and end apart: 5 -> 5, of which waited for: 4 -> 4; matrix products, arithmetic and copies ran while one was open for 7% -> 2% of each run, Pallas kernels for 0% -> 0%
where the time goes in v4:
time: 111 us
  starting transfers between devices  37.6 us (34%)
  waiting for transfers between devices  28.4 us (26%)
  blocking collectives  25.7 us (23%)
  local copies, waits for them, and re-layouts  6.6 us (6%)
  other arithmetic  6.4 us (6%)
  matrix products  3.7 us (3%)
  between operations  2.46 us (2%)
    all_to_all x1, blocking collectives, shards(): lax.all_to_all(back, 'gz', split_axis=0, concat_axis=0, tiled=True)  25.7 us
    all_to_all x1, waiting for transfers between devices, shards(): lax.all_to_all(slabs, 'gz', split_axis=0, concat_axis=0, tiled=True)  20.5 us
    ppermute x4, starting transfers between devices, partner_2(): return lax.ppermute(value, axis, pairs)  19.9 us
    all_to_all x1, starting transfers between devices, shards(): lax.all_to_all(slabs, 'gz', split_axis=0, concat_axis=0, tiled=True)  17.7 us
    ppermute x4, waiting for transfers between devices, partner_2(): return lax.ppermute(value, axis, pairs)  7.82 us
    unnamed x30, local copies, waits for them, and re-layouts  3.99 us
    dot_general x5, matrix products, matmul(): return jnp.einsum(spec, left, right, precision=highest)  2.82 us
    mul x6, other arithmetic, shards(): sum((kernel[source][target] * spec[:, part, target] for target in range(3)))  2.33 us
  transfers between devices with their start and end apart: 5, of which 4 were waited for; matrix products, arithmetic and copies ran while one was open for 2% of the time, Pallas kernels for 0%

profile of v4, /device:TPU:1, one launch (start us, length us, event | category | flops | bytes accessed | tf_op | source)
XLA Modules:
  0.0 110.9 jit_solution(2561614410719452170)
XLA Ops:
  0.0 3.9 %collective-permute-start = (f32[2,3,2,8,512]{4,3,2,1,0:T(8,128)}, f32[2,3,2,8,512]{4,3,2,1,0:T(8,128)S(1)}, u32[]{:S(2)}, u32[]{:S(2)}) collective-permute-start(f32[2,3,2,8,512]{4,3,2,1,0:T(8,128)} %param.29), channel_id=1, source_target_pairs={{0,256},{128,384},{256,0},{384,128},{1,257},{129,385},{257,1},{385... | collective-permute-start | bytes 589832 | tf_op jit(solution)/shard_map/ppermute | solution.py:21
  4.0 0.6 copy-done.10
  4.6 0.6 fusion.44
  7.1 0.9 slice_reduce_fusion.11
  8.1 0.1 multiply_add_fusion.36
  8.2 0.1 pad_maximum_fusion.5
  8.2 0.3 slice_reduce_fusion.7
  8.5 0.1 fusion.31
  8.9 1.0 add_select_fusion.3
  9.9 7.7 %collective-permute-start.1 = (f32[2,3,2,8,512]{4,3,2,1,0:T(8,128)S(1)}, f32[2,3,2,8,512]{4,3,2,1,0:T(8,128)S(1)}, u32[]{:S(2)}, u32[]{:S(2)}) collective-permute-start(f32[2,3,2,8,512]{4,3,2,1,0:T(8,128)S(1)} %maximum_select_fusion), channel_id=1, source_target_pairs={{0,128},{128,0},{256,384},{384,256},{1,129},{129,1},{257,385},{385... | collective-permute-start | bytes 589832 | tf_op jit(solution)/shard_map/ppermute | solution.py:21
  17.6 1.0 collective-permute-done.1
  18.7 0.6 copy-done.8
  19.4 0.6 copy-done.11
  20.2 0.6 copy-done.13
  20.9 0.1 copy.53
  21.0 0.8 copy-done
  21.8 0.5 fusion.45
  22.3 0.1 slice_add_fusion.2
  22.4 0.1 maximum_bitcast_fusion
  22.5 0.9 copy.54
  23.4 17.7 %all-to-all-start = ((f32[128,1,384]{2,1,0:T(1,128)}), f32[128,1,384]{2,1,0:T(1,128)S(1)}, u32[]{:S(2)}, u32[]{:S(2)}) async-start(f32[128,1,384]{2,1,0:T(1,128)} %copy.54), calls=%async_computation | async-start | bytes 393216 | tf_op jit(solution)/shard_map/all_to_all | solution.py:250
  41.2 20.5 %all-to-all-done = f32[128,1,384]{2,1,0:T(1,128)S(1)} async-done(((f32[128,1,384]{2,1,0:T(1,128)}), f32[128,1,384]{2,1,0:T(1,128)S(1)}, u32[]{:S(2)}, u32[]{:S(2)}) %all-to-all-start) | async-done | bytes 196640 | tf_op jit(solution)/shard_map/all_to_all | solution.py:250
  61.8 0.5 fusion.7
  62.3 0.4 fusion.13
  62.7 0.5 copy-done.5
  63.2 0.4 convolution_add_fusion
  63.7 0.1 copy.55
  63.8 0.4 add_multiply_fusion
  64.2 0.4 add_multiply_fusion.3
  64.6 0.4 add_multiply_fusion.1
  65.0 0.4 add_multiply_fusion.4
  65.4 0.4 add_multiply_fusion.2
  65.8 0.4 add_multiply_fusion.5
  66.3 0.8 fusion.46
  67.2 0.1 multiply_subtract_fusion
  67.3 0.5 fusion
  67.8 0.1 slice_subtract_fusion
  68.0 0.1 maximum_bitcast_fusion.1
  68.1 0.2 copy.56
  68.3 25.7 %all_to_all.24 = f32[128,1,384]{2,1,0:T(1,128)S(1)} all-to-all(f32[128,1,384]{2,1,0:T(1,128)S(1)} %copy.56), channel_id=1, replica_groups=mesh['gy'=4,'gz'=128] {'gz'}, dimensions={0} | all-to-all | bytes 393216 | tf_op jit(solution)/shard_map/all_to_all | solution.py:282
  94.0 0.5 fusion.4
  94.6 0.1 fusion.43
  94.7 0.1 fusion.42
  94.9 6.1 %collective-permute-start.2 = (f32[2,3,2,8,512]{4,3,2,1,0:T(8,128)S(1)}, f32[2,3,2,8,512]{4,3,2,1,0:T(8,128)S(1)}, u32[]{:S(2)}, u32[]{:S(2)}) collective-permute-start(f32[2,3,2,8,512]{4,3,2,1,0:T(8,128)S(1)} %pad_maximum_fusion.2), channel_id=1, source_target_pairs={{0,128},{128,0},{256,384},{384,256},{1,129},{129,1},{257,385},{385... | collective-permute-start | bytes 589832 | tf_op jit(solution)/shard_map/ppermute | solution.py:21
  101.0 1.0 collective-permute-done.2
  102.2 2.2 %collective-permute-start.3 = (f32[2,3,2,8,512]{4,3,2,1,0:T(8,128)S(1)}, f32[2,3,2,8,512]{4,3,2,1,0:T(8,128)S(1)}, u32[]{:S(2)}, u32[]{:S(2)}) collective-permute-start(f32[2,3,2,8,512]{4,3,2,1,0:T(8,128)S(1)} %maximum_select_fusion.1), channel_id=1, source_target_pairs={{0,256},{128,384},{256,0},{384,128},{1,257},{129,385},{257,1},{385... | collective-permute-start | bytes 589832 | tf_op jit(solution)/shard_map/ppermute | solution.py:21
  104.4 5.8 %collective-permute-done.3 = f32[2,3,2,8,512]{4,3,2,1,0:T(8,128)S(1)} collective-permute-done((f32[2,3,2,8,512]{4,3,2,1,0:T(8,128)S(1)}, f32[2,3,2,8,512]{4,3,2,1,0:T(8,128)S(1)}, u32[]{:S(2)}, u32[]{:S(2)}) %collective-permute-start.3) | collective-permute-done | bytes 196640 | tf_op jit(solution)/shard_map/ppermute | solution.py:21
  110.2 0.7 add_select_fusion
  (63 shorter events, 1.1 us)
Async XLA Ops:
  0.0 8.9 %collective-permute-start = (f32[2,3,2,8,512]{4,3,2,1,0:T(8,128)}, f32[2,3,2,8,512]{4,3,2,1,0:T(8,128)S(1)}, u32[]{:S(2)}, u32[]{:S(2)}) collective-permute-start(f32[2,3,2,8,512]{4,3,2,1,0:T(8,128)} %param.29), channel_id=1, source_target_pairs={{0,256},{128,384},{256,0},{384,128},{1,257},{129,385},{257,1},{385... | collective-permute-start | bytes 589832 | tf_op jit(solution)/shard_map/ppermute | solution.py:21
  4.0 0.7 copy-start.10
  5.8 1.3 %copy-start.6 = (f32[3,6]{1,0:T(4,128)S(1)}, f32[3,6]{1,0:T(4,128)}, u32[]{:S(2)}) copy-start(f32[3,6]{1,0:T(4,128)} %param.30) | copy-start | bytes 220
  9.9 8.7 %collective-permute-start.1 = (f32[2,3,2,8,512]{4,3,2,1,0:T(8,128)S(1)}, f32[2,3,2,8,512]{4,3,2,1,0:T(8,128)S(1)}, u32[]{:S(2)}, u32[]{:S(2)}) collective-permute-start(f32[2,3,2,8,512]{4,3,2,1,0:T(8,128)S(1)} %maximum_select_fusion), channel_id=1, source_target_pairs={{0,128},{128,0},{256,384},{384,256},{1,129},{129,1},{257,385},{385... | collective-permute-start | bytes 589832 | tf_op jit(solution)/shard_map/ppermute | solution.py:21
  18.7 0.7 copy-start.8
  18.7 0.7 copy-start.9
  19.4 0.7 copy-start.11
  19.4 0.7 copy-start.12
  20.1 0.7 copy-start.13
  20.1 0.7 copy-start.14
  20.9 0.9 copy-start
  23.4 38.4 %all-to-all-start = ((f32[128,1,384]{2,1,0:T(1,128)}), f32[128,1,384]{2,1,0:T(1,128)S(1)}, u32[]{:S(2)}, u32[]{:S(2)}) async-start(f32[128,1,384]{2,1,0:T(1,128)} %copy.54), calls=%async_computation | async-start | bytes 393216 | tf_op jit(solution)/shard_map/all_to_all | solution.py:250
  41.2 21.0 %copy-start.1 = (f32[128,192]{1,0:T(8,128)S(1)}, f32[128,192]{1,0:T(8,128)}, u32[]{:S(2)}) copy-start(f32[128,192]{1,0:T(8,128)} %constant.154.clone) | copy-start | bytes 294916
  41.2 21.0 %copy-start.3 = (f32[128,192]{1,0:T(8,128)S(1)}, f32[128,192]{1,0:T(8,128)}, u32[]{:S(2)}) copy-start(f32[128,192]{1,0:T(8,128)} %constant.155.clone) | copy-start | bytes 294916
  41.2 21.0 %copy-start.4 = (f32[192,384]{1,0:T(8,128)S(1)}, f32[192,384]{1,0:T(8,128)}, u32[]{:S(2)}) copy-start(f32[192,384]{1,0:T(8,128)} %constant.159) | copy-start | bytes 884740
  62.3 1.0 copy-start.5
  65.0 1.3 %copy-start.2 = (f32[384,384]{1,0:T(8,128)S(1)}, f32[384,384]{1,0:T(8,128)}, u32[]{:S(2)}) copy-start(f32[384,384]{1,0:T(8,128)} %constant.156.clone) | copy-start | bytes 1769476
  66.3 0.9 copy-start.7
  94.9 7.1 %collective-permute-start.2 = (f32[2,3,2,8,512]{4,3,2,1,0:T(8,128)S(1)}, f32[2,3,2,8,512]{4,3,2,1,0:T(8,128)S(1)}, u32[]{:S(2)}, u32[]{:S(2)}) collective-permute-start(f32[2,3,2,8,512]{4,3,2,1,0:T(8,128)S(1)} %pad_maximum_fusion.2), channel_id=1, source_target_pairs={{0,128},{128,0},{256,384},{384,256},{1,129},{129,1},{257,385},{385... | collective-permute-start | bytes 589832 | tf_op jit(solution)/shard_map/ppermute | solution.py:21
  102.2 8.0 %collective-permute-start.3 = (f32[2,3,2,8,512]{4,3,2,1,0:T(8,128)S(1)}, f32[2,3,2,8,512]{4,3,2,1,0:T(8,128)S(1)}, u32[]{:S(2)}, u32[]{:S(2)}) collective-permute-start(f32[2,3,2,8,512]{4,3,2,1,0:T(8,128)S(1)} %maximum_select_fusion.1), channel_id=1, source_target_pairs={{0,256},{128,384},{256,0},{384,128},{1,257},{129,385},{257,1},{385... | collective-permute-start | bytes 589832 | tf_op jit(solution)/shard_map/ppermute | solution.py:21

commit v5 on v4

--- a/solution.py
+++ b/solution.py
@@ -185,6 +185,21 @@
     return [(ar + cr, ai + ci), (br + dr, bi + di), (ar - cr, ai - ci), (br - dr, bi - di)]
 
 
+def dft4_across(gathered, index, sign):
+    (r0, i0), (r1, i1), (r2, i2), (r3, i3) = [(gathered[g, 0], gathered[g, 1]) for g in range(4)]
+    ar, ai = r0 + r2, i0 + i2
+    br, bi = r0 - r2, i0 - i2
+    cr, ci = r1 + r3, i1 + i3
+    dr, di = times_i(r1 - r3, i1 - i3, sign)
+    choices = [(ar + cr, ai + ci), (br + dr, bi + di), (ar - cr, ai - ci), (br - dr, bi - di)]
+    real_part = choices[3][0]
+    imag_part = choices[3][1]
+    for position in (2, 1, 0):
+        real_part = jnp.where(index == position, choices[position][0], real_part)
+        imag_part = jnp.where(index == position, choices[position][1], imag_part)
+    return jnp.stack([real_part, imag_part])
+
+
 def y_forward(spectral):
     parts = [(spectral[0, ..., 128 * a:128 * a + 128], spectral[1, ..., 128 * a:128 * a + 128]) for a in range(4)]
     mixed = dft4(parts, -1)
@@ -232,16 +247,10 @@
     gy_count = lax.axis_size("gy")
     gy_index = lax.axis_index("gy")
     gz_index = lax.axis_index("gz")
-    low_bit = lax.rem(gy_index, 2)
-    high_bit = lax.div(gy_index, 2)
     y_local = fields.shape[4]
     positions = lax.broadcasted_iota(jnp.int32, (y_local,), 0)
-    partner = partner_2(fields, "gy", 1)
-    halves = jnp.where(high_bit == 1, partner - fields, fields + partner)
-    halves = jnp.where(high_bit * low_bit == 1, rotate_neg(halves), halves)
-    partner = partner_2(halves, "gy", 0)
-    spectral = jnp.where(low_bit == 1, partner - halves, halves + partner)
-    residue = 2 * low_bit + high_bit
+    spectral = dft4_across(lax.all_gather(fields, "gy", axis=0), gy_index, -1)
+    residue = gy_index
     angle = 2.0 * math.pi / NY * (positions * residue % NY).astype(jnp.float32)
     phase_cos = jnp.cos(angle)
     phase_sin = jnp.sin(angle)
@@ -282,11 +291,7 @@
     returned = lax.all_to_all(back, "gz", split_axis=0, concat_axis=0, tiled=True)
     spatial = y_inverse(returned)
     spatial = twiddle(spatial, phase_cos, phase_sin)
-    partner = partner_2(spatial, "gy", 0)
-    halves = jnp.where(low_bit == 1, partner - spatial, spatial + partner)
-    halves = jnp.where(high_bit * low_bit == 1, rotate_pos(halves), halves)
-    partner = partner_2(halves, "gy", 1)
-    result = jnp.where(high_bit == 1, partner - halves, halves + partner)
+    result = dft4_across(lax.all_gather(spatial, "gy", axis=0), gy_index, 1)
     return result
 
 

time: 111 us -> 104 us (0.937)
  starting transfers between devices: 37.6 us -> 24.7 us
  waiting for transfers between devices: 28.4 us -> 35 us
    all_gather x0 -> x2, blocking collectives: none -> 26.1 us  [the longest x1 14.2 us: shards(): spectral = dft4_across(lax.all_gather(fields, 'gy', axis=0), gy_index, -1)]
    all_to_all x1 -> x0, blocking collectives: 25.7 us -> none  [shards(): lax.all_to_all(back, 'gz', split_axis=0, concat_axis=0, tiled=True)]
    ppermute x4 -> x0, starting transfers between devices: 19.9 us -> none  [partner_2(): return lax.ppermute(value, axis, pairs)]
    all_to_all x0 -> x1, waiting for transfers between devices: none -> 18.7 us  [shards(): lax.all_to_all(back, 'gz', split_axis=0, concat_axis=0, tiled=True)]
    ppermute x4 -> x0, waiting for transfers between devices: 7.82 us -> none  [partner_2(): return lax.ppermute(value, axis, pairs)]
    all_to_all x0 -> x1, starting transfers between devices: none -> 6.77 us  [shards(): lax.all_to_all(back, 'gz', split_axis=0, concat_axis=0, tiled=True)]
    all_to_all x1, waiting for transfers between devices: 20.5 us -> 16.3 us  [shards(): lax.all_to_all(slabs, 'gz', split_axis=0, concat_axis=0, tiled=True)]
    select_n x6 -> x1, other arithmetic: 1.85 us -> 0.09 us  [dft4_across(): real_part = jnp.where(index == position, choices[position][0], real_part)]
  transfers between devices with their start and end apart: 5 -> 2, of which waited for: 4 -> 2; matrix products, arithmetic and copies ran while one was open for 2% -> 2% of each run, Pallas kernels for 0% -> 0%
where the time goes in v5:
time: 104 us
  waiting for transfers between devices  35 us (34%)
  blocking collectives  26.1 us (25%)
  starting transfers between devices  24.7 us (24%)
  local copies, waits for them, and re-layouts  6.65 us (6%)
  other arithmetic  5.37 us (5%)
  matrix products  3.69 us (4%)
  between operations  2.47 us (2%)
    all_to_all x1, waiting for transfers between devices, shards(): lax.all_to_all(back, 'gz', split_axis=0, concat_axis=0, tiled=True)  18.7 us
    all_to_all x1, starting transfers between devices, shards(): lax.all_to_all(slabs, 'gz', split_axis=0, concat_axis=0, tiled=True)  18 us
    all_to_all x1, waiting for transfers between devices, shards(): lax.all_to_all(slabs, 'gz', split_axis=0, concat_axis=0, tiled=True)  16.3 us
    all_gather x1, blocking collectives, shards(): spectral = dft4_across(lax.all_gather(fields, 'gy', axis=0), gy_index, -1)  14.2 us
    all_gather x1, blocking collectives, shards(): result = dft4_across(lax.all_gather(spatial, 'gy', axis=0), gy_index, 1)  12 us
    all_to_all x1, starting transfers between devices, shards(): lax.all_to_all(back, 'gz', split_axis=0, concat_axis=0, tiled=True)  6.77 us
    unnamed x30, local copies, waits for them, and re-layouts  3.35 us
    dot_general x5, matrix products, matmul(): return jnp.einsum(spec, left, right, precision=highest)  2.81 us
  transfers between devices with their start and end apart: 2, of which 2 were waited for; matrix products, arithmetic and copies ran while one was open for 2% of the time, Pallas kernels for 0%

profile of v5, /device:TPU:1, one launch (start us, length us, event | category | flops | bytes accessed | tf_op | source)
XLA Modules:
  0.0 104.0 jit_solution(6602280016511352055)
XLA Ops:
  0.1 14.2 %all-gather = f32[8,3,2,8,512]{4,3,2,1,0:T(8,128)S(1)} all-gather(f32[2,3,2,8,512]{4,3,2,1,0:T(8,128)} %param.29), channel_id=2, replica_groups=mesh['gy'=4,'gz'=128] {'gy'}, dimensions={0}, use_global_device_ids=true | all-gather | bytes 983040 | tf_op jit(solution)/shard_map/all_gather | solution.py:252
  14.2 0.1 fusion.17
  14.4 0.6 copy-done.8
  15.1 0.6 copy-done.11
  15.8 0.6 copy-done.13
  16.5 0.1 copy.53
  16.7 0.8 copy-done
  17.4 0.5 fusion.46
  17.9 0.1 slice_add_fusion.2
  18.1 0.1 maximum_bitcast_fusion
  18.2 0.9 copy.54
  19.0 18.0 %all-to-all-start = ((f32[128,1,384]{2,1,0:T(1,128)}), f32[128,1,384]{2,1,0:T(1,128)S(1)}, u32[]{:S(2)}, u32[]{:S(2)}) async-start(f32[128,1,384]{2,1,0:T(1,128)} %copy.54), calls=%async_computation | async-start | bytes 393216 | tf_op jit(solution)/shard_map/all_to_all | solution.py:259
  37.0 0.7 fusion.45
  39.0 0.9 slice_reduce_fusion.11
  40.6 0.1 multiply_add_fusion.35
  40.7 0.3 slice_reduce_fusion.7
  40.9 0.1 pad_maximum_fusion.6
  41.0 0.1 fusion.33
  41.1 0.1 broadcast_in_dim.20
  41.2 0.1 broadcast_in_dim.19
  41.3 0.1 broadcast_in_dim.18
  41.4 16.3 %all-to-all-done = f32[128,1,384]{2,1,0:T(1,128)S(1)} async-done(((f32[128,1,384]{2,1,0:T(1,128)}), f32[128,1,384]{2,1,0:T(1,128)S(1)}, u32[]{:S(2)}, u32[]{:S(2)}) %all-to-all-start) | async-done | bytes 196640 | tf_op jit(solution)/shard_map/all_to_all | solution.py:259
  57.7 0.5 fusion.7
  58.2 0.4 fusion.13
  58.7 0.5 copy-done.5
  59.2 0.4 convolution_add_fusion
  59.6 0.1 copy.55
  59.8 0.4 add_multiply_fusion.5
  60.2 0.4 add_multiply_fusion.2
  60.5 0.4 add_multiply_fusion.4
  61.0 0.4 add_multiply_fusion.1
  61.3 0.4 add_multiply_fusion.3
  61.7 0.4 add_multiply_fusion
  62.2 0.8 fusion.47
  63.0 0.1 copy-done.7
  63.1 0.1 multiply_subtract_fusion
  63.2 0.5 fusion
  63.8 0.1 slice_subtract_fusion
  63.9 0.1 maximum_bitcast_fusion.1
  64.0 0.9 copy.56
  64.9 6.8 %all-to-all-start.1 = ((f32[128,1,384]{2,1,0:T(1,128)}), f32[128,1,384]{2,1,0:T(1,128)S(1)}, u32[]{:S(2)}, u32[]{:S(2)}) async-start(f32[128,1,384]{2,1,0:T(1,128)} %copy.56), calls=%async_computation.1 | async-start | bytes 393216 | tf_op jit(solution)/shard_map/all_to_all | solution.py:291
  71.7 18.7 %all-to-all-done.1 = f32[128,1,384]{2,1,0:T(1,128)S(1)} async-done(((f32[128,1,384]{2,1,0:T(1,128)}), f32[128,1,384]{2,1,0:T(1,128)S(1)}, u32[]{:S(2)}, u32[]{:S(2)}) %all-to-all-start.1) | async-done | bytes 196640 | tf_op jit(solution)/shard_map/all_to_all | solution.py:291
  90.4 0.5 fusion.4
  90.9 0.1 fusion.43
  91.0 0.1 fusion.44
  91.3 12.0 %all-gather.1 = f32[8,3,2,8,512]{4,3,2,1,0:T(8,128)S(1)} all-gather(f32[2,3,2,8,512]{4,3,2,1,0:T(8,128)S(1)} %pad_maximum_fusion.2), channel_id=3, replica_groups=mesh['gy'=4,'gz'=128] {'gy'}, dimensions={0}, use_global_device_ids=true | all-gather | bytes 983040 | tf_op jit(solution)/shard_map/all_gather | solution.py:294
  103.2 0.1 select_bitcast_fusion
  103.3 0.7 pad_maximum_fusion.3
  (53 shorter events, 0.6 us)
Async XLA Ops:
  14.3 0.7 copy-start.8
  14.4 0.7 copy-start.9
  15.1 0.7 copy-start.11
  15.1 0.7 copy-start.12
  15.8 0.7 copy-start.13
  15.8 0.7 copy-start.14
  16.5 0.9 copy-start
  19.0 18.0 %copy-start.10 = (f32[3]{0:T(128)S(1)}, f32[3]{0:T(128)}, u32[]{:S(2)}) copy-start(f32[3]{0:T(128)} %param.31) | copy-start | bytes 40
  19.0 38.7 %all-to-all-start = ((f32[128,1,384]{2,1,0:T(1,128)}), f32[128,1,384]{2,1,0:T(1,128)S(1)}, u32[]{:S(2)}, u32[]{:S(2)}) async-start(f32[128,1,384]{2,1,0:T(1,128)} %copy.54), calls=%async_computation | async-start | bytes 393216 | tf_op jit(solution)/shard_map/all_to_all | solution.py:259
  37.7 1.3 %copy-start.6 = (f32[3,6]{1,0:T(4,128)S(1)}, f32[3,6]{1,0:T(4,128)}, u32[]{:S(2)}) copy-start(f32[3,6]{1,0:T(4,128)} %param.30) | copy-start | bytes 220
  41.4 16.8 %copy-start.1 = (f32[128,192]{1,0:T(8,128)S(1)}, f32[128,192]{1,0:T(8,128)}, u32[]{:S(2)}) copy-start(f32[128,192]{1,0:T(8,128)} %constant.152.clone) | copy-start | bytes 294916
  41.4 16.8 %copy-start.3 = (f32[128,192]{1,0:T(8,128)S(1)}, f32[128,192]{1,0:T(8,128)}, u32[]{:S(2)}) copy-start(f32[128,192]{1,0:T(8,128)} %constant.153.clone) | copy-start | bytes 294916
  41.4 16.8 %copy-start.4 = (f32[192,384]{1,0:T(8,128)S(1)}, f32[192,384]{1,0:T(8,128)}, u32[]{:S(2)}) copy-start(f32[192,384]{1,0:T(8,128)} %constant.157) | copy-start | bytes 884740
  58.2 1.0 copy-start.5
  60.9 1.3 %copy-start.2 = (f32[384,384]{1,0:T(8,128)S(1)}, f32[384,384]{1,0:T(8,128)}, u32[]{:S(2)}) copy-start(f32[384,384]{1,0:T(8,128)} %constant.154.clone) | copy-start | bytes 1769476
  62.2 0.9 copy-start.7
  64.9 25.5 %all-to-all-start.1 = ((f32[128,1,384]{2,1,0:T(1,128)}), f32[128,1,384]{2,1,0:T(1,128)S(1)}, u32[]{:S(2)}, u32[]{:S(2)}) async-start(f32[128,1,384]{2,1,0:T(1,128)} %copy.56), calls=%async_computation.1 | async-start | bytes 393216 | tf_op jit(solution)/shard_map/all_to_all | solution.py:291

commit v6 on v5

--- a/solution.py
+++ b/solution.py
@@ -12,7 +12,7 @@
 NZ = 1024
 
 
-highest = lax.Precision.HIGHEST
+highest = lax.Precision.HIGH
 
 
 def partner_2(value, axis, stride):
@@ -123,21 +123,21 @@
 
 def block_dft8():
     size = 192
-    rows_idx = np.arange(size)[:, None]
-    cols_idx = np.arange(size)[None, :]
+    rows_idx = lax.broadcasted_iota(jnp.int32, (size, size), 0)
+    cols_idx = lax.broadcasted_iota(jnp.int32, (size, size), 1)
     same = (rows_idx // 32 == cols_idx // 32) & (rows_idx % 4 == cols_idx % 4)
-    cosine, sine = np_cos_sin(((rows_idx // 4) % 8) * ((cols_idx // 4) % 8), 8)
-    cosine = np.where(same, cosine, 0.0).astype(np.float32)
-    sine = np.where(same, sine, 0.0).astype(np.float32)
-    top = np.concatenate([cosine, -sine], axis=1)
-    bottom = np.concatenate([sine, cosine], axis=1)
-    return np.concatenate([top, bottom], axis=0)
+    cosine, sine = cos_sin(((rows_idx // 4) % 8) * ((cols_idx // 4) % 8), 8)
+    cosine = jnp.where(same, cosine, 0.0)
+    sine = jnp.where(same, sine, 0.0)
+    top = jnp.concatenate([cosine, -sine], axis=1)
+    bottom = jnp.concatenate([sine, cosine], axis=1)
+    return jnp.concatenate([top, bottom], axis=0)
 
 
 def z_twiddle_table():
-    rows_idx = np.arange(128)[:, None]
-    cols_idx = np.arange(192)[None, :]
-    return np.stack(np_cos_sin(rows_idx * ((cols_idx // 4) % 8), 1024))
+    rows_idx = lax.broadcasted_iota(jnp.int32, (128, 192), 0)
+    cols_idx = lax.broadcasted_iota(jnp.int32, (128, 192), 1)
+    return jnp.stack(cos_sin(rows_idx * ((cols_idx // 4) % 8), 1024))
 
 
 def y_twiddle_table():

time: 104 us -> 104 us (level)
  other arithmetic: 5.37 us -> 8.07 us
  waiting for transfers between devices: 35 us -> 32.7 us
    all_to_all x1, waiting for transfers between devices: 16.3 us -> 14 us  [shards(): lax.all_to_all(slabs, 'gz', split_axis=0, concat_axis=0, tiled=True)]
    neg x0 -> x1, other arithmetic: none -> 1.6 us  [block_dft8(): top = jnp.concatenate([cosine, -sine], axis=1)]
    sub x1 -> x2, other arithmetic: 0.11 us -> 1.17 us  [z_twiddle(): re * tw_cos - im * tw_sin]
    unnamed x30 -> x18, local copies, waits for them, and re-layouts: 3.35 us -> 3.38 us
  transfers between devices with their start and end apart: 2 -> 2, of which waited for: 2 -> 2; matrix products, arithmetic and copies ran while one was open for 2% -> 4% of each run, Pallas kernels for 0% -> 0%
where the time goes in v6:
time: 104 us; the launch traced here: 103 us
  waiting for transfers between devices  32.7 us (31%)
  blocking collectives  26.1 us (25%)
  starting transfers between devices  24.6 us (24%)
  other arithmetic  8.07 us (8%)
  local copies, waits for them, and re-layouts  6.55 us (6%)
  matrix products  2.81 us (3%)
  between operations  2.41 us (2%)
    all_to_all x1, waiting for transfers between devices, shards(): lax.all_to_all(back, 'gz', split_axis=0, concat_axis=0, tiled=True)  18.7 us
    all_to_all x1, starting transfers between devices, shards(): lax.all_to_all(slabs, 'gz', split_axis=0, concat_axis=0, tiled=True)  17.8 us
    all_gather x1, blocking collectives, shards(): spectral = dft4_across(lax.all_gather(fields, 'gy', axis=0), gy_index, -1)  14.2 us
    all_to_all x1, waiting for transfers between devices, shards(): lax.all_to_all(slabs, 'gz', split_axis=0, concat_axis=0, tiled=True)  14 us
    all_gather x1, blocking collectives, shards(): result = dft4_across(lax.all_gather(spatial, 'gy', axis=0), gy_index, 1)  12 us
    all_to_all x1, starting transfers between devices, shards(): lax.all_to_all(back, 'gz', split_axis=0, concat_axis=0, tiled=True)  6.76 us
    unnamed x18, local copies, waits for them, and re-layouts  3.38 us
    mul x6, other arithmetic, shards(): sum((kernel[source][target] * spec[:, part, target] for target in range(3)))  2.34 us
  transfers between devices with their start and end apart: 2, of which 2 were waited for; matrix products, arithmetic and copies ran while one was open for 4% of the time, Pallas kernels for 0%

profile of v6, /device:TPU:1, one launch (start us, length us, event | category | flops | bytes accessed | tf_op | source)
XLA Modules:
  0.0 103.3 jit_solution(16209249492128068716)
XLA Ops:
  0.0 0.1 fusion.53
  0.1 14.2 %all-gather = f32[8,3,2,8,512]{4,3,2,1,0:T(8,128)S(1)} all-gather(f32[2,3,2,8,512]{4,3,2,1,0:T(8,128)} %param.23), channel_id=2, replica_groups=mesh['gy'=4,'gz'=128] {'gy'}, dimensions={0}, use_global_device_ids=true | all-gather | bytes 983040 | tf_op jit(solution)/shard_map/all_gather | solution.py:252
  14.2 0.1 fusion.27
  14.4 0.6 copy-done.2
  15.1 0.6 copy-done.5
  15.8 0.6 copy-done.7
  16.5 0.1 copy.47
  16.7 0.8 copy-done
  17.4 0.3 fusion.65
  17.8 0.1 slice_add_fusion.2
  17.9 0.1 maximum_bitcast_fusion
  18.0 0.9 copy.48
  18.9 17.8 %all-to-all-start = ((f32[128,1,384]{2,1,0:T(1,128)}), f32[128,1,384]{2,1,0:T(1,128)S(1)}, u32[]{:S(2)}, u32[]{:S(2)}) async-start(f32[128,1,384]{2,1,0:T(1,128)} %copy.48), calls=%async_computation | async-start | bytes 393216 | tf_op jit(solution)/shard_map/all_to_all | solution.py:259
  36.8 0.6 copy-done.4
  37.4 0.7 fusion.64
  39.4 0.9 slice_reduce_fusion.11
  41.0 0.1 multiply_add_fusion.36
  41.0 0.3 slice_reduce_fusion.7
  41.3 0.1 pad_maximum_fusion.6
  41.4 0.1 fusion.46
  41.5 0.1 broadcast_in_dim.27
  41.6 0.1 broadcast_in_dim.26
  41.6 0.1 broadcast_in_dim.25
  41.8 1.6 %fusion.44 = (f32[192,192]{1,0:T(8,128)S(1)}, f32[192,192]{1,0:T(8,128)S(1)}, f32[192,192]{1,0:T(8,128)S(1)}) fusion(s32[192]{0:T(256)S(1)} %get-tuple-element.126, s32[192]{0:T(256)S(1)} %get-tuple-element.127, pred[192]{0:T(512)(128)(4,1)S(1)} %fusion.51, s32[192]{0:T(256)S(1)} %get-tuple-element.128, s32[192]{0:T(256)S(1)} %get-tuple-element.132, ...), kind=kLoop, calls=%fused_computation.211 | loop fusion | flops 1769472 | bytes 447552 | tf_op jit(solution)/shard_map/neg | solution.py:132
  43.4 14.0 %all-to-all-done = f32[128,1,384]{2,1,0:T(1,128)S(1)} async-done(((f32[128,1,384]{2,1,0:T(1,128)}), f32[128,1,384]{2,1,0:T(1,128)S(1)}, u32[]{:S(2)}, u32[]{:S(2)}) %all-to-all-start) | async-done | bytes 196640 | tf_op jit(solution)/shard_map/all_to_all | solution.py:259
  57.4 0.3 fusion.18
  57.7 0.6 multiply_subtract_fusion.1
  58.3 0.8 fusion.1
  59.1 0.4 add_multiply_fusion.5
  59.5 0.4 add_multiply_fusion.2
  59.9 0.4 add_multiply_fusion.4
  60.3 0.4 add_multiply_fusion.1
  60.7 0.4 add_multiply_fusion.3
  61.1 0.4 add_multiply_fusion
  61.6 0.6 fusion
  62.2 0.6 multiply_subtract_fusion
  62.8 0.4 fusion.11
  63.2 0.1 slice_subtract_fusion
  63.3 0.1 maximum_bitcast_fusion.1
  63.4 0.9 copy.50
  64.3 6.8 %all-to-all-start.1 = ((f32[128,1,384]{2,1,0:T(1,128)}), f32[128,1,384]{2,1,0:T(1,128)S(1)}, u32[]{:S(2)}, u32[]{:S(2)}) async-start(f32[128,1,384]{2,1,0:T(1,128)} %copy.50), calls=%async_computation.1 | async-start | bytes 393216 | tf_op jit(solution)/shard_map/all_to_all | solution.py:291
  71.1 18.7 %all-to-all-done.1 = f32[128,1,384]{2,1,0:T(1,128)S(1)} async-done(((f32[128,1,384]{2,1,0:T(1,128)}), f32[128,1,384]{2,1,0:T(1,128)S(1)}, u32[]{:S(2)}, u32[]{:S(2)}) %all-to-all-start.1) | async-done | bytes 196640 | tf_op jit(solution)/shard_map/all_to_all | solution.py:291
  89.8 0.4 fusion.15
  90.2 0.1 fusion.62
  90.3 0.1 fusion.63
  90.5 12.0 %all-gather.1 = f32[8,3,2,8,512]{4,3,2,1,0:T(8,128)S(1)} all-gather(f32[2,3,2,8,512]{4,3,2,1,0:T(8,128)S(1)} %pad_maximum_fusion.2), channel_id=3, replica_groups=mesh['gy'=4,'gz'=128] {'gy'}, dimensions={0}, use_global_device_ids=true | all-gather | bytes 983040 | tf_op jit(solution)/shard_map/all_gather | solution.py:294
  102.5 0.1 select_bitcast_fusion
  102.6 0.7 pad_maximum_fusion.3
  (46 shorter events, 0.5 us)
Async XLA Ops:
  14.3 0.7 copy-start.2
  14.4 0.7 copy-start.3
  15.1 0.7 copy-start.5
  15.1 0.7 copy-start.6
  15.8 0.7 copy-start.7
  15.8 0.7 copy-start.8
  16.5 0.9 copy-start
  18.9 38.5 %all-to-all-start = ((f32[128,1,384]{2,1,0:T(1,128)}), f32[128,1,384]{2,1,0:T(1,128)S(1)}, u32[]{:S(2)}, u32[]{:S(2)}) async-start(f32[128,1,384]{2,1,0:T(1,128)} %copy.48), calls=%async_computation | async-start | bytes 393216 | tf_op jit(solution)/shard_map/all_to_all | solution.py:259
  36.8 0.7 copy-start.4
  38.1 1.3 %copy-start.1 = (f32[3,6]{1,0:T(4,128)S(1)}, f32[3,6]{1,0:T(4,128)}, u32[]{:S(2)}) copy-start(f32[3,6]{1,0:T(4,128)} %param.24) | copy-start | bytes 220
  64.3 25.5 %all-to-all-start.1 = ((f32[128,1,384]{2,1,0:T(1,128)}), f32[128,1,384]{2,1,0:T(1,128)S(1)}, u32[]{:S(2)}, u32[]{:S(2)}) async-start(f32[128,1,384]{2,1,0:T(1,128)} %copy.50), calls=%async_computation.1 | async-start | bytes 393216 | tf_op jit(solution)/shard_map/all_to_all | solution.py:291

commit v7 on v6

--- a/solution.py
+++ b/solution.py
@@ -140,10 +140,6 @@
     return jnp.stack(cos_sin(rows_idx * ((cols_idx // 4) % 8), 1024))
 
 
-def y_twiddle_table():
-    return np.stack(np_cos_sin(np.arange(4)[:, None] * np.arange(128)[None, :], 512))
-
-
 def matmul(spec, left, right):
     return jnp.einsum(spec, left, right, precision=highest)
 
@@ -203,10 +199,10 @@
 def y_forward(spectral):
     parts = [(spectral[0, ..., 128 * a:128 * a + 128], spectral[1, ..., 128 * a:128 * a + 128]) for a in range(4)]
     mixed = dft4(parts, -1)
-    table = y_twiddle_table()
+    lanes = lax.broadcasted_iota(jnp.int32, (128,), 0)
     out = []
     for k1 in range(4):
-        tw_cos, tw_sin = table[0, k1], table[1, k1]
+        tw_cos, tw_sin = cos_sin(lanes * k1, 512)
         re, im = mixed[k1]
         out.append(jnp.stack([re * tw_cos + im * tw_sin, im * tw_cos - re * tw_sin]))
     stacked = jnp.stack(out, axis=-2).reshape(384, 128)
@@ -223,10 +219,10 @@
     s_im = product[192:, 128:]
     re = (c_re - s_im).reshape(3, 2, 8, 4, 128)
     im = (c_im + s_re).reshape(3, 2, 8, 4, 128)
-    table = y_twiddle_table()
+    lanes = lax.broadcasted_iota(jnp.int32, (128,), 0)
     parts = []
     for k1 in range(4):
-        tw_cos, tw_sin = table[0, k1], table[1, k1]
+        tw_cos, tw_sin = cos_sin(lanes * k1, 512)
         r = re[..., k1, :]
         i = im[..., k1, :]
         parts.append((r * tw_cos - i * tw_sin, i * tw_cos + r * tw_sin))

time: 104 us -> 102 us (0.981)
  local copies, waits for them, and re-layouts: 6.55 us -> 4.58 us
    unnamed x18 -> x6, local copies, waits for them, and re-layouts: 3.38 us -> 1.4 us
where the time goes in v7:
time: 102 us
  waiting for transfers between devices  32.9 us (32%)
  blocking collectives  26.1 us (26%)
  starting transfers between devices  24.8 us (24%)
  other arithmetic  8.15 us (8%)
  local copies, waits for them, and re-layouts  4.58 us (4%)
  matrix products  2.81 us (3%)
  between operations  2.24 us (2%)
    all_to_all x1, waiting for transfers between devices, shards(): lax.all_to_all(back, 'gz', split_axis=0, concat_axis=0, tiled=True)  18.7 us
    all_to_all x1, starting transfers between devices, shards(): lax.all_to_all(slabs, 'gz', split_axis=0, concat_axis=0, tiled=True)  17.8 us
    all_to_all x1, waiting for transfers between devices, shards(): lax.all_to_all(slabs, 'gz', split_axis=0, concat_axis=0, tiled=True)  14.3 us
    all_gather x1, blocking collectives, shards(): spectral = dft4_across(lax.all_gather(fields, 'gy', axis=0), gy_index, -1)  14.2 us
    all_gather x1, blocking collectives, shards(): result = dft4_across(lax.all_gather(spatial, 'gy', axis=0), gy_index, 1)  12 us
    all_to_all x1, starting transfers between devices, shards(): lax.all_to_all(back, 'gz', split_axis=0, concat_axis=0, tiled=True)  6.95 us
    mul x6, other arithmetic, shards(): sum((kernel[source][target] * spec[:, part, target] for target in range(3)))  2.34 us
  transfers between devices with their start and end apart: 2, of which 2 were waited for; matrix products, arithmetic and copies ran while one was open for 4% of the time, Pallas kernels for 0%

profile of v7, /device:TPU:1, one launch (start us, length us, event | category | flops | bytes accessed | tf_op | source)
XLA Modules:
  0.0 101.6 jit_solution(7279598620454835328)
XLA Ops:
  0.0 0.1 fusion.67
  0.1 0.1 fusion.65
  0.2 0.1 fusion.53
  0.2 14.2 %all-gather = f32[8,3,2,8,512]{4,3,2,1,0:T(8,128)S(1)} all-gather(f32[2,3,2,8,512]{4,3,2,1,0:T(8,128)} %param.7), channel_id=2, replica_groups=mesh['gy'=4,'gz'=128] {'gy'}, dimensions={0}, use_global_device_ids=true | all-gather | bytes 983040 | tf_op jit(solution)/shard_map/all_gather | solution.py:248
  14.4 0.1 fusion.27
  14.7 0.1 copy.31
  14.8 0.8 copy-done
  15.6 0.3 fusion.79
  15.9 0.1 slice_add_fusion.2
  16.0 0.1 maximum_bitcast_fusion
  16.1 0.9 copy.32
  17.0 17.8 %all-to-all-start = ((f32[128,1,384]{2,1,0:T(1,128)}), f32[128,1,384]{2,1,0:T(1,128)S(1)}, u32[]{:S(2)}, u32[]{:S(2)}) async-start(f32[128,1,384]{2,1,0:T(1,128)} %copy.32), calls=%async_computation | async-start | bytes 393216 | tf_op jit(solution)/shard_map/all_to_all | solution.py:255
  34.9 0.6 copy-done.2
  35.6 0.7 fusion.78
  37.5 0.8 slice_reduce_fusion.11
  38.9 0.1 multiply_add_fusion.36
  39.0 0.3 slice_reduce_fusion.7
  39.2 0.1 pad_maximum_fusion.6
  39.4 0.1 fusion.46
  39.5 0.1 broadcast_in_dim.27
  39.5 0.1 broadcast_in_dim.26
  39.6 0.1 broadcast_in_dim.25
  39.7 1.6 %fusion.44 = (f32[192,192]{1,0:T(8,128)S(1)}, f32[192,192]{1,0:T(8,128)S(1)}, f32[192,192]{1,0:T(8,128)S(1)}) fusion(s32[192]{0:T(256)S(1)} %get-tuple-element.126, s32[192]{0:T(256)S(1)} %get-tuple-element.127, pred[192]{0:T(512)(128)(4,1)S(1)} %fusion.51, s32[192]{0:T(256)S(1)} %get-tuple-element.128, s32[192]{0:T(256)S(1)} %get-tuple-element.132, ...), kind=kLoop, calls=%fused_computation.211 | loop fusion | flops 1769472 | bytes 447552 | tf_op jit(solution)/shard_map/neg | solution.py:132
  41.3 14.3 %all-to-all-done = f32[128,1,384]{2,1,0:T(1,128)S(1)} async-done(((f32[128,1,384]{2,1,0:T(1,128)}), f32[128,1,384]{2,1,0:T(1,128)S(1)}, u32[]{:S(2)}, u32[]{:S(2)}) %all-to-all-start) | async-done | bytes 196640 | tf_op jit(solution)/shard_map/all_to_all | solution.py:255
  55.6 0.3 fusion.18
  55.9 0.6 multiply_subtract_fusion.1
  56.5 0.8 fusion.1
  57.3 0.4 add_multiply_fusion.5
  57.7 0.4 add_multiply_fusion.2
  58.1 0.4 add_multiply_fusion.4
  58.5 0.4 add_multiply_fusion.1
  58.9 0.4 add_multiply_fusion.3
  59.3 0.4 add_multiply_fusion
  59.7 0.6 fusion
  60.4 0.6 multiply_subtract_fusion
  60.9 0.4 fusion.11
  61.3 0.1 slice_subtract_fusion
  61.5 0.1 maximum_bitcast_fusion.1
  61.6 0.9 copy.34
  62.5 6.9 %all-to-all-start.1 = ((f32[128,1,384]{2,1,0:T(1,128)}), f32[128,1,384]{2,1,0:T(1,128)S(1)}, u32[]{:S(2)}, u32[]{:S(2)}) async-start(f32[128,1,384]{2,1,0:T(1,128)} %copy.34), calls=%async_computation.1 | async-start | bytes 393216 | tf_op jit(solution)/shard_map/all_to_all | solution.py:287
  69.4 0.1 fusion.52
  69.5 18.7 %all-to-all-done.1 = f32[128,1,384]{2,1,0:T(1,128)S(1)} async-done(((f32[128,1,384]{2,1,0:T(1,128)}), f32[128,1,384]{2,1,0:T(1,128)S(1)}, u32[]{:S(2)}, u32[]{:S(2)}) %all-to-all-start.1) | async-done | bytes 196640 | tf_op jit(solution)/shard_map/all_to_all | solution.py:287
  88.1 0.4 fusion.15
  88.5 0.1 fusion.76
  88.6 0.1 fusion.77
  88.9 12.0 %all-gather.1 = f32[8,3,2,8,512]{4,3,2,1,0:T(8,128)S(1)} all-gather(f32[2,3,2,8,512]{4,3,2,1,0:T(8,128)S(1)} %pad_maximum_fusion.2), channel_id=3, replica_groups=mesh['gy'=4,'gz'=128] {'gy'}, dimensions={0}, use_global_device_ids=true | all-gather | bytes 983040 | tf_op jit(solution)/shard_map/all_gather | solution.py:290
  100.8 0.1 select_bitcast_fusion
  100.9 0.7 pad_maximum_fusion.3
  (37 shorter events, 0.5 us)
Async XLA Ops:
  14.7 0.9 copy-start
  17.0 38.5 %all-to-all-start = ((f32[128,1,384]{2,1,0:T(1,128)}), f32[128,1,384]{2,1,0:T(1,128)S(1)}, u32[]{:S(2)}, u32[]{:S(2)}) async-start(f32[128,1,384]{2,1,0:T(1,128)} %copy.32), calls=%async_computation | async-start | bytes 393216 | tf_op jit(solution)/shard_map/all_to_all | solution.py:255
  34.9 0.7 copy-start.2
  36.2 1.3 %copy-start.1 = (f32[3,6]{1,0:T(4,128)S(1)}, f32[3,6]{1,0:T(4,128)}, u32[]{:S(2)}) copy-start(f32[3,6]{1,0:T(4,128)} %param.8) | copy-start | bytes 220
  62.5 25.7 %all-to-all-start.1 = ((f32[128,1,384]{2,1,0:T(1,128)}), f32[128,1,384]{2,1,0:T(1,128)S(1)}, u32[]{:S(2)}, u32[]{:S(2)}) async-start(f32[128,1,384]{2,1,0:T(1,128)} %copy.34), calls=%async_computation.1 | async-start | bytes 393216 | tf_op jit(solution)/shard_map/all_to_all | solution.py:287

commit v8 on v7

--- a/solution.py
+++ b/solution.py
@@ -12,7 +12,7 @@
 NZ = 1024
 
 
-highest = lax.Precision.HIGH
+highest = lax.Precision.HIGHEST
 
 
 def partner_2(value, axis, stride):

time: 102 us -> 103 us (level)
  matrix products: 2.81 us -> 4.28 us
where the time goes in v8:
time: 103 us
  waiting for transfers between devices  32.7 us (32%)
  blocking collectives  26.1 us (25%)
  starting transfers between devices  24.8 us (24%)
  other arithmetic  8.15 us (8%)
  local copies, waits for them, and re-layouts  4.58 us (4%)
  matrix products  4.28 us (4%)
  between operations  2.24 us (2%)
    all_to_all x1, waiting for transfers between devices, shards(): lax.all_to_all(back, 'gz', split_axis=0, concat_axis=0, tiled=True)  18.7 us
    all_to_all x1, starting transfers between devices, shards(): lax.all_to_all(slabs, 'gz', split_axis=0, concat_axis=0, tiled=True)  18 us
    all_gather x1, blocking collectives, shards(): spectral = dft4_across(lax.all_gather(fields, 'gy', axis=0), gy_index, -1)  14.2 us
    all_to_all x1, waiting for transfers between devices, shards(): lax.all_to_all(slabs, 'gz', split_axis=0, concat_axis=0, tiled=True)  14.1 us
    all_gather x1, blocking collectives, shards(): result = dft4_across(lax.all_gather(spatial, 'gy', axis=0), gy_index, 1)  12 us
    all_to_all x1, starting transfers between devices, shards(): lax.all_to_all(back, 'gz', split_axis=0, concat_axis=0, tiled=True)  6.76 us
    dot_general x5, matrix products, matmul(): return jnp.einsum(spec, left, right, precision=highest)  2.98 us
    mul x6, other arithmetic, shards(): sum((kernel[source][target] * spec[:, part, target] for target in range(3)))  2.34 us
  transfers between devices with their start and end apart: 2, of which 2 were waited for; matrix products, arithmetic and copies ran while one was open for 4% of the time, Pallas kernels for 0%

profile of v8, /device:TPU:1, one launch (start us, length us, event | category | flops | bytes accessed | tf_op | source)
XLA Modules:
  0.0 102.9 jit_solution(2316654655067563992)
XLA Ops:
  0.0 0.1 fusion.67
  0.1 0.1 fusion.65
  0.2 0.1 fusion.53
  0.2 14.2 %all-gather = f32[8,3,2,8,512]{4,3,2,1,0:T(8,128)S(1)} all-gather(f32[2,3,2,8,512]{4,3,2,1,0:T(8,128)} %param.7), channel_id=2, replica_groups=mesh['gy'=4,'gz'=128] {'gy'}, dimensions={0}, use_global_device_ids=true | all-gather | bytes 983040 | tf_op jit(solution)/shard_map/all_gather | solution.py:248
  14.4 0.1 fusion.27
  14.7 0.1 copy.31
  14.8 0.8 copy-done
  15.6 0.5 fusion.79
  16.1 0.1 slice_add_fusion.2
  16.2 0.1 maximum_bitcast_fusion
  16.3 0.9 copy.32
  17.2 18.0 %all-to-all-start = ((f32[128,1,384]{2,1,0:T(1,128)}), f32[128,1,384]{2,1,0:T(1,128)S(1)}, u32[]{:S(2)}, u32[]{:S(2)}) async-start(f32[128,1,384]{2,1,0:T(1,128)} %copy.32), calls=%async_computation | async-start | bytes 393216 | tf_op jit(solution)/shard_map/all_to_all | solution.py:255
  35.3 0.6 copy-done.2
  35.9 0.7 fusion.78
  37.8 0.8 slice_reduce_fusion.11
  39.3 0.1 multiply_add_fusion.36
  39.3 0.3 slice_reduce_fusion.7
  39.6 0.1 pad_maximum_fusion.6
  39.7 0.1 fusion.46
  39.8 0.1 broadcast_in_dim.27
  39.9 0.1 broadcast_in_dim.26
  39.9 0.1 broadcast_in_dim.25
  40.1 1.6 %fusion.44 = (f32[192,192]{1,0:T(8,128)S(1)}, f32[192,192]{1,0:T(8,128)S(1)}, f32[192,192]{1,0:T(8,128)S(1)}) fusion(s32[192]{0:T(256)S(1)} %get-tuple-element.126, s32[192]{0:T(256)S(1)} %get-tuple-element.127, pred[192]{0:T(512)(128)(4,1)S(1)} %fusion.51, s32[192]{0:T(256)S(1)} %get-tuple-element.128, s32[192]{0:T(256)S(1)} %get-tuple-element.132, ...), kind=kLoop, calls=%fused_computation.211 | loop fusion | flops 1769472 | bytes 447552 | tf_op jit(solution)/shard_map/neg | solution.py:132
  41.7 14.1 %all-to-all-done = f32[128,1,384]{2,1,0:T(1,128)S(1)} async-done(((f32[128,1,384]{2,1,0:T(1,128)}), f32[128,1,384]{2,1,0:T(1,128)S(1)}, u32[]{:S(2)}, u32[]{:S(2)}) %all-to-all-start) | async-done | bytes 196640 | tf_op jit(solution)/shard_map/all_to_all | solution.py:255
  55.7 0.5 fusion.18
  56.2 0.6 multiply_subtract_fusion.1
  56.8 1.3 %fusion.1 = f32[128,384]{0,1:T(8,128)S(1)} fusion(f32[192,192]{1,0:T(8,128)S(1)} %get-tuple-element.108, f32[192,192]{1,0:T(8,128)S(1)} %get-tuple-element.107, f32[192,192]{1,0:T(8,128)S(1)} %get-tuple-element.106, f32[128,192]{1,0:T(8,128)S(1)} %get-tuple-element.51, f32[128,192]{1,0:T(8,128)S(1)} %get-tuple-element.50), kind=kOutput, calls=%fused_computation.8 | convolution fusion | flops 226983936 | bytes 835584 | tf_op jit(solution)/shard_map/dot_general | solution.py:258
  58.1 0.4 add_multiply_fusion.5
  58.5 0.4 add_multiply_fusion.2
  58.9 0.4 add_multiply_fusion.4
  59.3 0.4 add_multiply_fusion.1
  59.7 0.4 add_multiply_fusion.3
  60.1 0.4 add_multiply_fusion
  60.5 1.0 fusion
  61.5 0.6 multiply_subtract_fusion
  62.1 0.5 fusion.11
  62.6 0.1 slice_subtract_fusion
  62.8 0.1 maximum_bitcast_fusion.1
  62.9 0.9 copy.34
  63.8 6.8 %all-to-all-start.1 = ((f32[128,1,384]{2,1,0:T(1,128)}), f32[128,1,384]{2,1,0:T(1,128)S(1)}, u32[]{:S(2)}, u32[]{:S(2)}) async-start(f32[128,1,384]{2,1,0:T(1,128)} %copy.34), calls=%async_computation.1 | async-start | bytes 393216 | tf_op jit(solution)/shard_map/all_to_all | solution.py:287
  70.5 0.1 fusion.52
  70.6 18.7 %all-to-all-done.1 = f32[128,1,384]{2,1,0:T(1,128)S(1)} async-done(((f32[128,1,384]{2,1,0:T(1,128)}), f32[128,1,384]{2,1,0:T(1,128)S(1)}, u32[]{:S(2)}, u32[]{:S(2)}) %all-to-all-start.1) | async-done | bytes 196640 | tf_op jit(solution)/shard_map/all_to_all | solution.py:287
  89.3 0.5 fusion.15
  89.8 0.1 fusion.76
  89.9 0.1 fusion.77
  90.1 12.0 %all-gather.1 = f32[8,3,2,8,512]{4,3,2,1,0:T(8,128)S(1)} all-gather(f32[2,3,2,8,512]{4,3,2,1,0:T(8,128)S(1)} %pad_maximum_fusion.2), channel_id=3, replica_groups=mesh['gy'=4,'gz'=128] {'gy'}, dimensions={0}, use_global_device_ids=true | all-gather | bytes 983040 | tf_op jit(solution)/shard_map/all_gather | solution.py:290
  102.1 0.1 select_bitcast_fusion
  102.2 0.7 pad_maximum_fusion.3
  (37 shorter events, 0.5 us)
Async XLA Ops:
  14.7 0.9 copy-start
  17.2 38.5 %all-to-all-start = ((f32[128,1,384]{2,1,0:T(1,128)}), f32[128,1,384]{2,1,0:T(1,128)S(1)}, u32[]{:S(2)}, u32[]{:S(2)}) async-start(f32[128,1,384]{2,1,0:T(1,128)} %copy.32), calls=%async_computation | async-start | bytes 393216 | tf_op jit(solution)/shard_map/all_to_all | solution.py:255
  35.3 0.7 copy-start.2
  36.6 1.3 %copy-start.1 = (f32[3,6]{1,0:T(4,128)S(1)}, f32[3,6]{1,0:T(4,128)}, u32[]{:S(2)}) copy-start(f32[3,6]{1,0:T(4,128)} %param.8) | copy-start | bytes 220
  63.8 25.5 %all-to-all-start.1 = ((f32[128,1,384]{2,1,0:T(1,128)}), f32[128,1,384]{2,1,0:T(1,128)S(1)}, u32[]{:S(2)}, u32[]{:S(2)}) async-start(f32[128,1,384]{2,1,0:T(1,128)} %copy.34), calls=%async_computation.1 | async-start | bytes 393216 | tf_op jit(solution)/shard_map/all_to_all | solution.py:287

commit v9 on v8

--- a/solution.py
+++ b/solution.py
@@ -267,19 +267,9 @@
     kernel = kernel_rows(kx_wave, ky_wave, kz_wave, eigenstrain, moduli)
     scale = 1.0 / (NY * NZ)
     spec = spectrum.reshape(128, 2, 3, 64)
-    forced = jnp.stack(
-        [
-            jnp.stack(
-                [
-                    sum((kernel[source][target] * spec[:, part, target] for target in range(3))) * scale
-                    for source in range(3)
-                ],
-                axis=1,
-            )
-            for part in range(2)
-        ],
-        axis=1,
-    ).reshape(128, 384)
+    coupled = jnp.stack([jnp.stack([kernel[source][target] for target in range(3)], axis=1) for source in range(3)], axis=1)
+    forced = (coupled[:, None] * spec[:, :, None]).sum(axis=3) * scale
+    forced = forced.reshape(128, 384)
     back = matmul("kr,sr->ks", forced, block_dft8())
     back = z_twiddle(back[:, :192], back[:, 192:], 1)
     re, im = combine_rows(matmul("kg,gc->kc", table, back), 1)

time: 103 us -> 101 us (0.981)
  waiting for transfers between devices: 32.7 us -> 30.7 us
    select_n x0 -> x9, other arithmetic: none -> 2.47 us  [kernel_rows(): kernel_row.append(jnp.where(inside, energy[source, target] - coupling, 0.0))]
    mul x6 -> x1, other arithmetic: 2.34 us -> 0.02 us  [shards(): forced = (coupled[:, None] * spec[:, :, None]).sum(axis=3) * scale]
    all_to_all x1, waiting for transfers between devices: 14.1 us -> 12 us  [shards(): lax.all_to_all(slabs, 'gz', split_axis=0, concat_axis=0, tiled=True)]
  transfers between devices with their start and end apart: 2 -> 2, of which waited for: 2 -> 2; matrix products, arithmetic and copies ran while one was open for 4% -> 6% of each run, Pallas kernels for 0% -> 0%
where the time goes in v9:
time: 101 us
  waiting for transfers between devices  30.7 us (30%)
  blocking collectives  26.1 us (26%)
  starting transfers between devices  24.9 us (25%)
  other arithmetic  8.41 us (8%)
  matrix products  4.27 us (4%)
  local copies, waits for them, and re-layouts  3.93 us (4%)
  between operations  2.32 us (2%)
    all_to_all x1, waiting for transfers between devices, shards(): lax.all_to_all(back, 'gz', split_axis=0, concat_axis=0, tiled=True)  18.7 us
    all_to_all x1, starting transfers between devices, shards(): lax.all_to_all(slabs, 'gz', split_axis=0, concat_axis=0, tiled=True)  18.1 us
    all_gather x1, blocking collectives, shards(): spectral = dft4_across(lax.all_gather(fields, 'gy', axis=0), gy_index, -1)  14.2 us
    all_to_all x1, waiting for transfers between devices, shards(): lax.all_to_all(slabs, 'gz', split_axis=0, concat_axis=0, tiled=True)  12 us
    all_gather x1, blocking collectives, shards(): result = dft4_across(lax.all_gather(spatial, 'gy', axis=0), gy_index, 1)  12 us
    all_to_all x1, starting transfers between devices, shards(): lax.all_to_all(back, 'gz', split_axis=0, concat_axis=0, tiled=True)  6.76 us
    dot_general x5, matrix products, matmul(): return jnp.einsum(spec, left, right, precision=highest)  2.99 us
    select_n x9, other arithmetic, kernel_rows(): kernel_row.append(jnp.where(inside, energy[source, target] - coupling, 0.0))  2.47 us
  transfers between devices with their start and end apart: 2, of which 2 were waited for; matrix products, arithmetic and copies ran while one was open for 6% of the time, Pallas kernels for 0%

profile of v9, /device:TPU:1, one launch (start us, length us, event | category | flops | bytes accessed | tf_op | source)
XLA Modules:
  0.0 100.7 jit_solution(14616450029151161426)
XLA Ops:
  0.1 0.1 fusion.65
  0.2 0.1 fusion.53
  0.2 14.2 %all-gather = f32[8,3,2,8,512]{4,3,2,1,0:T(8,128)S(1)} all-gather(f32[2,3,2,8,512]{4,3,2,1,0:T(8,128)} %param.7), channel_id=2, replica_groups=mesh['gy'=4,'gz'=128] {'gy'}, dimensions={0}, use_global_device_ids=true | all-gather | bytes 983040 | tf_op jit(solution)/shard_map/all_gather | solution.py:248
  14.4 0.1 fusion.27
  14.7 0.1 copy.43
  14.8 0.8 copy-done
  15.6 0.5 fusion.79
  16.1 0.1 slice_add_fusion.2
  16.2 0.1 maximum_bitcast_fusion
  16.3 0.9 copy.44
  17.2 18.1 %all-to-all-start = ((f32[128,1,384]{2,1,0:T(1,128)}), f32[128,1,384]{2,1,0:T(1,128)S(1)}, u32[]{:S(2)}, u32[]{:S(2)}) async-start(f32[128,1,384]{2,1,0:T(1,128)} %copy.44), calls=%async_computation | async-start | bytes 393216 | tf_op jit(solution)/shard_map/all_to_all | solution.py:255
  35.4 0.6 fusion.78
  37.2 0.9 slice_reduce_fusion.11
  38.8 0.1 multiply_add_fusion.36
  38.8 0.3 slice_reduce_fusion.7
  39.1 0.1 pad_maximum_fusion.6
  39.3 0.1 fusion.46
  39.4 0.1 broadcast_in_dim.27
  39.4 0.1 broadcast_in_dim.26
  39.5 0.1 broadcast_in_dim.25
  39.6 0.2 subtract_select_fusion.8
  39.9 0.3 subtract_select_fusion.6
  40.2 0.3 subtract_select_fusion.7
  40.5 0.3 subtract_select_fusion.3
  40.8 0.3 subtract_select_fusion.5
  41.0 0.2 subtract_select_fusion.4
  41.3 0.3 subtract_select_fusion.1
  41.6 0.2 subtract_select_fusion
  41.9 0.3 subtract_select_fusion.2
  42.2 1.6 %fusion.44 = (f32[192,192]{1,0:T(8,128)S(1)}, f32[192,192]{1,0:T(8,128)S(1)}, f32[192,192]{1,0:T(8,128)S(1)}) fusion(s32[192]{0:T(256)S(1)} %get-tuple-element.126, s32[192]{0:T(256)S(1)} %get-tuple-element.127, pred[192]{0:T(512)(128)(4,1)S(1)} %fusion.51, s32[192]{0:T(256)S(1)} %get-tuple-element.128, s32[192]{0:T(256)S(1)} %get-tuple-element.132, ...), kind=kLoop, calls=%fused_computation.202 | loop fusion | flops 1769472 | bytes 447552 | tf_op jit(solution)/shard_map/neg | solution.py:132
  43.9 12.0 %all-to-all-done = f32[128,1,384]{2,1,0:T(1,128)S(1)} async-done(((f32[128,1,384]{2,1,0:T(1,128)}), f32[128,1,384]{2,1,0:T(1,128)S(1)}, u32[]{:S(2)}, u32[]{:S(2)}) %all-to-all-start) | async-done | bytes 196640 | tf_op jit(solution)/shard_map/all_to_all | solution.py:255
  55.9 0.5 fusion.18
  56.3 0.6 multiply_subtract_fusion.1
  56.9 1.3 %fusion.1 = f32[128,384]{0,1:T(8,128)S(1)} fusion(f32[192,192]{1,0:T(8,128)S(1)} %get-tuple-element.108, f32[192,192]{1,0:T(8,128)S(1)} %get-tuple-element.107, f32[192,192]{1,0:T(8,128)S(1)} %get-tuple-element.106, f32[128,192]{1,0:T(8,128)S(1)} %get-tuple-element.51, f32[128,192]{1,0:T(8,128)S(1)} %get-tuple-element.50), kind=kOutput, calls=%fused_computation.9 | convolution fusion | flops 226983936 | bytes 835584 | tf_op jit(solution)/shard_map/dot_general | solution.py:258
  58.3 1.0 fusion
  59.3 0.6 multiply_subtract_fusion
  59.9 0.5 fusion.11
  60.4 0.1 slice_subtract_fusion
  60.6 0.1 maximum_bitcast_fusion.1
  60.7 0.9 copy.46
  61.5 6.8 %all-to-all-start.1 = ((f32[128,1,384]{2,1,0:T(1,128)}), f32[128,1,384]{2,1,0:T(1,128)S(1)}, u32[]{:S(2)}, u32[]{:S(2)}) async-start(f32[128,1,384]{2,1,0:T(1,128)} %copy.46), calls=%async_computation.1 | async-start | bytes 393216 | tf_op jit(solution)/shard_map/all_to_all | solution.py:277
  68.4 18.7 %all-to-all-done.1 = f32[128,1,384]{2,1,0:T(1,128)S(1)} async-done(((f32[128,1,384]{2,1,0:T(1,128)}), f32[128,1,384]{2,1,0:T(1,128)S(1)}, u32[]{:S(2)}, u32[]{:S(2)}) %all-to-all-start.1) | async-done | bytes 196640 | tf_op jit(solution)/shard_map/all_to_all | solution.py:277
  87.0 0.5 fusion.15
  87.6 0.1 fusion.76
  87.7 0.1 fusion.77
  87.9 12.0 %all-gather.1 = f32[8,3,2,8,512]{4,3,2,1,0:T(8,128)S(1)} all-gather(f32[2,3,2,8,512]{4,3,2,1,0:T(8,128)S(1)} %pad_maximum_fusion.2), channel_id=3, replica_groups=mesh['gy'=4,'gz'=128] {'gy'}, dimensions={0}, use_global_device_ids=true | all-gather | bytes 983040 | tf_op jit(solution)/shard_map/all_gather | solution.py:280
  99.9 0.1 select_bitcast_fusion
  100.0 0.7 pad_maximum_fusion.3
  (43 shorter events, 0.6 us)
Async XLA Ops:
  14.7 0.9 copy-start
  17.2 18.2 %copy-start.2 = (f32[3]{0:T(128)S(1)}, f32[3]{0:T(128)}, u32[]{:S(2)}) copy-start(f32[3]{0:T(128)} %param.9) | copy-start | bytes 40
  17.2 38.7 %all-to-all-start = ((f32[128,1,384]{2,1,0:T(1,128)}), f32[128,1,384]{2,1,0:T(1,128)S(1)}, u32[]{:S(2)}, u32[]{:S(2)}) async-start(f32[128,1,384]{2,1,0:T(1,128)} %copy.44), calls=%async_computation | async-start | bytes 393216 | tf_op jit(solution)/shard_map/all_to_all | solution.py:255
  36.0 1.2 %copy-start.1 = (f32[3,6]{1,0:T(4,128)S(1)}, f32[3,6]{1,0:T(4,128)}, u32[]{:S(2)}) copy-start(f32[3,6]{1,0:T(4,128)} %param.8) | copy-start | bytes 220
  61.5 25.5 %all-to-all-start.1 = ((f32[128,1,384]{2,1,0:T(1,128)}), f32[128,1,384]{2,1,0:T(1,128)S(1)}, u32[]{:S(2)}, u32[]{:S(2)}) async-start(f32[128,1,384]{2,1,0:T(1,128)} %copy.46), calls=%async_computation.1 | async-start | bytes 393216 | tf_op jit(solution)/shard_map/all_to_all | solution.py:277

commit v10 on v9

--- a/solution.py
+++ b/solution.py
@@ -5,7 +5,7 @@
 import jax
 import jax.numpy as jnp
 from jax import lax
-from jax.sharding import PartitionSpec as P
+from jax.sharding import Mesh, PartitionSpec as P
 
 NX = 2048
 NY = 2048
@@ -240,12 +240,12 @@
 
 
 def shards(fields, eigenstrain, moduli):
-    gy_count = lax.axis_size("gy")
-    gy_index = lax.axis_index("gy")
+    gy_count = lax.axis_size("gy_chip") * lax.axis_size("gy_core")
+    gy_index = lax.axis_index("gy_chip") * lax.axis_size("gy_core") + lax.axis_index("gy_core")
     gz_index = lax.axis_index("gz")
     y_local = fields.shape[4]
     positions = lax.broadcasted_iota(jnp.int32, (y_local,), 0)
-    spectral = dft4_across(lax.all_gather(fields, "gy", axis=0), gy_index, -1)
+    spectral = dft4_across(lax.all_gather(fields, ("gy_chip", "gy_core"), axis=0), gy_index, -1)
     residue = gy_index
     angle = 2.0 * math.pi / NY * (positions * residue % NY).astype(jnp.float32)
     phase_cos = jnp.cos(angle)
@@ -277,11 +277,14 @@
     returned = lax.all_to_all(back, "gz", split_axis=0, concat_axis=0, tiled=True)
     spatial = y_inverse(returned)
     spatial = twiddle(spatial, phase_cos, phase_sin)
-    result = dft4_across(lax.all_gather(spatial, "gy", axis=0), gy_index, 1)
+    gathered = lax.all_gather(spatial, ("gy_core", "gy_chip"), axis=0)
+    result = dft4_across(gathered[jnp.array([0, 2, 1, 3])], gy_index, 1)
     return result
 
 
 def solution(mesh):
-    in_specs = (P(None, None, None, "gz", "gy"), P(), P())
-    out_specs = P(None, None, None, "gz", "gy")
-    return jax.shard_map(shards, mesh=mesh, in_specs=in_specs, out_specs=out_specs, check_vma=False)
+    chips = mesh.shape["gy"] // 2
+    split = Mesh(mesh.devices.reshape(chips, 2, mesh.shape["gz"]), ("gy_chip", "gy_core", "gz"))
+    block = P(None, None, None, "gz", ("gy_chip", "gy_core"))
+    in_specs = (block, P(), P())
+    return jax.shard_map(shards, mesh=split, in_specs=in_specs, out_specs=block, check_vma=False)

time: 101 us -> 109 us (1.079)
  blocking collectives: 26.1 us -> 34 us
  local copies, waits for them, and re-layouts: 3.93 us -> 5.15 us
    all_gather x2, blocking collectives: 26.1 us -> 34 us  [the longest x1 19.9 us: shards(): gathered = lax.all_gather(spatial, ('gy_core', 'gy_chip'), axis=0)]
where the time goes in v10:
time: 109 us
  blocking collectives  34 us (31%)
  waiting for transfers between devices  30.1 us (28%)
  starting transfers between devices  24.9 us (23%)
  other arithmetic  8.36 us (8%)
  local copies, waits for them, and re-layouts  5.15 us (5%)
  matrix products  4.27 us (4%)
  between operations  2.38 us (2%)
    all_gather x1, blocking collectives, shards(): gathered = lax.all_gather(spatial, ('gy_core', 'gy_chip'), axis=0)  19.9 us
    all_to_all x1, starting transfers between devices, shards(): lax.all_to_all(slabs, 'gz', split_axis=0, concat_axis=0, tiled=True)  18.1 us
    all_to_all x1, waiting for transfers between devices, shards(): lax.all_to_all(back, 'gz', split_axis=0, concat_axis=0, tiled=True)  18 us
    all_gather x1, blocking collectives, shards(): lax.all_gather(fields, ('gy_chip', 'gy_core'), axis=0)  14.2 us
    all_to_all x1, waiting for transfers between devices, shards(): lax.all_to_all(slabs, 'gz', split_axis=0, concat_axis=0, tiled=True)  12 us
    all_to_all x1, starting transfers between devices, shards(): lax.all_to_all(back, 'gz', split_axis=0, concat_axis=0, tiled=True)  6.76 us
    dot_general x5, matrix products, matmul(): return jnp.einsum(spec, left, right, precision=highest)  2.99 us
    select_n x9, other arithmetic, kernel_rows(): kernel_row.append(jnp.where(inside, energy[source, target] - coupling, 0.0))  2.47 us
  transfers between devices with their start and end apart: 2, of which 2 were waited for; matrix products, arithmetic and copies ran while one was open for 6% of the time, Pallas kernels for 0%

profile of v10, /device:TPU:1, one launch (start us, length us, event | category | flops | bytes accessed | tf_op | source)
XLA Modules:
  0.0 109.2 jit_solution(8910604910924250958)
XLA Ops:
  0.2 14.2 %all-gather = f32[8,3,2,8,512]{4,3,2,1,0:T(8,128)S(1)} all-gather(f32[2,3,2,8,512]{4,3,2,1,0:T(8,128)} %param.8), channel_id=2, replica_groups=mesh['gy_chip'=2,'gy_core'=2,'gz'=128] {'gy_chip','gy_core'}, dimensions={0}, use_global_device_ids=true | all-gather | bytes 983040 | tf_op jit(solution)/shard_map/all_gather | solution.py:248
  14.4 0.1 fusion.27
  14.7 0.1 copy.44
  14.8 0.8 copy-done
  15.6 0.5 fusion.79
  16.1 0.1 slice_add_fusion.2
  16.2 0.1 maximum_bitcast_fusion
  16.3 0.9 copy.45
  17.2 18.1 %all-to-all-start = ((f32[128,1,384]{2,1,0:T(1,128)}), f32[128,1,384]{2,1,0:T(1,128)S(1)}, u32[]{:S(2)}, u32[]{:S(2)}) async-start(f32[128,1,384]{2,1,0:T(1,128)} %copy.45), calls=%async_computation | async-start | bytes 393216 | tf_op jit(solution)/shard_map/all_to_all | solution.py:255
  35.4 0.7 fusion.78
  37.3 0.8 slice_reduce_fusion.11
  38.8 0.1 multiply_add_fusion.36
  38.9 0.3 slice_reduce_fusion.7
  39.1 0.1 pad_maximum_fusion.6
  39.3 0.1 fusion.46
  39.4 0.1 broadcast_in_dim.29
  39.4 0.1 broadcast_in_dim.28
  39.5 0.1 broadcast_in_dim.27
  39.6 0.2 subtract_select_fusion.8
  39.9 0.3 subtract_select_fusion.6
  40.2 0.3 subtract_select_fusion.7
  40.5 0.3 subtract_select_fusion.3
  40.8 0.3 subtract_select_fusion.5
  41.1 0.2 subtract_select_fusion.4
  41.3 0.3 subtract_select_fusion.1
  41.6 0.2 subtract_select_fusion
  41.9 0.3 subtract_select_fusion.2
  42.3 1.6 %fusion.44 = (f32[192,192]{1,0:T(8,128)S(1)}, f32[192,192]{1,0:T(8,128)S(1)}, f32[192,192]{1,0:T(8,128)S(1)}) fusion(s32[192]{0:T(256)S(1)} %get-tuple-element.126, s32[192]{0:T(256)S(1)} %get-tuple-element.127, pred[192]{0:T(512)(128)(4,1)S(1)} %fusion.51, s32[192]{0:T(256)S(1)} %get-tuple-element.128, s32[192]{0:T(256)S(1)} %get-tuple-element.132, ...), kind=kLoop, calls=%fused_computation.204 | loop fusion | flops 1769472 | bytes 447552 | tf_op jit(solution)/shard_map/neg | solution.py:132
  43.9 12.0 %all-to-all-done = f32[128,1,384]{2,1,0:T(1,128)S(1)} async-done(((f32[128,1,384]{2,1,0:T(1,128)}), f32[128,1,384]{2,1,0:T(1,128)S(1)}, u32[]{:S(2)}, u32[]{:S(2)}) %all-to-all-start) | async-done | bytes 196640 | tf_op jit(solution)/shard_map/all_to_all | solution.py:255
  55.9 0.5 fusion.18
  56.3 0.6 multiply_subtract_fusion.1
  56.9 1.3 %fusion.1 = f32[128,384]{0,1:T(8,128)S(1)} fusion(f32[192,192]{1,0:T(8,128)S(1)} %get-tuple-element.108, f32[192,192]{1,0:T(8,128)S(1)} %get-tuple-element.107, f32[192,192]{1,0:T(8,128)S(1)} %get-tuple-element.106, f32[128,192]{1,0:T(8,128)S(1)} %get-tuple-element.51, f32[128,192]{1,0:T(8,128)S(1)} %get-tuple-element.50), kind=kOutput, calls=%fused_computation.10 | convolution fusion | flops 226983936 | bytes 835584 | tf_op jit(solution)/shard_map/dot_general | solution.py:258
  58.3 1.0 fusion
  59.3 0.6 multiply_subtract_fusion
  59.9 0.5 fusion.11
  60.4 0.1 slice_subtract_fusion
  60.5 0.1 maximum_bitcast_fusion.1
  60.6 0.9 copy.47
  61.5 6.8 %all-to-all-start.1 = ((f32[128,1,384]{2,1,0:T(1,128)}), f32[128,1,384]{2,1,0:T(1,128)S(1)}, u32[]{:S(2)}, u32[]{:S(2)}) async-start(f32[128,1,384]{2,1,0:T(1,128)} %copy.47), calls=%async_computation.1 | async-start | bytes 393216 | tf_op jit(solution)/shard_map/all_to_all | solution.py:277
  68.4 0.6 copy-done.3
  69.0 18.0 %all-to-all-done.1 = f32[128,1,384]{2,1,0:T(1,128)S(1)} async-done(((f32[128,1,384]{2,1,0:T(1,128)}), f32[128,1,384]{2,1,0:T(1,128)S(1)}, u32[]{:S(2)}, u32[]{:S(2)}) %all-to-all-start.1) | async-done | bytes 196640 | tf_op jit(solution)/shard_map/all_to_all | solution.py:277
  87.0 0.5 fusion.15
  87.6 0.1 fusion.76
  87.7 0.1 fusion.77
  87.9 19.9 %all-gather.1 = f32[8,3,2,8,512]{4,3,2,1,0:T(8,128)S(1)} all-gather(f32[2,3,2,8,512]{4,3,2,1,0:T(8,128)S(1)} %pad_maximum_fusion.2), channel_id=3, replica_groups=mesh['gy_chip'=2,'gy_core'=2,'gz'=128] {'gy_core','gy_chip'}, dimensions={0}, use_global_device_ids=true | all-gather | bytes 983040 | tf_op jit(solution)/shard_map/all_gather | solution.py:280
  107.8 0.6 gather_fusion
  108.4 0.1 select_bitcast_fusion
  108.5 0.7 pad_maximum_fusion.3
  (47 shorter events, 0.7 us)
Async XLA Ops:
  14.7 0.9 copy-start
  17.2 18.2 %copy-start.2 = (f32[3]{0:T(128)S(1)}, f32[3]{0:T(128)}, u32[]{:S(2)}) copy-start(f32[3]{0:T(128)} %param.10) | copy-start | bytes 40
  17.2 38.7 %all-to-all-start = ((f32[128,1,384]{2,1,0:T(1,128)}), f32[128,1,384]{2,1,0:T(1,128)S(1)}, u32[]{:S(2)}, u32[]{:S(2)}) async-start(f32[128,1,384]{2,1,0:T(1,128)} %copy.45), calls=%async_computation | async-start | bytes 393216 | tf_op jit(solution)/shard_map/all_to_all | solution.py:255
  36.0 1.3 %copy-start.1 = (f32[3,6]{1,0:T(4,128)S(1)}, f32[3,6]{1,0:T(4,128)}, u32[]{:S(2)}) copy-start(f32[3,6]{1,0:T(4,128)} %param.9) | copy-start | bytes 220
  61.5 25.5 %all-to-all-start.1 = ((f32[128,1,384]{2,1,0:T(1,128)}), f32[128,1,384]{2,1,0:T(1,128)S(1)}, u32[]{:S(2)}, u32[]{:S(2)}) async-start(f32[128,1,384]{2,1,0:T(1,128)} %copy.47), calls=%async_computation.1 | async-start | bytes 393216 | tf_op jit(solution)/shard_map/all_to_all | solution.py:277
  68.3 0.7 copy-start.3

commit v11 on v9

--- a/solution.py
+++ b/solution.py
@@ -134,6 +134,36 @@
     return jnp.concatenate([top, bottom], axis=0)
 
 
+def dft8_apply(values, inverse):
+    matrix = block_dft8_np()
+    if inverse:
+        matrix = matrix.T
+    unit = np.where(np.abs(matrix) > 0.9, np.sign(matrix), 0.0)
+    half = np.where((np.abs(matrix) > 0.5) & (np.abs(matrix) < 0.9), np.sign(matrix), 0.0)
+    table = jnp.asarray(np.concatenate([unit, half], axis=1), jnp.bfloat16)
+    first = lax.reduce_precision(values, exponent_bits=8, mantissa_bits=7)
+    rest = values - first
+    second = lax.reduce_precision(rest, exponent_bits=8, mantissa_bits=7)
+    third = rest - second
+    parts = jnp.concatenate([first, second, third], axis=0).astype(jnp.bfloat16)
+    product = jnp.dot(parts, table, preferred_element_type=jnp.float32)
+    summed = product[:128] + product[128:256] + product[256:]
+    return summed[:, :384] + np.float32(math.sqrt(0.5)) * summed[:, 384:]
+
+
+def block_dft8_np():
+    size = 192
+    rows_idx = np.arange(size)[:, None]
+    cols_idx = np.arange(size)[None, :]
+    same = (rows_idx // 32 == cols_idx // 32) & (rows_idx % 4 == cols_idx % 4)
+    cosine, sine = np_cos_sin(((rows_idx // 4) % 8) * ((cols_idx // 4) % 8), 8)
+    cosine = np.where(same, cosine, 0.0).astype(np.float32)
+    sine = np.where(same, sine, 0.0).astype(np.float32)
+    top = np.concatenate([cosine, -sine], axis=1)
+    bottom = np.concatenate([sine, cosine], axis=1)
+    return np.concatenate([top, bottom], axis=0)
+
+
 def z_twiddle_table():
     rows_idx = lax.broadcasted_iota(jnp.int32, (128, 192), 0)
     cols_idx = lax.broadcasted_iota(jnp.int32, (128, 192), 1)
@@ -255,7 +285,7 @@
     pencils = lax.all_to_all(slabs, "gz", split_axis=0, concat_axis=0, tiled=True)
     table = stacked_table(128)
     re, im = combine_rows(matmul("kg,gc->kc", table, pencils), -1)
-    spectrum = jnp.dot(z_twiddle(re, im, -1), block_dft8(), precision=highest)
+    spectrum = dft8_apply(z_twiddle(re, im, -1), False)
     rows_idx = lax.broadcasted_iota(jnp.int32, (128, 64), 0)
     cols_idx = lax.broadcasted_iota(jnp.int32, (128, 64), 1)
     plane = cols_idx // 32
@@ -270,7 +300,7 @@
     coupled = jnp.stack([jnp.stack([kernel[source][target] for target in range(3)], axis=1) for source in range(3)], axis=1)
     forced = (coupled[:, None] * spec[:, :, None]).sum(axis=3) * scale
     forced = forced.reshape(128, 384)
-    back = matmul("kr,sr->ks", forced, block_dft8())
+    back = dft8_apply(forced, True)
     back = z_twiddle(back[:, :192], back[:, 192:], 1)
     re, im = combine_rows(matmul("kg,gc->kc", table, back), 1)
     back = jnp.concatenate([re, im], axis=1)

time: 101 us -> 101 us (level)
  waiting for transfers between devices: 30.7 us -> 32.5 us
  matrix products: 4.27 us -> 2.94 us
  other arithmetic: 8.41 us -> 7.15 us
    all_to_all x1, waiting for transfers between devices: 12 us -> 13.8 us  [shards(): lax.all_to_all(slabs, 'gz', split_axis=0, concat_axis=0, tiled=True)]
    neg x1 -> x0, other arithmetic: 1.6 us -> none  [block_dft8(): top = jnp.concatenate([cosine, -sine], axis=1)]
    dot_general x5 -> x4, matrix products: 2.99 us -> 1.99 us  [matmul(): return jnp.einsum(spec, left, right, precision=highest)]
  transfers between devices with their start and end apart: 2 -> 2, of which waited for: 2 -> 2; matrix products, arithmetic and copies ran while one was open for 6% -> 5% of each run, Pallas kernels for 0% -> 0%
where the time goes in v11:
time: 101 us; the launch traced here: 100 us
  waiting for transfers between devices  32.5 us (32%)
  blocking collectives  26.2 us (26%)
  starting transfers between devices  24.6 us (24%)
  other arithmetic  7.15 us (7%)
  local copies, waits for them, and re-layouts  4.64 us (5%)
  matrix products  2.94 us (3%)
  between operations  2.37 us (2%)
    all_to_all x1, waiting for transfers between devices, shards(): lax.all_to_all(back, 'gz', split_axis=0, concat_axis=0, tiled=True)  18.7 us
    all_to_all x1, starting transfers between devices, shards(): lax.all_to_all(slabs, 'gz', split_axis=0, concat_axis=0, tiled=True)  17.8 us
    all_gather x1, blocking collectives, shards(): spectral = dft4_across(lax.all_gather(fields, 'gy', axis=0), gy_index, -1)  14.2 us
    all_to_all x1, waiting for transfers between devices, shards(): lax.all_to_all(slabs, 'gz', split_axis=0, concat_axis=0, tiled=True)  13.8 us
    all_gather x1, blocking collectives, shards(): result = dft4_across(lax.all_gather(spatial, 'gy', axis=0), gy_index, 1)  12 us
    all_to_all x1, starting transfers between devices, shards(): lax.all_to_all(back, 'gz', split_axis=0, concat_axis=0, tiled=True)  6.76 us
    select_n x9, other arithmetic, kernel_rows(): kernel_row.append(jnp.where(inside, energy[source, target] - coupling, 0.0))  2.47 us
  transfers between devices with their start and end apart: 2, of which 2 were waited for; matrix products, arithmetic and copies ran while one was open for 5% of the time, Pallas kernels for 0%

profile of v11, /device:TPU:1, one launch (start us, length us, event | category | flops | bytes accessed | tf_op | source)
XLA Modules:
  0.0 100.4 jit_solution(11909493270800179215)
XLA Ops:
  0.2 14.2 %all-gather = f32[8,3,2,8,512]{4,3,2,1,0:T(8,128)S(1)} all-gather(f32[2,3,2,8,512]{4,3,2,1,0:T(8,128)} %param.9), channel_id=2, replica_groups=mesh['gy'=4,'gz'=128] {'gy'}, dimensions={0}, use_global_device_ids=true | all-gather | bytes 983040 | tf_op jit(solution)/shard_map/all_gather | solution.py:278
  14.4 0.1 fusion.31
  14.7 0.1 copy.45
  14.8 0.6 copy-done
  15.4 0.5 fusion.78
  15.9 0.1 slice_add_fusion.6
  16.0 0.1 maximum_bitcast_fusion
  16.1 0.9 copy.46
  17.0 17.8 %all-to-all-start = ((f32[128,1,384]{2,1,0:T(1,128)}), f32[128,1,384]{2,1,0:T(1,128)S(1)}, u32[]{:S(2)}, u32[]{:S(2)}) async-start(f32[128,1,384]{2,1,0:T(1,128)} %copy.46), calls=%async_computation | async-start | bytes 393216 | tf_op jit(solution)/shard_map/all_to_all | solution.py:285
  34.9 0.6 fusion.77
  36.7 0.9 slice_reduce_fusion.11
  38.3 0.1 multiply_add_fusion.36
  38.4 0.1 pad_maximum_fusion.7
  38.4 0.2 slice_reduce_fusion.7
  38.7 0.1 fusion.49
  38.8 0.1 broadcast_in_dim.18
  38.9 0.1 broadcast_in_dim.19
  39.0 0.1 broadcast_in_dim.20
  39.1 0.2 subtract_select_fusion
  39.3 0.3 subtract_select_fusion.1
  39.6 0.3 subtract_select_fusion.3
  39.9 0.2 subtract_select_fusion.4
  40.2 0.3 subtract_select_fusion.2
  40.5 0.3 subtract_select_fusion.5
  40.8 0.2 subtract_select_fusion.8
  41.1 0.3 subtract_select_fusion.6
  41.4 0.3 subtract_select_fusion.7
  41.7 13.8 %all-to-all-done = f32[128,1,384]{2,1,0:T(1,128)S(1)} async-done(((f32[128,1,384]{2,1,0:T(1,128)}), f32[128,1,384]{2,1,0:T(1,128)S(1)}, u32[]{:S(2)}, u32[]{:S(2)}) %all-to-all-start) | async-done | bytes 196640 | tf_op jit(solution)/shard_map/all_to_all | solution.py:285
  55.6 0.5 fusion.23
  56.0 0.6 multiply_subtract_fusion.1
  56.6 0.1 reduce-precision_convert_fusion.3
  56.8 0.5 fusion
  57.4 0.1 copy.47
  57.6 0.8 copy-done.1
  58.4 0.5 fusion.6
  59.0 0.6 multiply_subtract_fusion
  59.5 0.5 fusion.16
  60.1 0.1 slice_subtract_fusion
  60.2 0.1 maximum_bitcast_fusion.1
  60.3 0.9 copy.48
  61.2 6.8 %all-to-all-start.1 = ((f32[128,1,384]{2,1,0:T(1,128)}), f32[128,1,384]{2,1,0:T(1,128)S(1)}, u32[]{:S(2)}, u32[]{:S(2)}) async-start(f32[128,1,384]{2,1,0:T(1,128)} %copy.48), calls=%async_computation.1 | async-start | bytes 393216 | tf_op jit(solution)/shard_map/all_to_all | solution.py:307
  68.0 18.7 %all-to-all-done.1 = f32[128,1,384]{2,1,0:T(1,128)S(1)} async-done(((f32[128,1,384]{2,1,0:T(1,128)}), f32[128,1,384]{2,1,0:T(1,128)S(1)}, u32[]{:S(2)}, u32[]{:S(2)}) %all-to-all-start.1) | async-done | bytes 196640 | tf_op jit(solution)/shard_map/all_to_all | solution.py:307
  86.7 0.5 fusion.20
  87.2 0.1 fusion.76
  87.3 0.1 fusion.75
  87.6 12.0 %all-gather.1 = f32[8,3,2,8,512]{4,3,2,1,0:T(8,128)S(1)} all-gather(f32[2,3,2,8,512]{4,3,2,1,0:T(8,128)S(1)} %pad_maximum_fusion.3), channel_id=3, replica_groups=mesh['gy'=4,'gz'=128] {'gy'}, dimensions={0}, use_global_device_ids=true | all-gather | bytes 983040 | tf_op jit(solution)/shard_map/all_gather | solution.py:310
  99.6 0.1 select_bitcast_fusion
  99.7 0.7 pad_maximum_fusion.4
  (50 shorter events, 1.0 us)
Async XLA Ops:
  14.5 0.9 copy-start
  15.9 19.0 %copy-start.4 = (f32[3]{0:T(128)S(1)}, f32[3]{0:T(128)}, u32[]{:S(2)}) copy-start(f32[3]{0:T(128)} %param.11) | copy-start | bytes 40
  15.9 20.8 %copy-start.3 = (f32[3,6]{1,0:T(4,128)S(1)}, f32[3,6]{1,0:T(4,128)}, u32[]{:S(2)}) copy-start(f32[3,6]{1,0:T(4,128)} %param.10) | copy-start | bytes 220
  17.0 38.5 %all-to-all-start = ((f32[128,1,384]{2,1,0:T(1,128)}), f32[128,1,384]{2,1,0:T(1,128)S(1)}, u32[]{:S(2)}, u32[]{:S(2)}) async-start(f32[128,1,384]{2,1,0:T(1,128)} %copy.46), calls=%async_computation | async-start | bytes 393216 | tf_op jit(solution)/shard_map/all_to_all | solution.py:285
  41.7 15.0 %copy-start.2 = (bf16[384,768]{1,0:T(8,128)(2,1)S(1)}, bf16[384,768]{1,0:T(8,128)(2,1)}, u32[]{:S(2)}) copy-start(bf16[384,768]{1,0:T(8,128)(2,1)} %constant.226.clone) | copy-start | bytes 1769476
  57.3 1.1 %copy-start.1 = (bf16[384,768]{1,0:T(8,128)(2,1)S(1)}, bf16[384,768]{1,0:T(8,128)(2,1)}, u32[]{:S(2)}) copy-start(bf16[384,768]{1,0:T(8,128)(2,1)} %constant.227.clone) | copy-start | bytes 1769476
  61.2 25.5 %all-to-all-start.1 = ((f32[128,1,384]{2,1,0:T(1,128)}), f32[128,1,384]{2,1,0:T(1,128)S(1)}, u32[]{:S(2)}, u32[]{:S(2)}) async-start(f32[128,1,384]{2,1,0:T(1,128)} %copy.48), calls=%async_computation.1 | async-start | bytes 393216 | tf_op jit(solution)/shard_map/all_to_all | solution.py:307

commit v12 on v11

--- a/solution.py
+++ b/solution.py
@@ -134,13 +134,30 @@
     return jnp.concatenate([top, bottom], axis=0)
 
 
+def dft8_parts(inverse):
+    rows = lax.broadcasted_iota(jnp.int32, (384, 384), 0)
+    cols = lax.broadcasted_iota(jnp.int32, (384, 384), 1)
+    if inverse:
+        rows, cols = cols, rows
+    inner_r = rows % 192
+    inner_c = cols % 192
+    same = (inner_r // 32 == inner_c // 32) & (inner_r % 4 == inner_c % 4)
+    m = (((inner_r // 4) % 8) * ((inner_c // 4) % 8)) % 8
+
+    def pick(plus, minus):
+        hit_plus = (m == plus[0]) | (m == plus[-1])
+        hit_minus = (m == minus[0]) | (m == minus[-1])
+        return jnp.where(hit_plus, 1.0, jnp.where(hit_minus, -1.0, 0.0))
+
+    diag = rows // 192 == cols // 192
+    sign = jnp.where(rows // 192 == 0, -1.0, 1.0)
+    unit = jnp.where(same, jnp.where(diag, pick((0,), (4,)), sign * pick((2,), (6,))), 0.0)
+    half = jnp.where(same, jnp.where(diag, pick((1, 7), (3, 5)), sign * pick((1, 3), (5, 7))), 0.0)
+    return jnp.concatenate([unit, half], axis=1).astype(jnp.bfloat16)
+
+
 def dft8_apply(values, inverse):
-    matrix = block_dft8_np()
-    if inverse:
-        matrix = matrix.T
-    unit = np.where(np.abs(matrix) > 0.9, np.sign(matrix), 0.0)
-    half = np.where((np.abs(matrix) > 0.5) & (np.abs(matrix) < 0.9), np.sign(matrix), 0.0)
-    table = jnp.asarray(np.concatenate([unit, half], axis=1), jnp.bfloat16)
+    table = dft8_parts(inverse)
     first = lax.reduce_precision(values, exponent_bits=8, mantissa_bits=7)
     rest = values - first
     second = lax.reduce_precision(rest, exponent_bits=8, mantissa_bits=7)

time: 101 us -> 99.9 us (0.989)
  other arithmetic: 7.15 us -> 9.46 us
  waiting for transfers between devices: 32.5 us -> 30.2 us
    all_to_all x1, waiting for transfers between devices: 13.8 us -> 11.4 us  [shards(): lax.all_to_all(slabs, 'gz', split_axis=0, concat_axis=0, tiled=True)]
    another operation x2 -> x3, other arithmetic: 0.17 us -> 2.39 us
  transfers between devices with their start and end apart: 2 -> 2, of which waited for: 2 -> 2; matrix products, arithmetic and copies ran while one was open for 5% -> 7% of each run, Pallas kernels for 0% -> 0%
where the time goes in v12:
time: 99.9 us; the launch traced here: 99.6 us
  waiting for transfers between devices  30.2 us (30%)
  blocking collectives  26 us (26%)
  starting transfers between devices  24.6 us (25%)
  other arithmetic  9.46 us (9%)
  local copies, waits for them, and re-layouts  3.89 us (4%)
  matrix products  2.95 us (3%)
  between operations  2.43 us (2%)
    all_to_all x1, waiting for transfers between devices, shards(): lax.all_to_all(back, 'gz', split_axis=0, concat_axis=0, tiled=True)  18.8 us
    all_to_all x1, starting transfers between devices, shards(): lax.all_to_all(slabs, 'gz', split_axis=0, concat_axis=0, tiled=True)  17.8 us
    all_gather x1, blocking collectives, shards(): spectral = dft4_across(lax.all_gather(fields, 'gy', axis=0), gy_index, -1)  14.2 us
    all_gather x1, blocking collectives, shards(): result = dft4_across(lax.all_gather(spatial, 'gy', axis=0), gy_index, 1)  11.9 us
    all_to_all x1, waiting for transfers between devices, shards(): lax.all_to_all(slabs, 'gz', split_axis=0, concat_axis=0, tiled=True)  11.4 us
    all_to_all x1, starting transfers between devices, shards(): lax.all_to_all(back, 'gz', split_axis=0, concat_axis=0, tiled=True)  6.76 us
    select_n x9, other arithmetic, kernel_rows(): kernel_row.append(jnp.where(inside, energy[source, target] - coupling, 0.0))  2.47 us
    another operation x3, other arithmetic  2.39 us
  transfers between devices with their start and end apart: 2, of which 2 were waited for; matrix products, arithmetic and copies ran while one was open for 7% of the time, Pallas kernels for 0%

profile of v12, /device:TPU:1, one launch (start us, length us, event | category | flops | bytes accessed | tf_op | source)
XLA Modules:
  0.0 99.6 jit_solution(16368538653393908535)
XLA Ops:
  0.2 14.2 %all-gather = f32[8,3,2,8,512]{4,3,2,1,0:T(8,128)S(1)} all-gather(f32[2,3,2,8,512]{4,3,2,1,0:T(8,128)} %param.7), channel_id=2, replica_groups=mesh['gy'=4,'gz'=128] {'gy'}, dimensions={0}, use_global_device_ids=true | all-gather | bytes 983040 | tf_op jit(solution)/shard_map/all_gather | solution.py:295
  14.4 0.1 fusion.73
  14.7 0.1 copy.43
  14.8 0.6 copy-done
  15.4 0.5 fusion.126
  15.9 0.1 slice_add_fusion.6
  16.1 0.1 maximum_bitcast_fusion
  16.2 0.9 copy.44
  17.0 17.8 %all-to-all-start = ((f32[128,1,384]{2,1,0:T(1,128)}), f32[128,1,384]{2,1,0:T(1,128)S(1)}, u32[]{:S(2)}, u32[]{:S(2)}) async-start(f32[128,1,384]{2,1,0:T(1,128)} %copy.44), calls=%async_computation | async-start | bytes 393216 | tf_op jit(solution)/shard_map/all_to_all | solution.py:302
  34.9 0.7 fusion.125
  36.9 1.0 slice_reduce_fusion.11
  38.5 0.1 multiply_add_fusion.36
  38.6 0.1 pad_maximum_fusion.7
  38.6 0.2 slice_reduce_fusion.7
  39.0 0.1 fusion.94
  39.0 0.1 broadcast_in_dim.61
  39.1 0.1 broadcast_in_dim.62
  39.2 0.1 broadcast_in_dim.63
  39.3 0.2 subtract_select_fusion
  39.5 0.3 subtract_select_fusion.1
  39.8 0.3 subtract_select_fusion.3
  40.1 0.2 subtract_select_fusion.4
  40.4 0.3 subtract_select_fusion.2
  40.7 0.3 subtract_select_fusion.5
  41.0 0.3 subtract_select_fusion.6
  41.3 0.3 subtract_select_fusion.7
  41.6 0.2 subtract_select_fusion.8
  41.9 2.2 %fusion.2 = (bf16[384,384]{1,0:T(8,128)(2,1)S(1)}, bf16[384,384]{1,0:T(8,128)(2,1)S(1)}, bf16[384,384]{1,0:T(8,128)(2,1)S(1)}, bf16[384,384]{1,0:T(8,128)(2,1)S(1)}) fusion(s32[384]{0:T(512)S(1)} %get-tuple-element.133, s32[384]{0:T(512)S(1)} %get-tuple-element.136, pred[384]{0:T(512)(128)(4,1)S(1)} %get-tuple-element.137, s32[384]{0:T(512)S(1)} %get-tuple-element.134, ...), kind=kLoop, calls=%fused_computation.41 | loop fusion | flops 21823488 | bytes 1186560 | tf_op jit(solution)/shard_map/convert.5
  44.1 11.4 %all-to-all-done = f32[128,1,384]{2,1,0:T(1,128)S(1)} async-done(((f32[128,1,384]{2,1,0:T(1,128)}), f32[128,1,384]{2,1,0:T(1,128)S(1)}, u32[]{:S(2)}, u32[]{:S(2)}) %all-to-all-start) | async-done | bytes 196640 | tf_op jit(solution)/shard_map/all_to_all | solution.py:302
  55.6 0.5 fusion.65
  56.0 0.6 multiply_subtract_fusion.1
  56.6 0.1 reduce-precision_convert_fusion.3
  56.8 0.5 fusion.28
  57.3 0.1 copy.45
  57.6 0.5 fusion.32
  58.2 0.6 multiply_subtract_fusion
  58.8 0.5 fusion.58
  59.3 0.1 slice_subtract_fusion
  59.5 0.1 maximum_bitcast_fusion.1
  59.6 0.9 copy.46
  60.4 6.8 %all-to-all-start.1 = ((f32[128,1,384]{2,1,0:T(1,128)}), f32[128,1,384]{2,1,0:T(1,128)S(1)}, u32[]{:S(2)}, u32[]{:S(2)}) async-start(f32[128,1,384]{2,1,0:T(1,128)} %copy.46), calls=%async_computation.1 | async-start | bytes 393216 | tf_op jit(solution)/shard_map/all_to_all | solution.py:324
  67.3 18.8 %all-to-all-done.1 = f32[128,1,384]{2,1,0:T(1,128)S(1)} async-done(((f32[128,1,384]{2,1,0:T(1,128)}), f32[128,1,384]{2,1,0:T(1,128)S(1)}, u32[]{:S(2)}, u32[]{:S(2)}) %all-to-all-start.1) | async-done | bytes 196640 | tf_op jit(solution)/shard_map/all_to_all | solution.py:324
  86.1 0.5 fusion.62
  86.6 0.1 fusion.124
  86.7 0.1 fusion.123
  86.9 11.9 %all-gather.1 = f32[8,3,2,8,512]{4,3,2,1,0:T(8,128)S(1)} all-gather(f32[2,3,2,8,512]{4,3,2,1,0:T(8,128)S(1)} %pad_maximum_fusion.3), channel_id=3, replica_groups=mesh['gy'=4,'gz'=128] {'gy'}, dimensions={0}, use_global_device_ids=true | all-gather | bytes 983040 | tf_op jit(solution)/shard_map/all_gather | solution.py:327
  98.8 0.1 select_bitcast_fusion
  98.9 0.7 pad_maximum_fusion.4
  (50 shorter events, 1.0 us)
Async XLA Ops:
  14.5 0.9 copy-start
  15.9 19.1 %copy-start.2 = (f32[3]{0:T(128)S(1)}, f32[3]{0:T(128)}, u32[]{:S(2)}) copy-start(f32[3]{0:T(128)} %param.9) | copy-start | bytes 40
  15.9 21.0 %copy-start.1 = (f32[3,6]{1,0:T(4,128)S(1)}, f32[3,6]{1,0:T(4,128)}, u32[]{:S(2)}) copy-start(f32[3,6]{1,0:T(4,128)} %param.8) | copy-start | bytes 220
  17.0 38.5 %all-to-all-start = ((f32[128,1,384]{2,1,0:T(1,128)}), f32[128,1,384]{2,1,0:T(1,128)S(1)}, u32[]{:S(2)}, u32[]{:S(2)}) async-start(f32[128,1,384]{2,1,0:T(1,128)} %copy.44), calls=%async_computation | async-start | bytes 393216 | tf_op jit(solution)/shard_map/all_to_all | solution.py:302
  60.4 25.6 %all-to-all-start.1 = ((f32[128,1,384]{2,1,0:T(1,128)}), f32[128,1,384]{2,1,0:T(1,128)S(1)}, u32[]{:S(2)}, u32[]{:S(2)}) async-start(f32[128,1,384]{2,1,0:T(1,128)} %copy.46), calls=%async_computation.1 | async-start | bytes 393216 | tf_op jit(solution)/shard_map/all_to_all | solution.py:324

commit v13 on v12

--- a/solution.py
+++ b/solution.py
@@ -266,13 +266,12 @@
     s_im = product[192:, 128:]
     re = (c_re - s_im).reshape(3, 2, 8, 4, 128)
     im = (c_im + s_re).reshape(3, 2, 8, 4, 128)
-    lanes = lax.broadcasted_iota(jnp.int32, (128,), 0)
-    parts = []
-    for k1 in range(4):
-        tw_cos, tw_sin = cos_sin(lanes * k1, 512)
-        r = re[..., k1, :]
-        i = im[..., k1, :]
-        parts.append((r * tw_cos - i * tw_sin, i * tw_cos + r * tw_sin))
+    k1 = lax.broadcasted_iota(jnp.int32, (4, 128), 0)
+    lanes = lax.broadcasted_iota(jnp.int32, (4, 128), 1)
+    tw_cos, tw_sin = cos_sin(lanes * k1, 512)
+    turned_re = re * tw_cos - im * tw_sin
+    turned_im = im * tw_cos + re * tw_sin
+    parts = [(turned_re[..., k, :], turned_im[..., k, :]) for k in range(4)]
     mixed = dft4(parts, 1)
     real_part = jnp.concatenate([m[0] for m in mixed], axis=-1)
     imag_part = jnp.concatenate([m[1] for m in mixed], axis=-1)

time: 99.9 us -> 99.7 us (level)
  no operation moved by 1% of the time
where the time goes in v13:
time: 99.7 us; the launch traced here: 99.4 us
  waiting for transfers between devices  30.2 us (30%)
  blocking collectives  26.2 us (26%)
  starting transfers between devices  24.6 us (25%)
  other arithmetic  9.36 us (9%)
  local copies, waits for them, and re-layouts  3.74 us (4%)
  matrix products  2.94 us (3%)
  between operations  2.41 us (2%)
    all_to_all x1, waiting for transfers between devices, shards(): lax.all_to_all(back, 'gz', split_axis=0, concat_axis=0, tiled=True)  18.6 us
    all_to_all x1, starting transfers between devices, shards(): lax.all_to_all(slabs, 'gz', split_axis=0, concat_axis=0, tiled=True)  17.8 us
    all_gather x1, blocking collectives, shards(): spectral = dft4_across(lax.all_gather(fields, 'gy', axis=0), gy_index, -1)  14.2 us
    all_gather x1, blocking collectives, shards(): result = dft4_across(lax.all_gather(spatial, 'gy', axis=0), gy_index, 1)  12 us
    all_to_all x1, waiting for transfers between devices, shards(): lax.all_to_all(slabs, 'gz', split_axis=0, concat_axis=0, tiled=True)  11.6 us
    all_to_all x1, starting transfers between devices, shards(): lax.all_to_all(back, 'gz', split_axis=0, concat_axis=0, tiled=True)  6.76 us
    select_n x9, other arithmetic, kernel_rows(): kernel_row.append(jnp.where(inside, energy[source, target] - coupling, 0.0))  2.47 us
    another operation x3, other arithmetic  2.39 us
  transfers between devices with their start and end apart: 2, of which 2 were waited for; matrix products, arithmetic and copies ran while one was open for 7% of the time, Pallas kernels for 0%

profile of v13, /device:TPU:1, one launch (start us, length us, event | category | flops | bytes accessed | tf_op | source)
XLA Modules:
  0.0 99.4 jit_solution(17595801614033627233)
XLA Ops:
  0.2 14.2 %all-gather = f32[8,3,2,8,512]{4,3,2,1,0:T(8,128)S(1)} all-gather(f32[2,3,2,8,512]{4,3,2,1,0:T(8,128)} %param.7), channel_id=2, replica_groups=mesh['gy'=4,'gz'=128] {'gy'}, dimensions={0}, use_global_device_ids=true | all-gather | bytes 983040 | tf_op jit(solution)/shard_map/all_gather | solution.py:294
  14.4 0.1 fusion.73
  14.7 0.1 copy.31
  14.8 0.6 copy-done
  15.4 0.5 fusion.129
  15.9 0.1 slice_add_fusion.6
  16.0 0.1 maximum_bitcast_fusion
  16.1 0.9 copy.32
  17.0 17.8 %all-to-all-start = ((f32[128,1,384]{2,1,0:T(1,128)}), f32[128,1,384]{2,1,0:T(1,128)S(1)}, u32[]{:S(2)}, u32[]{:S(2)}) async-start(f32[128,1,384]{2,1,0:T(1,128)} %copy.32), calls=%async_computation | async-start | bytes 393216 | tf_op jit(solution)/shard_map/all_to_all | solution.py:301
  34.9 0.7 fusion.128
  36.9 0.8 slice_reduce_fusion.11
  38.3 0.1 multiply_add_fusion.33
  38.4 0.1 pad_maximum_fusion.7
  38.5 0.2 slice_reduce_fusion.7
  38.8 0.1 fusion.94
  38.9 0.1 broadcast_in_dim.111
  39.0 0.1 broadcast_in_dim.112
  39.0 0.1 broadcast_in_dim.113
  39.1 0.2 subtract_select_fusion
  39.4 0.3 subtract_select_fusion.1
  39.7 0.3 subtract_select_fusion.3
  40.0 0.2 subtract_select_fusion.4
  40.2 0.3 subtract_select_fusion.2
  40.5 0.3 subtract_select_fusion.5
  40.8 0.3 subtract_select_fusion.6
  41.1 0.3 subtract_select_fusion.7
  41.4 0.2 subtract_select_fusion.8
  41.8 2.2 %fusion.2 = (bf16[384,384]{1,0:T(8,128)(2,1)S(1)}, bf16[384,384]{1,0:T(8,128)(2,1)S(1)}, bf16[384,384]{1,0:T(8,128)(2,1)S(1)}, bf16[384,384]{1,0:T(8,128)(2,1)S(1)}) fusion(s32[384]{0:T(512)S(1)} %get-tuple-element.117, s32[384]{0:T(512)S(1)} %get-tuple-element.120, pred[384]{0:T(512)(128)(4,1)S(1)} %get-tuple-element.121, s32[384]{0:T(512)S(1)} %get-tuple-element.118, ...), kind=kLoop, calls=%fused_computation.41 | loop fusion | flops 21823488 | bytes 1186560 | tf_op jit(solution)/shard_map/convert.5
  44.0 11.6 %all-to-all-done = f32[128,1,384]{2,1,0:T(1,128)S(1)} async-done(((f32[128,1,384]{2,1,0:T(1,128)}), f32[128,1,384]{2,1,0:T(1,128)S(1)}, u32[]{:S(2)}, u32[]{:S(2)}) %all-to-all-start) | async-done | bytes 196640 | tf_op jit(solution)/shard_map/all_to_all | solution.py:301
  55.6 0.5 fusion.65
  56.0 0.6 multiply_subtract_fusion.1
  56.6 0.1 reduce-precision_convert_fusion.3
  56.8 0.5 fusion.28
  57.2 0.1 slice_add_fusion.2
  57.3 0.1 copy.33
  57.6 0.5 fusion.32
  58.1 0.1 slice_add_fusion
  58.2 0.6 multiply_subtract_fusion
  58.8 0.5 fusion.58
  59.3 0.1 slice_subtract_fusion
  59.4 0.1 maximum_bitcast_fusion.1
  59.5 0.9 copy.34
  60.4 6.8 %all-to-all-start.1 = ((f32[128,1,384]{2,1,0:T(1,128)}), f32[128,1,384]{2,1,0:T(1,128)S(1)}, u32[]{:S(2)}, u32[]{:S(2)}) async-start(f32[128,1,384]{2,1,0:T(1,128)} %copy.34), calls=%async_computation.1 | async-start | bytes 393216 | tf_op jit(solution)/shard_map/all_to_all | solution.py:323
  67.3 18.6 %all-to-all-done.1 = f32[128,1,384]{2,1,0:T(1,128)S(1)} async-done(((f32[128,1,384]{2,1,0:T(1,128)}), f32[128,1,384]{2,1,0:T(1,128)S(1)}, u32[]{:S(2)}, u32[]{:S(2)}) %all-to-all-start.1) | async-done | bytes 196640 | tf_op jit(solution)/shard_map/all_to_all | solution.py:323
  85.9 0.5 fusion.62
  86.6 12.0 %all-gather.1 = f32[8,3,2,8,512]{4,3,2,1,0:T(8,128)S(1)} all-gather(f32[2,3,2,8,512]{4,3,2,1,0:T(8,128)S(1)} %pad_maximum_fusion.3), channel_id=3, replica_groups=mesh['gy'=4,'gz'=128] {'gy'}, dimensions={0}, use_global_device_ids=true | all-gather | bytes 983040 | tf_op jit(solution)/shard_map/all_gather | solution.py:326
  98.6 0.1 select_bitcast_fusion
  98.7 0.7 pad_maximum_fusion.4
  (49 shorter events, 0.9 us)
Async XLA Ops:
  14.5 0.9 copy-start
  15.9 19.1 %copy-start.2 = (f32[3]{0:T(128)S(1)}, f32[3]{0:T(128)}, u32[]{:S(2)}) copy-start(f32[3]{0:T(128)} %param.9) | copy-start | bytes 40
  15.9 21.0 %copy-start.1 = (f32[3,6]{1,0:T(4,128)S(1)}, f32[3,6]{1,0:T(4,128)}, u32[]{:S(2)}) copy-start(f32[3,6]{1,0:T(4,128)} %param.8) | copy-start | bytes 220
  17.0 38.5 %all-to-all-start = ((f32[128,1,384]{2,1,0:T(1,128)}), f32[128,1,384]{2,1,0:T(1,128)S(1)}, u32[]{:S(2)}, u32[]{:S(2)}) async-start(f32[128,1,384]{2,1,0:T(1,128)} %copy.32), calls=%async_computation | async-start | bytes 393216 | tf_op jit(solution)/shard_map/all_to_all | solution.py:301
  60.4 25.5 %all-to-all-start.1 = ((f32[128,1,384]{2,1,0:T(1,128)}), f32[128,1,384]{2,1,0:T(1,128)S(1)}, u32[]{:S(2)}, u32[]{:S(2)}) async-start(f32[128,1,384]{2,1,0:T(1,128)} %copy.34), calls=%async_computation.1 | async-start | bytes 393216 | tf_op jit(solution)/shard_map/all_to_all | solution.py:323

commit v14 on v13

--- a/solution.py
+++ b/solution.py
@@ -246,13 +246,12 @@
 def y_forward(spectral):
     parts = [(spectral[0, ..., 128 * a:128 * a + 128], spectral[1, ..., 128 * a:128 * a + 128]) for a in range(4)]
     mixed = dft4(parts, -1)
-    lanes = lax.broadcasted_iota(jnp.int32, (128,), 0)
-    out = []
-    for k1 in range(4):
-        tw_cos, tw_sin = cos_sin(lanes * k1, 512)
-        re, im = mixed[k1]
-        out.append(jnp.stack([re * tw_cos + im * tw_sin, im * tw_cos - re * tw_sin]))
-    stacked = jnp.stack(out, axis=-2).reshape(384, 128)
+    re = jnp.stack([m[0] for m in mixed], axis=-2)
+    im = jnp.stack([m[1] for m in mixed], axis=-2)
+    k1 = lax.broadcasted_iota(jnp.int32, (4, 128), 0)
+    lanes = lax.broadcasted_iota(jnp.int32, (4, 128), 1)
+    tw_cos, tw_sin = cos_sin(lanes * k1, 512)
+    stacked = jnp.stack([re * tw_cos + im * tw_sin, im * tw_cos - re * tw_sin]).reshape(384, 128)
     product = matmul("kb,rb->kr", stacked_table(128), stacked)
     re, im = combine_rows(product, -1)
     return jnp.concatenate([re, im], axis=1)

time: 99.7 us -> 99.5 us (level)
    another operation x8 -> x7, other arithmetic: 2.43 us -> 2.44 us
where the time goes in v14:
time: 99.5 us; the launch traced here: 99.2 us
  waiting for transfers between devices  30.2 us (30%)
  blocking collectives  26.1 us (26%)
  starting transfers between devices  24.6 us (25%)
  other arithmetic  9.24 us (9%)
  local copies, waits for them, and re-layouts  3.69 us (4%)
  matrix products  2.95 us (3%)
  between operations  2.38 us (2%)
    all_to_all x1, waiting for transfers between devices, shards(): lax.all_to_all(back, 'gz', split_axis=0, concat_axis=0, tiled=True)  18.7 us
    all_to_all x1, starting transfers between devices, shards(): lax.all_to_all(slabs, 'gz', split_axis=0, concat_axis=0, tiled=True)  17.8 us
    all_gather x1, blocking collectives, shards(): spectral = dft4_across(lax.all_gather(fields, 'gy', axis=0), gy_index, -1)  14.2 us
    all_gather x1, blocking collectives, shards(): result = dft4_across(lax.all_gather(spatial, 'gy', axis=0), gy_index, 1)  12 us
    all_to_all x1, waiting for transfers between devices, shards(): lax.all_to_all(slabs, 'gz', split_axis=0, concat_axis=0, tiled=True)  11.6 us
    all_to_all x1, starting transfers between devices, shards(): lax.all_to_all(back, 'gz', split_axis=0, concat_axis=0, tiled=True)  6.76 us
    select_n x9, other arithmetic, kernel_rows(): kernel_row.append(jnp.where(inside, energy[source, target] - coupling, 0.0))  2.47 us
    another operation x3, other arithmetic  2.39 us
  transfers between devices with their start and end apart: 2, of which 2 were waited for; matrix products, arithmetic and copies ran while one was open for 7% of the time, Pallas kernels for 0%

profile of v14, /device:TPU:1, one launch (start us, length us, event | category | flops | bytes accessed | tf_op | source)
XLA Modules:
  0.0 99.2 jit_solution(314497604099701088)
XLA Ops:
  0.1 14.2 %all-gather = f32[8,3,2,8,512]{4,3,2,1,0:T(8,128)S(1)} all-gather(f32[2,3,2,8,512]{4,3,2,1,0:T(8,128)} %param.7), channel_id=2, replica_groups=mesh['gy'=4,'gz'=128] {'gy'}, dimensions={0}, use_global_device_ids=true | all-gather | bytes 983040 | tf_op jit(solution)/shard_map/all_gather | solution.py:293
  14.2 0.1 fusion.73
  14.5 0.1 copy.31
  14.6 0.6 copy-done
  15.2 0.5 fusion.115
  15.8 0.1 slice_add_fusion.6
  15.9 0.1 maximum_bitcast_fusion
  16.0 0.9 copy.32
  16.9 17.8 %all-to-all-start = ((f32[128,1,384]{2,1,0:T(1,128)}), f32[128,1,384]{2,1,0:T(1,128)S(1)}, u32[]{:S(2)}, u32[]{:S(2)}) async-start(f32[128,1,384]{2,1,0:T(1,128)} %copy.32), calls=%async_computation | async-start | bytes 393216 | tf_op jit(solution)/shard_map/all_to_all | solution.py:300
  34.8 0.6 fusion.114
  36.6 0.9 slice_reduce_fusion.11
  38.2 0.1 multiply_add_fusion.30
  38.3 0.1 pad_maximum_fusion.9
  38.3 0.2 slice_reduce_fusion.7
  38.7 0.1 fusion.94
  38.7 0.1 broadcast_in_dim.99
  38.8 0.1 broadcast_in_dim.100
  38.9 0.1 broadcast_in_dim.101
  39.0 0.2 subtract_select_fusion
  39.2 0.3 subtract_select_fusion.1
  39.5 0.3 subtract_select_fusion.3
  39.8 0.2 subtract_select_fusion.4
  40.1 0.3 subtract_select_fusion.2
  40.4 0.3 subtract_select_fusion.5
  40.7 0.3 subtract_select_fusion.6
  41.0 0.3 subtract_select_fusion.7
  41.3 0.2 subtract_select_fusion.8
  41.6 2.2 %fusion.2 = (bf16[384,384]{1,0:T(8,128)(2,1)S(1)}, bf16[384,384]{1,0:T(8,128)(2,1)S(1)}, bf16[384,384]{1,0:T(8,128)(2,1)S(1)}, bf16[384,384]{1,0:T(8,128)(2,1)S(1)}) fusion(s32[384]{0:T(512)S(1)} %get-tuple-element.106, s32[384]{0:T(512)S(1)} %get-tuple-element.109, pred[384]{0:T(512)(128)(4,1)S(1)} %get-tuple-element.110, s32[384]{0:T(512)S(1)} %get-tuple-element.107, ...), kind=kLoop, calls=%fused_computation.41 | loop fusion | flops 21823488 | bytes 1186560 | tf_op jit(solution)/shard_map/convert.5
  43.8 11.6 %all-to-all-done = f32[128,1,384]{2,1,0:T(1,128)S(1)} async-done(((f32[128,1,384]{2,1,0:T(1,128)}), f32[128,1,384]{2,1,0:T(1,128)S(1)}, u32[]{:S(2)}, u32[]{:S(2)}) %all-to-all-start) | async-done | bytes 196640 | tf_op jit(solution)/shard_map/all_to_all | solution.py:300
  55.4 0.5 fusion.65
  55.9 0.6 multiply_subtract_fusion.1
  56.5 0.1 reduce-precision_convert_fusion.3
  56.6 0.5 fusion.28
  57.1 0.1 slice_add_fusion.2
  57.2 0.1 copy.33
  57.4 0.5 fusion.32
  57.9 0.1 slice_add_fusion
  58.0 0.6 multiply_subtract_fusion
  58.6 0.5 fusion.58
  59.1 0.1 slice_subtract_fusion
  59.3 0.1 maximum_bitcast_fusion.1
  59.4 0.9 copy.34
  60.3 6.8 %all-to-all-start.1 = ((f32[128,1,384]{2,1,0:T(1,128)}), f32[128,1,384]{2,1,0:T(1,128)S(1)}, u32[]{:S(2)}, u32[]{:S(2)}) async-start(f32[128,1,384]{2,1,0:T(1,128)} %copy.34), calls=%async_computation.1 | async-start | bytes 393216 | tf_op jit(solution)/shard_map/all_to_all | solution.py:322
  67.1 18.7 %all-to-all-done.1 = f32[128,1,384]{2,1,0:T(1,128)S(1)} async-done(((f32[128,1,384]{2,1,0:T(1,128)}), f32[128,1,384]{2,1,0:T(1,128)S(1)}, u32[]{:S(2)}, u32[]{:S(2)}) %all-to-all-start.1) | async-done | bytes 196640 | tf_op jit(solution)/shard_map/all_to_all | solution.py:322
  85.8 0.5 fusion.62
  86.5 12.0 %all-gather.1 = f32[8,3,2,8,512]{4,3,2,1,0:T(8,128)S(1)} all-gather(f32[2,3,2,8,512]{4,3,2,1,0:T(8,128)S(1)} %pad_maximum_fusion.3), channel_id=3, replica_groups=mesh['gy'=4,'gz'=128] {'gy'}, dimensions={0}, use_global_device_ids=true | all-gather | bytes 983040 | tf_op jit(solution)/shard_map/all_gather | solution.py:325
  98.4 0.1 select_bitcast_fusion
  98.5 0.7 pad_maximum_fusion.4
  (43 shorter events, 0.7 us)
Async XLA Ops:
  14.3 0.9 copy-start
  15.7 19.0 %copy-start.2 = (f32[3]{0:T(128)S(1)}, f32[3]{0:T(128)}, u32[]{:S(2)}) copy-start(f32[3]{0:T(128)} %param.9) | copy-start | bytes 40
  15.7 20.9 %copy-start.1 = (f32[3,6]{1,0:T(4,128)S(1)}, f32[3,6]{1,0:T(4,128)}, u32[]{:S(2)}) copy-start(f32[3,6]{1,0:T(4,128)} %param.8) | copy-start | bytes 220
  16.9 38.5 %all-to-all-start = ((f32[128,1,384]{2,1,0:T(1,128)}), f32[128,1,384]{2,1,0:T(1,128)S(1)}, u32[]{:S(2)}, u32[]{:S(2)}) async-start(f32[128,1,384]{2,1,0:T(1,128)} %copy.32), calls=%async_computation | async-start | bytes 393216 | tf_op jit(solution)/shard_map/all_to_all | solution.py:300
  60.3 25.5 %all-to-all-start.1 = ((f32[128,1,384]{2,1,0:T(1,128)}), f32[128,1,384]{2,1,0:T(1,128)S(1)}, u32[]{:S(2)}, u32[]{:S(2)}) async-start(f32[128,1,384]{2,1,0:T(1,128)} %copy.34), calls=%async_computation.1 | async-start | bytes 393216 | tf_op jit(solution)/shard_map/all_to_all | solution.py:322
